TPU v7x, 128 devices: a whole 4x4x4 slice. The times are simulated.
128 devices in a mesh: dp: 4 (over x), expert: 32 (over y, z, core).
Axes of the slice: x: 4, y: 4, z: 4, core: 2. Of those that a mesh axis runs over, the one named last changes fastest.
Arguments:
- tokens: bfloat16 [16384, 4096], P(('dp', 'expert')), may hold values from -6 to 6
- cotangent: bfloat16 [16384, 4096], P(('dp', 'expert')), may hold values from -6 to 6
- routes: int32 [16384], P(('dp', 'expert')), may hold values from 0 to 31, as said below
- combine: float32 [16384], P(('dp', 'expert')), may hold values from 0.05 to 1
- expert_weights: bfloat16 [32, 3, 1536, 4096], P('expert', None, 'dp'), may hold values from -0.09375 to 0.09375
Outputs:
- combined: bfloat16 [16384, 4096], P(('dp', 'expert'))
- token_grad: bfloat16 [16384, 4096], P(('dp', 'expert'))
- combine_grad: float32 [16384], P(('dp', 'expert'))
Inputs may be any that keep to these rules, and one draw needn't show every extreme that they name: `routes`: among the 128 rows of every device, two experts, the same two on every device, are each named by exactly 8 rows, and every other expert by 3 or 4 rows.
All inputs are finite; a program needn't handle non-finite values.
Results may differ from a plain program's by a relative error of at most 0.015.
Values may be sent and summed in bfloat16 or wider, within the bound.
No kernel may reach another device: no remote copies, remote signals or barrier semaphores. Data moves between devices by JAX's collectives and lax.ppermute only.
A program may use at most 192 MiB of HBM per device.

v0:
```python
import jax
import jax.numpy as jnp
from jax import lax
from jax.sharding import PartitionSpec as P


def placement(member, slot_count):
    within = jnp.sum((jnp.cumsum(member, 0) - 1) * member, 1)
    owner_group = jnp.sum(member * lax.iota(jnp.int32, member.shape[1])[None, :], 1)
    is_used = jnp.sum(member, 1) > 0
    target = owner_group * slot_count + within
    buffer_cells = lax.iota(jnp.int32, member.shape[1] * slot_count)
    return ((buffer_cells[:, None] == target[None, :]) & is_used[None, :]).astype(jnp.bfloat16)


def spread(layout, row_block):
    return jnp.dot(layout, row_block, preferred_element_type=jnp.float32).astype(jnp.bfloat16)


def collect(layout, buffer_rows):
    return lax.dot_general(
        layout, buffer_rows, (((0,), (0,)), ((), ())), preferred_element_type=jnp.float32
    )


def shifted(values, step):
    n = lax.axis_size("dp")
    return lax.ppermute(values, "dp", perm=[(i, (i + step) % n) for i in range(n)])


def group_rows(values):
    half = values.shape[0] // 2
    left_lo = shifted(values[:half], 1)
    right_hi = shifted(values[half:], -1)
    far_head = shifted(left_lo, 1)
    far_tail = shifted(right_hi, -1)
    left_hi = shifted(values[half:], 1)
    right_lo = shifted(values[:half], -1)
    return [values, left_lo, left_hi, right_lo, right_hi, far_head, far_tail]


def sum_start(parts):
    far_head = shifted(parts[5].astype(jnp.bfloat16), -1)
    far_tail = shifted(parts[6].astype(jnp.bfloat16), 1)
    return far_head, far_tail


def sum_finish(parts, received):
    own, left_lo, left_hi, right_lo, right_hi = parts[:5]
    far_head, far_tail = [r.astype(jnp.float32) for r in received]

    def wide(x):
        return x.astype(jnp.bfloat16).astype(jnp.float32)

    back_hi_a = shifted(left_hi.astype(jnp.bfloat16), -1).astype(jnp.float32)
    back_lo_b = shifted(right_lo.astype(jnp.bfloat16), 1).astype(jnp.float32)
    back_lo_a = shifted((wide(left_lo) + far_head).astype(jnp.bfloat16), -1).astype(jnp.float32)
    back_hi_b = shifted((wide(right_hi) + far_tail).astype(jnp.bfloat16), 1).astype(jnp.float32)
    return wide(own) + jnp.concatenate([back_lo_a + back_lo_b, back_hi_a + back_hi_b], 0)


def arrive_rows(cold_buf, experts, slot_count, model_width):
    return lax.all_to_all(
        cold_buf.reshape(experts, slot_count, model_width),
        "expert",
        split_axis=0,
        concat_axis=0,
        tiled=True,
    ).reshape(-1, model_width)


def return_rows(total, experts, slot_count, model_width):
    summed = total.astype(jnp.bfloat16).reshape(experts, slot_count, model_width)
    return lax.all_to_all(summed, "expert", split_axis=0, concat_axis=0, tiled=True).reshape(
        -1, model_width
    )


def forward_rows(row_block, matrices):
    gate_up = jnp.einsum("rd,kfd->krf", row_block, matrices[:2], preferred_element_type=jnp.float32)
    gate_act = gate_up[0]
    up_act = gate_up[1]
    hidden = (gate_act * jax.nn.sigmoid(gate_act) * up_act).astype(jnp.bfloat16)
    partial_out = jnp.dot(hidden, matrices[2], preferred_element_type=jnp.float32)
    return (gate_act, up_act, partial_out)


def backward_rows(row_block, gate_act, up_act, matrices):
    hidden_grad = lax.dot_general(
        row_block, matrices[2], (((1,), (1,)), ((), ())), preferred_element_type=jnp.float32
    )
    squashed = jax.nn.sigmoid(gate_act)
    gate_grad = (hidden_grad * up_act * squashed * (1.0 + gate_act * (1.0 - squashed))).astype(
        jnp.bfloat16
    )
    up_grad = (hidden_grad * gate_act * squashed).astype(jnp.bfloat16)
    both_grads = jnp.stack([gate_grad, up_grad])
    return jnp.einsum("krf,kfd->rd", both_grads, matrices[:2], preferred_element_type=jnp.float32)


def shards(tokens, cotangent, routes, combine, expert_weights):
    weights = expert_weights[0]
    tok_dev = tokens.shape[0]
    model_width = tokens.shape[1]
    experts = lax.axis_size("expert")
    capacity = 2 * tok_dev // experts
    labels = lax.iota(jnp.int32, experts)
    member = (routes[:, None] == labels[None, :]).astype(jnp.int32)
    cold_layout = placement(member, capacity)
    cold_buf = spread(cold_layout, tokens)
    tok_blocks = group_rows(arrive_rows(cold_buf, experts, capacity, model_width))
    cotangent_wide = cotangent.astype(jnp.float32)
    out_grad = (combine[:, None] * cotangent_wide).astype(jnp.bfloat16)
    cold_grad_buf = spread(cold_layout, out_grad)
    cold_grad_arrived = arrive_rows(cold_grad_buf, experts, capacity, model_width)
    cold_grad_arrived, tok_blocks = lax.optimization_barrier((cold_grad_arrived, tok_blocks))
    forward = [forward_rows(block, weights) for block in tok_blocks]
    fwd_parts = [f[2] for f in forward]
    cot_blocks = group_rows(cold_grad_arrived)
    fwd_received = sum_start(fwd_parts)
    fwd_received, cot_blocks = lax.optimization_barrier((fwd_received, cot_blocks))
    cold_out = return_rows(sum_finish(fwd_parts, fwd_received), experts, capacity, model_width)
    expert_out = collect(cold_layout, cold_out)
    combined = (combine[:, None] * expert_out).astype(jnp.bfloat16)
    combine_grad = jnp.sum(expert_out * cotangent_wide, 1)
    grad_parts = [
        backward_rows(block, f[0], f[1], weights) for block, f in zip(cot_blocks, forward)
    ]
    grad_total = sum_finish(grad_parts, sum_start(grad_parts))
    cold_grad_out = return_rows(grad_total, experts, capacity, model_width)
    input_grad = collect(cold_layout, cold_grad_out)
    token_grad = input_grad.astype(jnp.bfloat16)
    return (combined, token_grad, combine_grad)


def solution(mesh):
    return jax.shard_map(
        shards,
        mesh=mesh,
        in_specs=(
            P(("dp", "expert"), None),
            P(("dp", "expert"), None),
            P(("dp", "expert")),
            P(("dp", "expert")),
            P("expert", None, "dp", None),
        ),
        out_specs=(P(("dp", "expert"), None), P(("dp", "expert"), None), P(("dp", "expert"))),
        check_vma=False,
    )
```

profile of v0, /device:TPU:1, one launch (start us, length us, event | category | flops | bytes accessed | tf_op | source)
XLA Modules:
  0.0 375.5 jit_solution(593017993843552359)
XLA Ops:
  1.7 0.9 fusion.281
  3.3 37.5 %all_to_all.20 = bf16[32,8,4096]{2,1,0:T(8,128)(2,1)S(1)} all-to-all(bf16[32,8,4096]{2,1,0:T(8,128)(2,1)S(1)} %fusion.39), channel_id=1, replica_groups=mesh['dp'=4,'expert'=32] {'expert'}, dimensions={0} | all-to-all | bytes 4194304 | tf_op jit(solution)/shard_map/all_to_all | solution.py:63
  40.8 1.4 copy-done.2
  42.2 1.1 slice_bitcast_fusion
  43.3 1.2 collective-permute-start
  44.5 1.5 collective-permute-start.3
  46.0 2.1 fusion.38
  48.1 4.5 %all-to-all-start = ((bf16[32,8,4096]{2,1,0:T(8,128)(2,1)}), bf16[32,8,4096]{2,1,0:T(8,128)(2,1)S(1)}, u32[]{:S(2)}, u32[]{:S(2)}) async-start(bf16[32,8,4096]{2,1,0:T(8,128)(2,1)} %fusion.38), calls=%async_computation | async-start | bytes 4194304 | tf_op jit(solution)/shard_map/all_to_all | solution.py:63
  52.7 2.7 collective-permute-start.2
  55.3 13.9 %collective-permute-done = bf16[128,4096]{1,0:T(8,128)(2,1)} collective-permute-done((bf16[128,4096]{1,0:T(8,128)(2,1)S(1)}, bf16[128,4096]{1,0:T(8,128)(2,1)}, u32[]{:S(2)}, u32[]{:S(2)}) %collective-permute-start) | collective-permute-done | bytes 1048608 | tf_op jit(solution)/shard_map/ppermute | solution.py:28
  69.2 2.7 collective-permute-start.5
  71.9 9.0 %all-to-all-done = bf16[32,8,4096]{2,1,0:T(8,128)(2,1)S(1)} async-done(((bf16[32,8,4096]{2,1,0:T(8,128)(2,1)}), bf16[32,8,4096]{2,1,0:T(8,128)(2,1)S(1)}, u32[]{:S(2)}, u32[]{:S(2)}) %all-to-all-start) | async-done | bytes 2097184 | tf_op jit(solution)/shard_map/all_to_all | solution.py:63
  80.9 10.8 %collective-permute-done.1 = bf16[128,4096]{1,0:T(8,128)(2,1)} collective-permute-done((bf16[128,4096]{1,0:T(8,128)(2,1)}, bf16[128,4096]{1,0:T(8,128)(2,1)}, u32[]{:S(2)}, u32[]{:S(2)}) %collective-permute-start.1) | collective-permute-done | bytes 1048608 | tf_op jit(solution)/shard_map/ppermute | solution.py:28
  91.7 22.5 %collective-permute-done.4 = bf16[128,4096]{1,0:T(8,128)(2,1)} collective-permute-done((bf16[128,4096]{1,0:T(8,128)(2,1)}, bf16[128,4096]{1,0:T(8,128)(2,1)}, u32[]{:S(2)}, u32[]{:S(2)}) %collective-permute-start.4) | collective-permute-done | bytes 1048608 | tf_op jit(solution)/shard_map/ppermute | solution.py:28
  114.3 1.2 collective-permute-start.8
  115.5 1.6 collective-permute-start.10
  117.0 1.4 collective-permute-start.11
  118.5 5.5 %fusion.127 = f32[2,128,384]{2,1,0:T(8,128)S(1)} fusion(bf16[128,4096]{1,0:T(8,128)(2,1)} %collective-permute-done.4, bf16[1,3,384,4096]{3,2,1,0:T(8,128)(2,1)} %param.9), kind=kOutput, calls=%fused_computation.106 | convolution fusion | flops 805306368 | bytes 7733248 | tf_op jit(solution)/shard_map/rd,kfd->krf/dot_general | solution.py:80
  124.0 2.8 convolution_convert_fusion.8
  126.8 2.8 collective-permute-start.6
  129.6 5.3 %fusion.130 = f32[2,128,384]{2,1,0:T(8,128)S(1)} fusion(bf16[128,4096]{1,0:T(8,128)(2,1)} %collective-permute-done.5, bf16[1,3,384,4096]{3,2,1,0:T(8,128)(2,1)} %param.9), kind=kOutput, calls=%fused_computation.107 | convolution fusion | flops 805306368 | bytes 7733248 | tf_op jit(solution)/shard_map/rd,kfd->krf/dot_general | solution.py:80
  135.7 3.4 fusion.124
  139.2 3.4 fusion.133
  144.1 3.4 fusion.136
  147.6 3.6 fusion.139
  151.3 9.8 %collective-permute-done.11 = bf16[128,4096]{1,0:T(8,128)(2,1)S(1)} collective-permute-done((bf16[128,4096]{1,0:T(8,128)(2,1)S(1)}, bf16[128,4096]{1,0:T(8,128)(2,1)S(1)}, u32[]{:S(2)}, u32[]{:S(2)}) %collective-permute-start.11) | collective-permute-done | bytes 1048608 | tf_op jit(solution)/shard_map/ppermute | solution.py:28
  161.0 0.9 collective-permute-start.12
  162.0 2.2 collective-permute-start.13
  165.6 0.8 copy-done.3
  166.5 1.8 fusion.119
  168.4 15.1 %collective-permute-done.6 = bf16[128,4096]{1,0:T(8,128)(2,1)S(1)} collective-permute-done((bf16[128,4096]{1,0:T(8,128)(2,1)S(1)}, bf16[128,4096]{1,0:T(8,128)(2,1)S(1)}, u32[]{:S(2)}, u32[]{:S(2)}) %collective-permute-start.6) | collective-permute-done | bytes 1048608 | tf_op jit(solution)/shard_map/ppermute | solution.py:28
  183.5 2.9 collective-permute-start.16
  186.4 20.1 %collective-permute-done.12 = bf16[128,4096]{1,0:T(8,128)(2,1)S(1)} collective-permute-done((bf16[128,4096]{1,0:T(8,128)(2,1)S(1)}, bf16[128,4096]{1,0:T(8,128)(2,1)S(1)}, u32[]{:S(2)}, u32[]{:S(2)}) %collective-permute-start.12) | collective-permute-done | bytes 1048608 | tf_op jit(solution)/shard_map/ppermute | solution.py:28
  206.5 2.1 fusion.267
  208.6 1.0 fusion.73
  209.6 2.5 collective-permute-start.18
  212.1 1.1 fusion.266
  213.2 1.1 fusion.268
  214.3 2.0 fusion.70
  216.3 1.1 fusion.269
  217.4 1.1 fusion.271
  218.5 1.0 fusion.58
  220.3 1.1 fusion.270
  221.4 1.3 fusion.248
  222.8 2.0 fusion.67
  224.7 26.3 %collective-permute-done.18 = bf16[128,4096]{1,0:T(8,128)(2,1)S(1)} collective-permute-done((bf16[128,4096]{1,0:T(8,128)(2,1)S(1)}, bf16[128,4096]{1,0:T(8,128)(2,1)S(1)}, u32[]{:S(2)}, u32[]{:S(2)}) %collective-permute-start.18) | collective-permute-done | bytes 1048608 | tf_op jit(solution)/shard_map/ppermute | solution.py:28
  251.0 2.8 collective-permute-start.14
  253.8 2.0 add_convert_fusion.1
  255.8 18.1 %collective-permute-done.22 = bf16[128,4096]{1,0:T(8,128)(2,1)S(1)} collective-permute-done((bf16[128,4096]{1,0:T(8,128)(2,1)S(1)}, bf16[128,4096]{1,0:T(8,128)(2,1)S(1)}, u32[]{:S(2)}, u32[]{:S(2)}) %collective-permute-start.22) | collective-permute-done | bytes 1048608 | tf_op jit(solution)/shard_map/ppermute | solution.py:28
  273.9 2.0 add_convert_fusion
  275.9 2.7 collective-permute-start.21
  278.9 1.5 collective-permute-start.23
  280.4 17.3 %collective-permute-done.17 = bf16[128,4096]{1,0:T(8,128)(2,1)S(1)} collective-permute-done((bf16[128,4096]{1,0:T(8,128)(2,1)S(1)}, bf16[128,4096]{1,0:T(8,128)(2,1)S(1)}, u32[]{:S(2)}, u32[]{:S(2)}) %collective-permute-start.17) | collective-permute-done | bytes 1048608 | tf_op jit(solution)/shard_map/ppermute | solution.py:28
  297.9 2.8 fusion.109
  300.7 9.3 %all-to-all-start.2 = ((bf16[32,8,4096]{2,1,0:T(8,128)(2,1)}), bf16[32,8,4096]{2,1,0:T(8,128)(2,1)S(1)}, u32[]{:S(2)}, u32[]{:S(2)}) async-start(bf16[32,8,4096]{2,1,0:T(8,128)(2,1)} %fusion.109), calls=%async_computation.2 | async-start | bytes 4194304 | tf_op jit(solution)/shard_map/all_to_all | solution.py:74
  310.0 11.4 %collective-permute-done.19 = bf16[128,4096]{1,0:T(8,128)(2,1)} collective-permute-done((bf16[128,4096]{1,0:T(8,128)(2,1)}, bf16[128,4096]{1,0:T(8,128)(2,1)}, u32[]{:S(2)}, u32[]{:S(2)}) %collective-permute-start.19) | collective-permute-done | bytes 1048608 | tf_op jit(solution)/shard_map/ppermute | solution.py:28
  321.4 1.8 convert_add_fusion.1
  323.3 1.5 convert_add_fusion
  324.7 6.1 %fusion.114 = bf16[32,8,4096]{2,1,0:T(8,128)(2,1)} fusion(f32[128,4096]{1,0:T(8,128)S(1)} %convert_add_fusion, f32[128,4096]{1,0:T(8,128)S(1)} %convert_add_fusion.1, bf16[1,256,384]{2,1,0:T(8,128)(2,1)S(1)} %get-tuple-element.47, bf16[1,256,384]{2,1,0:T(8,128)(2,1)S(1)} %get-tuple-element.46, bf16[1,3,384,4096]{3,2,1,0:T(8,128)(2,1)} %param.9), kind=kOutput, calls=%fused_computation.90 | convolution fusion | flops 1616052224 | bytes 12976128 | tf_op jit(solution)/shard_map/krf,kfd->rd/dot_general | solution.py:98
  330.8 7.6 %all-to-all-done.2 = bf16[32,8,4096]{2,1,0:T(8,128)(2,1)S(1)} async-done(((bf16[32,8,4096]{2,1,0:T(8,128)(2,1)}), bf16[32,8,4096]{2,1,0:T(8,128)(2,1)S(1)}, u32[]{:S(2)}, u32[]{:S(2)}) %all-to-all-start.2) | async-done | bytes 2097184 | tf_op jit(solution)/shard_map/all_to_all | solution.py:74
  338.3 5.2 %all-to-all-start.3 = ((bf16[32,8,4096]{2,1,0:T(8,128)(2,1)}), bf16[32,8,4096]{2,1,0:T(8,128)(2,1)}, u32[]{:S(2)}, u32[]{:S(2)}) async-start(bf16[32,8,4096]{2,1,0:T(8,128)(2,1)} %fusion.114), calls=%async_computation.3 | async-start | bytes 4194304 | tf_op jit(solution)/shard_map/all_to_all | solution.py:74
  343.6 3.5 fusion.113
  347.1 24.9 %all-to-all-done.3 = bf16[32,8,4096]{2,1,0:T(8,128)(2,1)} async-done(((bf16[32,8,4096]{2,1,0:T(8,128)(2,1)}), bf16[32,8,4096]{2,1,0:T(8,128)(2,1)}, u32[]{:S(2)}, u32[]{:S(2)}) %all-to-all-start.3) | async-done | bytes 2097184 | tf_op jit(solution)/shard_map/all_to_all | solution.py:74
  372.0 3.1 convolution_convert_fusion.3
  (65 shorter events, 7.3 us)
Async XLA Ops:
  0.6 1.9 copy-start
  40.8 1.4 copy-start.2
  42.2 3.8 %copy-start.4 = (bf16[128,4096]{1,0:T(8,128)(2,1)S(1)}, bf16[128,4096]{1,0:T(8,128)(2,1)}, u32[]{:S(2)}) copy-start(bf16[128,4096]{1,0:T(8,128)(2,1)} %param.6) | copy-start | bytes 3145732
  42.2 3.8 %copy-start.5 = (f32[128]{0:T(128)S(1)}, f32[128]{0:T(128)}, u32[]{:S(2)}) copy-start(f32[128]{0:T(128)} %param.8) | copy-start | bytes 1540
  43.3 25.9 %collective-permute-start = (bf16[128,4096]{1,0:T(8,128)(2,1)S(1)}, bf16[128,4096]{1,0:T(8,128)(2,1)}, u32[]{:S(2)}, u32[]{:S(2)}) collective-permute-start(bf16[128,4096]{1,0:T(8,128)(2,1)S(1)} %get-tuple-element.45), channel_id=1, source_target_pairs={{0,32},{32,64},{64,96},{96,0},{1,33},{33,65},{65,97},{97,1},{2,34}... | collective-permute-start | bytes 3145736 | tf_op jit(solution)/shard_map/ppermute | solution.py:28
  44.5 24.7 %collective-permute-start.3 = (bf16[128,4096]{1,0:T(8,128)(2,1)}, bf16[128,4096]{1,0:T(8,128)(2,1)}, u32[]{:S(2)}, u32[]{:S(2)}) collective-permute-start(bf16[128,4096]{1,0:T(8,128)(2,1)} %get-tuple-element.44), channel_id=1, source_target_pairs={{0,96},{32,0},{64,32},{96,64},{1,97},{33,1},{65,33},{97,65},{2,98}... | collective-permute-start | bytes 3145736 | tf_op jit(solution)/shard_map/ppermute | solution.py:28
  48.1 32.8 %all-to-all-start = ((bf16[32,8,4096]{2,1,0:T(8,128)(2,1)}), bf16[32,8,4096]{2,1,0:T(8,128)(2,1)S(1)}, u32[]{:S(2)}, u32[]{:S(2)}) async-start(bf16[32,8,4096]{2,1,0:T(8,128)(2,1)} %fusion.38), calls=%async_computation | async-start | bytes 4194304 | tf_op jit(solution)/shard_map/all_to_all | solution.py:63
  52.6 39.1 %collective-permute-start.1 = (bf16[128,4096]{1,0:T(8,128)(2,1)}, bf16[128,4096]{1,0:T(8,128)(2,1)}, u32[]{:S(2)}, u32[]{:S(2)}) collective-permute-start(bf16[128,4096]{1,0:T(8,128)(2,1)} %get-tuple-element.44), channel_id=1, source_target_pairs={{0,32},{32,64},{64,96},{96,0},{1,33},{33,65},{65,97},{97,1},{2,34}... | collective-permute-start | bytes 3145736 | tf_op jit(solution)/shard_map/ppermute | solution.py:28
  52.7 39.0 %collective-permute-start.2 = (bf16[128,4096]{1,0:T(8,128)(2,1)S(1)}, bf16[128,4096]{1,0:T(8,128)(2,1)}, u32[]{:S(2)}, u32[]{:S(2)}) collective-permute-start(bf16[128,4096]{1,0:T(8,128)(2,1)S(1)} %get-tuple-element.45), channel_id=1, source_target_pairs={{0,96},{32,0},{64,32},{96,64},{1,97},{33,1},{65,33},{97,65},{2,98}... | collective-permute-start | bytes 3145736 | tf_op jit(solution)/shard_map/ppermute | solution.py:28
  69.2 44.9 %collective-permute-start.4 = (bf16[128,4096]{1,0:T(8,128)(2,1)}, bf16[128,4096]{1,0:T(8,128)(2,1)}, u32[]{:S(2)}, u32[]{:S(2)}) collective-permute-start(bf16[128,4096]{1,0:T(8,128)(2,1)} %collective-permute-done), channel_id=1, source_target_pairs={{0,32},{32,64},{64,96},{96,0},{1,33},{33,65},{65,97},{97,1},{2,34}... | collective-permute-start | bytes 3145736 | tf_op jit(solution)/shard_map/ppermute | solution.py:28
  69.2 44.9 %collective-permute-start.5 = (bf16[128,4096]{1,0:T(8,128)(2,1)}, bf16[128,4096]{1,0:T(8,128)(2,1)}, u32[]{:S(2)}, u32[]{:S(2)}) collective-permute-start(bf16[128,4096]{1,0:T(8,128)(2,1)} %collective-permute-done.3), channel_id=1, source_target_pairs={{0,96},{32,0},{64,32},{96,64},{1,97},{33,1},{65,33},{97,65},{2,98}... | collective-permute-start | bytes 3145736 | tf_op jit(solution)/shard_map/ppermute | solution.py:28
  114.3 36.9 %collective-permute-start.8 = (bf16[128,4096]{1,0:T(8,128)(2,1)S(1)}, bf16[128,4096]{1,0:T(8,128)(2,1)S(1)}, u32[]{:S(2)}, u32[]{:S(2)}) collective-permute-start(bf16[128,4096]{1,0:T(8,128)(2,1)S(1)} %get-tuple-element.43), channel_id=1, source_target_pairs={{0,32},{32,64},{64,96},{96,0},{1,33},{33,65},{65,97},{97,1},{2,34}... | collective-permute-start | bytes 3145736 | tf_op jit(solution)/shard_map/ppermute | solution.py:28
  115.5 46.5 %collective-permute-start.10 = (bf16[128,4096]{1,0:T(8,128)(2,1)S(1)}, bf16[128,4096]{1,0:T(8,128)(2,1)S(1)}, u32[]{:S(2)}, u32[]{:S(2)}) collective-permute-start(bf16[128,4096]{1,0:T(8,128)(2,1)S(1)} %get-tuple-element.43), channel_id=1, source_target_pairs={{0,96},{32,0},{64,32},{96,64},{1,97},{33,1},{65,33},{97,65},{2,98}... | collective-permute-start | bytes 3145736 | tf_op jit(solution)/shard_map/ppermute | solution.py:28
  117.0 44.0 %collective-permute-start.11 = (bf16[128,4096]{1,0:T(8,128)(2,1)S(1)}, bf16[128,4096]{1,0:T(8,128)(2,1)S(1)}, u32[]{:S(2)}, u32[]{:S(2)}) collective-permute-start(bf16[128,4096]{1,0:T(8,128)(2,1)S(1)} %get-tuple-element.42), channel_id=1, source_target_pairs={{0,96},{32,0},{64,32},{96,64},{1,97},{33,1},{65,33},{97,65},{2,98}... | collective-permute-start | bytes 3145736 | tf_op jit(solution)/shard_map/ppermute | solution.py:28
  118.4 49.9 %collective-permute-start.9 = (bf16[128,4096]{1,0:T(8,128)(2,1)S(1)}, bf16[128,4096]{1,0:T(8,128)(2,1)S(1)}, u32[]{:S(2)}, u32[]{:S(2)}) collective-permute-start(bf16[128,4096]{1,0:T(8,128)(2,1)S(1)} %get-tuple-element.42), channel_id=1, source_target_pairs={{0,32},{32,64},{64,96},{96,0},{1,33},{33,65},{65,97},{97,1},{2,34}... | collective-permute-start | bytes 3145736 | tf_op jit(solution)/shard_map/ppermute | solution.py:28
  118.5 16.4 %slice-start = ((s8[9437184]{0:T(1024)(128)(4,1)}), s8[4194304]{0:T(1024)(128)(4,1)S(1)}, s32[]{:S(2)}) async-start(s8[9437184]{0:T(1024)(128)(4,1)} %bitcast.541), calls=%async_computation.4 | async-start | bytes 8388608
  118.5 16.4 %slice-start.1 = ((s8[9437184]{0:T(1024)(128)(4,1)}), s8[4194304]{0:T(1024)(128)(4,1)S(1)}, s32[]{:S(2)}) async-start(s8[9437184]{0:T(1024)(128)(4,1)} %bitcast.541), calls=%async_computation.5 | async-start | bytes 8388608
  124.0 11.0 %copy-start.10 = (f32[2,128,384]{2,1,0:T(8,128)}, f32[2,128,384]{2,1,0:T(8,128)S(1)}, u32[]{:S(2)}) copy-start(f32[2,128,384]{2,1,0:T(8,128)S(1)} %fusion.127) | copy-start | bytes 1179652
  126.8 8.2 %slice-start.2 = ((s8[9437184]{0:T(1024)(128)(4,1)}), s8[1048576]{0:T(1024)(128)(4,1)S(1)}, s32[]{:S(2)}) async-start(s8[9437184]{0:T(1024)(128)(4,1)} %bitcast.541), calls=%async_computation.6 | async-start | bytes 2097152
  126.8 56.7 %collective-permute-start.6 = (bf16[128,4096]{1,0:T(8,128)(2,1)S(1)}, bf16[128,4096]{1,0:T(8,128)(2,1)S(1)}, u32[]{:S(2)}, u32[]{:S(2)}) collective-permute-start(bf16[128,4096]{1,0:T(8,128)(2,1)S(1)} %convolution_convert_fusion.8), channel_id=1, source_target_pairs={{0,96},{32,0},{64,32},{96,64},{1,97},{33,1},{65,33},{97,65},{2,98}... | collective-permute-start | bytes 3145736 | tf_op jit(solution)/shard_map/ppermute | solution.py:28
  142.6 1.5 copy-start.8
  147.6 16.6 %copy-start.6 = (f32[2,128,384]{2,1,0:T(8,128)}, f32[2,128,384]{2,1,0:T(8,128)S(1)}, u32[]{:S(2)}) copy-start(f32[2,128,384]{2,1,0:T(8,128)S(1)} %fusion.136) | copy-start | bytes 1179652
  151.2 35.2 %collective-permute-start.7 = (bf16[128,4096]{1,0:T(8,128)(2,1)S(1)}, bf16[128,4096]{1,0:T(8,128)(2,1)S(1)}, u32[]{:S(2)}, u32[]{:S(2)}) collective-permute-start(bf16[128,4096]{1,0:T(8,128)(2,1)S(1)} %convolution_convert_fusion.7), channel_id=1, source_target_pairs={{0,32},{32,64},{64,96},{96,0},{1,33},{33,65},{65,97},{97,1},{2,34}... | collective-permute-start | bytes 3145736 | tf_op jit(solution)/shard_map/ppermute | solution.py:28
  161.0 45.4 %collective-permute-start.12 = (bf16[128,4096]{1,0:T(8,128)(2,1)S(1)}, bf16[128,4096]{1,0:T(8,128)(2,1)S(1)}, u32[]{:S(2)}, u32[]{:S(2)}) collective-permute-start(bf16[128,4096]{1,0:T(8,128)(2,1)S(1)} %collective-permute-done.8), channel_id=1, source_target_pairs={{0,32},{32,64},{64,96},{96,0},{1,33},{33,65},{65,97},{97,1},{2,34}... | collective-permute-start | bytes 3145736 | tf_op jit(solution)/shard_map/ppermute | solution.py:28
  162.0 44.5 %collective-permute-start.13 = (bf16[128,4096]{1,0:T(8,128)(2,1)S(1)}, bf16[128,4096]{1,0:T(8,128)(2,1)S(1)}, u32[]{:S(2)}, u32[]{:S(2)}) collective-permute-start(bf16[128,4096]{1,0:T(8,128)(2,1)S(1)} %collective-permute-done.11), channel_id=1, source_target_pairs={{0,96},{32,0},{64,32},{96,64},{1,97},{33,1},{65,33},{97,65},{2,98}... | collective-permute-start | bytes 3145736 | tf_op jit(solution)/shard_map/ppermute | solution.py:28
  164.9 1.6 copy-start.3
  168.3 107.6 %collective-permute-start.15 = (bf16[128,4096]{1,0:T(8,128)(2,1)S(1)}, bf16[128,4096]{1,0:T(8,128)(2,1)S(1)}, u32[]{:S(2)}, u32[]{:S(2)}) collective-permute-start(bf16[128,4096]{1,0:T(8,128)(2,1)S(1)} %convolution_convert_fusion.6), channel_id=1, source_target_pairs={{0,32},{32,64},{64,96},{96,0},{1,33},{33,65},{65,97},{97,1},{2,34}... | collective-permute-start | bytes 3145736 | tf_op jit(solution)/shard_map/ppermute | solution.py:28
  183.5 95.4 %collective-permute-start.16 = (bf16[128,4096]{1,0:T(8,128)(2,1)S(1)}, bf16[128,4096]{1,0:T(8,128)(2,1)S(1)}, u32[]{:S(2)}, u32[]{:S(2)}) collective-permute-start(bf16[128,4096]{1,0:T(8,128)(2,1)S(1)} %convolution_convert_fusion.5), channel_id=1, source_target_pairs={{0,96},{32,0},{64,32},{96,64},{1,97},{33,1},{65,33},{97,65},{2,98}... | collective-permute-start | bytes 3145736 | tf_op jit(solution)/shard_map/ppermute | solution.py:28
  209.6 3.6 copy-start.9
  209.6 41.4 %collective-permute-start.18 = (bf16[128,4096]{1,0:T(8,128)(2,1)S(1)}, bf16[128,4096]{1,0:T(8,128)(2,1)S(1)}, u32[]{:S(2)}, u32[]{:S(2)}) collective-permute-start(bf16[128,4096]{1,0:T(8,128)(2,1)S(1)} %fusion.73), channel_id=1, source_target_pairs={{0,96},{32,0},{64,32},{96,64},{1,97},{33,1},{65,33},{97,65},{2,98}... | collective-permute-start | bytes 3145736 | tf_op jit(solution)/shard_map/ppermute | solution.py:28
  214.3 2.0 copy-start.7
  216.3 93.7 %collective-permute-start.20 = (bf16[128,4096]{1,0:T(8,128)(2,1)}, bf16[128,4096]{1,0:T(8,128)(2,1)}, u32[]{:S(2)}, u32[]{:S(2)}) collective-permute-start(bf16[128,4096]{1,0:T(8,128)(2,1)} %fusion.70), channel_id=1, source_target_pairs={{0,32},{32,64},{64,96},{96,0},{1,33},{33,65},{65,97},{97,1},{2,34}... | collective-permute-start | bytes 3145736 | tf_op jit(solution)/shard_map/ppermute | solution.py:28
  219.5 54.4 %collective-permute-start.22 = (bf16[128,4096]{1,0:T(8,128)(2,1)S(1)}, bf16[128,4096]{1,0:T(8,128)(2,1)S(1)}, u32[]{:S(2)}, u32[]{:S(2)}) collective-permute-start(bf16[128,4096]{1,0:T(8,128)(2,1)S(1)} %fusion.58), channel_id=1, source_target_pairs={{0,32},{32,64},{64,96},{96,0},{1,33},{33,65},{65,97},{97,1},{2,34}... | collective-permute-start | bytes 3145736 | tf_op jit(solution)/shard_map/ppermute | solution.py:28
  251.0 27.5 %collective-permute-start.14 = (bf16[128,4096]{1,0:T(8,128)(2,1)S(1)}, bf16[128,4096]{1,0:T(8,128)(2,1)S(1)}, u32[]{:S(2)}, u32[]{:S(2)}) collective-permute-start(bf16[128,4096]{1,0:T(8,128)(2,1)S(1)} %add_convert_fusion.3), channel_id=1, source_target_pairs={{0,96},{32,0},{64,32},{96,64},{1,97},{33,1},{65,33},{97,65},{2,98}... | collective-permute-start | bytes 3145736 | tf_op jit(solution)/shard_map/ppermute | solution.py:28
  273.9 23.8 %collective-permute-start.17 = (bf16[128,4096]{1,0:T(8,128)(2,1)S(1)}, bf16[128,4096]{1,0:T(8,128)(2,1)S(1)}, u32[]{:S(2)}, u32[]{:S(2)}) collective-permute-start(bf16[128,4096]{1,0:T(8,128)(2,1)S(1)} %add_convert_fusion.2), channel_id=1, source_target_pairs={{0,32},{32,64},{64,96},{96,0},{1,33},{33,65},{65,97},{97,1},{2,34}... | collective-permute-start | bytes 3145736 | tf_op jit(solution)/shard_map/ppermute | solution.py:28
  275.9 47.4 %collective-permute-start.21 = (bf16[128,4096]{1,0:T(8,128)(2,1)}, bf16[128,4096]{1,0:T(8,128)(2,1)S(1)}, u32[]{:S(2)}, u32[]{:S(2)}) collective-permute-start(bf16[128,4096]{1,0:T(8,128)(2,1)} %fusion.67), channel_id=1, source_target_pairs={{0,96},{32,0},{64,32},{96,64},{1,97},{33,1},{65,33},{97,65},{2,98}... | collective-permute-start | bytes 3145736 | tf_op jit(solution)/shard_map/ppermute | solution.py:28
  278.6 42.9 %collective-permute-start.19 = (bf16[128,4096]{1,0:T(8,128)(2,1)}, bf16[128,4096]{1,0:T(8,128)(2,1)}, u32[]{:S(2)}, u32[]{:S(2)}) collective-permute-start(bf16[128,4096]{1,0:T(8,128)(2,1)} %add_convert_fusion.1), channel_id=1, source_target_pairs={{0,96},{32,0},{64,32},{96,64},{1,97},{33,1},{65,33},{97,65},{2,98}... | collective-permute-start | bytes 3145736 | tf_op jit(solution)/shard_map/ppermute | solution.py:28
  278.9 44.3 %collective-permute-start.23 = (bf16[128,4096]{1,0:T(8,128)(2,1)}, bf16[128,4096]{1,0:T(8,128)(2,1)}, u32[]{:S(2)}, u32[]{:S(2)}) collective-permute-start(bf16[128,4096]{1,0:T(8,128)(2,1)} %add_convert_fusion), channel_id=1, source_target_pairs={{0,32},{32,64},{64,96},{96,0},{1,33},{33,65},{65,97},{97,1},{2,34}... | collective-permute-start | bytes 3145736 | tf_op jit(solution)/shard_map/ppermute | solution.py:28
  300.7 37.7 %all-to-all-start.2 = ((bf16[32,8,4096]{2,1,0:T(8,128)(2,1)}), bf16[32,8,4096]{2,1,0:T(8,128)(2,1)S(1)}, u32[]{:S(2)}, u32[]{:S(2)}) async-start(bf16[32,8,4096]{2,1,0:T(8,128)(2,1)} %fusion.109), calls=%async_computation.2 | async-start | bytes 4194304 | tf_op jit(solution)/shard_map/all_to_all | solution.py:74
  338.3 33.6 %all-to-all-start.3 = ((bf16[32,8,4096]{2,1,0:T(8,128)(2,1)}), bf16[32,8,4096]{2,1,0:T(8,128)(2,1)}, u32[]{:S(2)}, u32[]{:S(2)}) async-start(bf16[32,8,4096]{2,1,0:T(8,128)(2,1)} %fusion.114), calls=%async_computation.3 | async-start | bytes 4194304 | tf_op jit(solution)/shard_map/all_to_all | solution.py:74
  343.6 31.5 %copy-start.1 = (bf16[128,4096]{1,0:T(8,128)(2,1)S(1)}, bf16[128,4096]{1,0:T(8,128)(2,1)}, u32[]{:S(2)}) copy-start(bf16[128,4096]{1,0:T(8,128)(2,1)} %param.5) | copy-start | bytes 3145732
where the time goes:
time: 383 us; the launch traced here: 375 us
  waiting for transfers between devices  207 us (54%)
  matrix products  70 us (18%)
  starting transfers between devices  50 us (13%)
  blocking collectives  37.5 us (10%)
  other arithmetic  6.07 us (2%)
    ppermute x24, waiting for transfers between devices, shifted(): lax.ppermute(values, 'dp', perm=[(i, (i + step) % n) for i in range(n)])  165 us
    all_to_all x1, blocking collectives, arrive_rows(): lax.all_to_all(cold_buf.reshape(experts, slot_count, model_width), 'exper...  37.5 us
    all_to_all x2, waiting for transfers between devices, return_rows(): lax.all_to_all(summed, 'expert', split_axis=0, concat_axis=0, tiled=True)  32.4 us
    ppermute x24, starting transfers between devices, shifted(): lax.ppermute(values, 'dp', perm=[(i, (i + step) % n) for i in range(n)])  31.1 us
    dot_general x7, matrix products, forward_rows(): jnp.einsum('rd,kfd->krf', row_block, matrices[:2], preferred_element_type...  26.5 us
    dot_general x7, matrix products, backward_rows(): jnp.einsum('krf,kfd->rd', both_grads, matrices[:2], preferred_element_typ...  16 us
    all_to_all x2, starting transfers between devices, return_rows(): lax.all_to_all(summed, 'expert', split_axis=0, concat_axis=0, tiled=True)  14.5 us
    dot_general x7, matrix products, forward_rows(): jnp.dot(hidden, matrices[2], preferred_element_type=jnp.float32)  9.16 us
  transfers between devices with their start and end apart: 27, of which 13 were waited for; matrix products, arithmetic and copies ran while one was open for 19% of the time, Pallas kernels for 0%

commit v1 on v0

--- a/solution.py
+++ b/solution.py
@@ -119,13 +119,15 @@
     cot_blocks = group_rows(cold_grad_arrived)
     fwd_received = sum_start(fwd_parts)
     fwd_received, cot_blocks = lax.optimization_barrier((fwd_received, cot_blocks))
-    cold_out = return_rows(sum_finish(fwd_parts, fwd_received), experts, capacity, model_width)
+    fwd_total = sum_finish(fwd_parts, fwd_received)
+    grad_parts = [
+        backward_rows(block, f[0], f[1], weights) for block, f in zip(cot_blocks, forward)
+    ]
+    fwd_total, grad_parts = lax.optimization_barrier((fwd_total, grad_parts))
+    cold_out = return_rows(fwd_total, experts, capacity, model_width)
     expert_out = collect(cold_layout, cold_out)
     combined = (combine[:, None] * expert_out).astype(jnp.bfloat16)
     combine_grad = jnp.sum(expert_out * cotangent_wide, 1)
-    grad_parts = [
-        backward_rows(block, f[0], f[1], weights) for block, f in zip(cot_blocks, forward)
-    ]
     grad_total = sum_finish(grad_parts, sum_start(grad_parts))
     cold_grad_out = return_rows(grad_total, experts, capacity, model_width)
     input_grad = collect(cold_layout, cold_grad_out)

time: 383 us -> 376 us (0.982)
  waiting for transfers between devices: 207 us -> 198 us
  matrix products: 70 us -> 65.8 us
    all_to_all x2, waiting for transfers between devices: 32.4 us -> 24.9 us  [return_rows(): lax.all_to_all(summed, 'expert', split_axis=0, concat_axis=0, tiled=True)]
    dot_general x7, matrix products: 16 us -> 11.2 us  [backward_rows(): jnp.einsum('krf,kfd->rd', both_grads, matrices[:2], preferred_element_typ...]
  transfers between devices with their start and end apart: 27 -> 27, of which waited for: 13 -> 14; matrix products, arithmetic and copies ran while one was open for 19% -> 18% of each run, Pallas kernels for 0% -> 0%
where the time goes in v1:
time: 376 us; the launch traced here: 369 us
  waiting for transfers between devices  198 us (53%)
  matrix products  65.8 us (18%)
  starting transfers between devices  52.6 us (14%)
  blocking collectives  37.6 us (10%)
  other arithmetic  9.87 us (3%)
    ppermute x24, waiting for transfers between devices, shifted(): lax.ppermute(values, 'dp', perm=[(i, (i + step) % n) for i in range(n)])  164 us
    all_to_all x1, blocking collectives, arrive_rows(): lax.all_to_all(cold_buf.reshape(experts, slot_count, model_width), 'exper...  37.6 us
    ppermute x24, starting transfers between devices, shifted(): lax.ppermute(values, 'dp', perm=[(i, (i + step) % n) for i in range(n)])  31.9 us
    dot_general x7, matrix products, forward_rows(): jnp.einsum('rd,kfd->krf', row_block, matrices[:2], preferred_element_type...  27.3 us
    all_to_all x2, waiting for transfers between devices, return_rows(): lax.all_to_all(summed, 'expert', split_axis=0, concat_axis=0, tiled=True)  24.9 us
    all_to_all x2, starting transfers between devices, return_rows(): lax.all_to_all(summed, 'expert', split_axis=0, concat_axis=0, tiled=True)  16.2 us
    dot_general x7, matrix products, backward_rows(): jnp.einsum('krf,kfd->rd', both_grads, matrices[:2], preferred_element_typ...  11.2 us
    dot_general x7, matrix products, forward_rows(): jnp.dot(hidden, matrices[2], preferred_element_type=jnp.float32)  9.01 us
  transfers between devices with their start and end apart: 27, of which 14 were waited for; matrix products, arithmetic and copies ran while one was open for 18% of the time, Pallas kernels for 0%

profile of v1, /device:TPU:1, one launch (start us, length us, event | category | flops | bytes accessed | tf_op | source)
XLA Modules:
  0.0 369.0 jit_solution(10986242033983879050)
XLA Ops:
  3.3 37.6 %all_to_all.20 = bf16[32,8,4096]{2,1,0:T(8,128)(2,1)S(1)} all-to-all(bf16[32,8,4096]{2,1,0:T(8,128)(2,1)S(1)} %fusion.33), channel_id=1, replica_groups=mesh['dp'=4,'expert'=32] {'expert'}, dimensions={0} | all-to-all | bytes 4194304 | tf_op jit(solution)/shard_map/all_to_all | solution.py:63
  40.8 1.4 copy-done.2
  42.2 1.1 slice_bitcast_fusion
  43.3 1.2 collective-permute-start
  44.5 1.5 collective-permute-start.3
  46.0 2.1 fusion.32
  48.1 4.5 %all-to-all-start = ((bf16[32,8,4096]{2,1,0:T(8,128)(2,1)}), bf16[32,8,4096]{2,1,0:T(8,128)(2,1)S(1)}, u32[]{:S(2)}, u32[]{:S(2)}) async-start(bf16[32,8,4096]{2,1,0:T(8,128)(2,1)} %fusion.32), calls=%async_computation | async-start | bytes 4194304 | tf_op jit(solution)/shard_map/all_to_all | solution.py:63
  52.7 2.7 collective-permute-start.2
  55.3 13.9 %collective-permute-done = bf16[128,4096]{1,0:T(8,128)(2,1)} collective-permute-done((bf16[128,4096]{1,0:T(8,128)(2,1)S(1)}, bf16[128,4096]{1,0:T(8,128)(2,1)}, u32[]{:S(2)}, u32[]{:S(2)}) %collective-permute-start) | collective-permute-done | bytes 1048608 | tf_op jit(solution)/shard_map/ppermute | solution.py:28
  69.2 2.7 collective-permute-start.5
  71.9 9.0 %all-to-all-done = bf16[32,8,4096]{2,1,0:T(8,128)(2,1)S(1)} async-done(((bf16[32,8,4096]{2,1,0:T(8,128)(2,1)}), bf16[32,8,4096]{2,1,0:T(8,128)(2,1)S(1)}, u32[]{:S(2)}, u32[]{:S(2)}) %all-to-all-start) | async-done | bytes 2097184 | tf_op jit(solution)/shard_map/all_to_all | solution.py:63
  80.9 10.8 %collective-permute-done.1 = bf16[128,4096]{1,0:T(8,128)(2,1)} collective-permute-done((bf16[128,4096]{1,0:T(8,128)(2,1)}, bf16[128,4096]{1,0:T(8,128)(2,1)}, u32[]{:S(2)}, u32[]{:S(2)}) %collective-permute-start.1) | collective-permute-done | bytes 1048608 | tf_op jit(solution)/shard_map/ppermute | solution.py:28
  91.7 22.5 %collective-permute-done.4 = bf16[128,4096]{1,0:T(8,128)(2,1)} collective-permute-done((bf16[128,4096]{1,0:T(8,128)(2,1)}, bf16[128,4096]{1,0:T(8,128)(2,1)}, u32[]{:S(2)}, u32[]{:S(2)}) %collective-permute-start.4) | collective-permute-done | bytes 1048608 | tf_op jit(solution)/shard_map/ppermute | solution.py:28
  114.3 1.2 collective-permute-start.8
  115.5 1.6 collective-permute-start.10
  117.0 1.4 collective-permute-start.11
  118.5 5.5 %fusion.93 = f32[2,128,384]{2,1,0:T(8,128)S(1)} fusion(bf16[128,4096]{1,0:T(8,128)(2,1)} %collective-permute-done.4, bf16[1,3,384,4096]{3,2,1,0:T(8,128)(2,1)} %param.9), kind=kOutput, calls=%fused_computation.95 | convolution fusion | flops 805306368 | bytes 7733248 | tf_op jit(solution)/shard_map/rd,kfd->krf/dot_general | solution.py:80
  124.0 2.6 convolution_convert_fusion.8
  126.6 2.8 collective-permute-start.6
  129.4 5.3 %fusion.96 = f32[2,128,384]{2,1,0:T(8,128)S(1)} fusion(bf16[128,4096]{1,0:T(8,128)(2,1)} %collective-permute-done.5, bf16[1,3,384,4096]{3,2,1,0:T(8,128)(2,1)} %param.9), kind=kOutput, calls=%fused_computation.96 | convolution fusion | flops 805306368 | bytes 7733248 | tf_op jit(solution)/shard_map/rd,kfd->krf/dot_general | solution.py:80
  135.6 3.4 fusion.99
  139.0 3.4 fusion.90
  144.0 3.4 fusion.105
  147.4 3.4 fusion.102
  151.0 10.1 %collective-permute-done.11 = bf16[128,4096]{1,0:T(8,128)(2,1)S(1)} collective-permute-done((bf16[128,4096]{1,0:T(8,128)(2,1)S(1)}, bf16[128,4096]{1,0:T(8,128)(2,1)S(1)}, u32[]{:S(2)}, u32[]{:S(2)}) %collective-permute-start.11) | collective-permute-done | bytes 1048608 | tf_op jit(solution)/shard_map/ppermute | solution.py:28
  161.0 0.9 collective-permute-start.12
  162.0 2.2 collective-permute-start.13
  166.5 2.7 fusion.85
  169.2 14.3 %collective-permute-done.6 = bf16[128,4096]{1,0:T(8,128)(2,1)S(1)} collective-permute-done((bf16[128,4096]{1,0:T(8,128)(2,1)S(1)}, bf16[128,4096]{1,0:T(8,128)(2,1)S(1)}, u32[]{:S(2)}, u32[]{:S(2)}) %collective-permute-start.6) | collective-permute-done | bytes 1048608 | tf_op jit(solution)/shard_map/ppermute | solution.py:28
  183.5 2.9 collective-permute-start.16
  186.4 20.1 %collective-permute-done.12 = bf16[128,4096]{1,0:T(8,128)(2,1)S(1)} collective-permute-done((bf16[128,4096]{1,0:T(8,128)(2,1)S(1)}, bf16[128,4096]{1,0:T(8,128)(2,1)S(1)}, u32[]{:S(2)}, u32[]{:S(2)}) %collective-permute-start.12) | collective-permute-done | bytes 1048608 | tf_op jit(solution)/shard_map/ppermute | solution.py:28
  206.5 2.1 fusion.225
  208.6 1.1 fusion.224
  209.7 1.1 fusion.223
  210.8 1.1 fusion.222
  211.9 1.1 fusion.221
  213.0 1.1 fusion.220
  214.4 2.5 collective-permute-start.14
  217.4 1.0 fusion.49
  218.4 1.0 fusion.46
  219.4 1.0 fusion.43
  220.4 2.0 fusion.40
  222.4 2.0 fusion.37
  224.4 1.3 fusion.202
  225.7 3.2 fusion.28
  228.9 1.0 fusion.34
  229.9 21.0 %collective-permute-done.14 = bf16[128,4096]{1,0:T(8,128)(2,1)S(1)} collective-permute-done((bf16[128,4096]{1,0:T(8,128)(2,1)S(1)}, bf16[128,4096]{1,0:T(8,128)(2,1)S(1)}, u32[]{:S(2)}, u32[]{:S(2)}) %collective-permute-start.14) | collective-permute-done | bytes 1048608 | tf_op jit(solution)/shard_map/ppermute | solution.py:28
  251.7 2.7 maximum_add_fusion
  254.4 2.7 collective-permute-start.18
  257.1 20.1 %collective-permute-done.18 = bf16[128,4096]{1,0:T(8,128)(2,1)S(1)} collective-permute-done((bf16[128,4096]{1,0:T(8,128)(2,1)S(1)}, bf16[128,4096]{1,0:T(8,128)(2,1)S(1)}, u32[]{:S(2)}, u32[]{:S(2)}) %collective-permute-start.18) | collective-permute-done | bytes 1048608 | tf_op jit(solution)/shard_map/ppermute | solution.py:28
  277.5 3.5 collective-permute-start.19
  281.1 1.2 add_convert_fusion
  282.3 1.7 collective-permute-start.23
  284.0 8.3 %all-to-all-start.2 = ((bf16[32,8,4096]{2,1,0:T(8,128)(2,1)}), bf16[32,8,4096]{2,1,0:T(8,128)(2,1)S(1)}, u32[]{:S(2)}, u32[]{:S(2)}) async-start(bf16[32,8,4096]{2,1,0:T(8,128)(2,1)} %bitcast.490), calls=%async_computation.2 | async-start | bytes 4194304 | tf_op jit(solution)/shard_map/all_to_all | solution.py:74
  292.3 10.6 %collective-permute-done.20 = bf16[128,4096]{1,0:T(8,128)(2,1)} collective-permute-done((bf16[128,4096]{1,0:T(8,128)(2,1)}, bf16[128,4096]{1,0:T(8,128)(2,1)}, u32[]{:S(2)}, u32[]{:S(2)}) %collective-permute-start.20) | collective-permute-done | bytes 1048608 | tf_op jit(solution)/shard_map/ppermute | solution.py:28
  302.9 1.8 convert_add_fusion.1
  304.7 18.0 %collective-permute-done.21 = bf16[128,4096]{1,0:T(8,128)(2,1)} collective-permute-done((bf16[128,4096]{1,0:T(8,128)(2,1)}, bf16[128,4096]{1,0:T(8,128)(2,1)}, u32[]{:S(2)}, u32[]{:S(2)}) %collective-permute-start.21) | collective-permute-done | bytes 1048608 | tf_op jit(solution)/shard_map/ppermute | solution.py:28
  322.7 2.6 collective-permute-done.23
  325.4 1.8 convert_add_fusion
  327.2 1.9 fusion.80
  329.1 7.9 %all-to-all-start.3 = ((bf16[32,8,4096]{2,1,0:T(8,128)(2,1)}), bf16[32,8,4096]{2,1,0:T(8,128)(2,1)}, u32[]{:S(2)}, u32[]{:S(2)}) async-start(bf16[32,8,4096]{2,1,0:T(8,128)(2,1)} %fusion.80), calls=%async_computation.3 | async-start | bytes 4194304 | tf_op jit(solution)/shard_map/all_to_all | solution.py:74
  337.0 3.5 fusion.79
  340.6 24.9 %all-to-all-done.3 = bf16[32,8,4096]{2,1,0:T(8,128)(2,1)} async-done(((bf16[32,8,4096]{2,1,0:T(8,128)(2,1)}), bf16[32,8,4096]{2,1,0:T(8,128)(2,1)}, u32[]{:S(2)}, u32[]{:S(2)}) %all-to-all-start.3) | async-done | bytes 2097184 | tf_op jit(solution)/shard_map/all_to_all | solution.py:74
  365.4 3.1 convolution_convert_fusion.3
  (64 shorter events, 9.5 us)
Async XLA Ops:
  0.6 1.9 copy-start
  40.8 1.4 copy-start.2
  42.2 3.8 %copy-start.4 = (bf16[128,4096]{1,0:T(8,128)(2,1)S(1)}, bf16[128,4096]{1,0:T(8,128)(2,1)}, u32[]{:S(2)}) copy-start(bf16[128,4096]{1,0:T(8,128)(2,1)} %param.6) | copy-start | bytes 3145732
  42.2 3.8 %copy-start.6 = (f32[128]{0:T(128)S(1)}, f32[128]{0:T(128)}, u32[]{:S(2)}) copy-start(f32[128]{0:T(128)} %param.8) | copy-start | bytes 1540
  43.3 25.9 %collective-permute-start = (bf16[128,4096]{1,0:T(8,128)(2,1)S(1)}, bf16[128,4096]{1,0:T(8,128)(2,1)}, u32[]{:S(2)}, u32[]{:S(2)}) collective-permute-start(bf16[128,4096]{1,0:T(8,128)(2,1)S(1)} %get-tuple-element.61), channel_id=1, source_target_pairs={{0,32},{32,64},{64,96},{96,0},{1,33},{33,65},{65,97},{97,1},{2,34}... | collective-permute-start | bytes 3145736 | tf_op jit(solution)/shard_map/ppermute | solution.py:28
  44.5 24.7 %collective-permute-start.3 = (bf16[128,4096]{1,0:T(8,128)(2,1)}, bf16[128,4096]{1,0:T(8,128)(2,1)}, u32[]{:S(2)}, u32[]{:S(2)}) collective-permute-start(bf16[128,4096]{1,0:T(8,128)(2,1)} %get-tuple-element.60), channel_id=1, source_target_pairs={{0,96},{32,0},{64,32},{96,64},{1,97},{33,1},{65,33},{97,65},{2,98}... | collective-permute-start | bytes 3145736 | tf_op jit(solution)/shard_map/ppermute | solution.py:28
  48.1 32.8 %all-to-all-start = ((bf16[32,8,4096]{2,1,0:T(8,128)(2,1)}), bf16[32,8,4096]{2,1,0:T(8,128)(2,1)S(1)}, u32[]{:S(2)}, u32[]{:S(2)}) async-start(bf16[32,8,4096]{2,1,0:T(8,128)(2,1)} %fusion.32), calls=%async_computation | async-start | bytes 4194304 | tf_op jit(solution)/shard_map/all_to_all | solution.py:63
  52.6 39.1 %collective-permute-start.1 = (bf16[128,4096]{1,0:T(8,128)(2,1)}, bf16[128,4096]{1,0:T(8,128)(2,1)}, u32[]{:S(2)}, u32[]{:S(2)}) collective-permute-start(bf16[128,4096]{1,0:T(8,128)(2,1)} %get-tuple-element.60), channel_id=1, source_target_pairs={{0,32},{32,64},{64,96},{96,0},{1,33},{33,65},{65,97},{97,1},{2,34}... | collective-permute-start | bytes 3145736 | tf_op jit(solution)/shard_map/ppermute | solution.py:28
  52.7 39.0 %collective-permute-start.2 = (bf16[128,4096]{1,0:T(8,128)(2,1)S(1)}, bf16[128,4096]{1,0:T(8,128)(2,1)}, u32[]{:S(2)}, u32[]{:S(2)}) collective-permute-start(bf16[128,4096]{1,0:T(8,128)(2,1)S(1)} %get-tuple-element.61), channel_id=1, source_target_pairs={{0,96},{32,0},{64,32},{96,64},{1,97},{33,1},{65,33},{97,65},{2,98}... | collective-permute-start | bytes 3145736 | tf_op jit(solution)/shard_map/ppermute | solution.py:28
  69.2 44.9 %collective-permute-start.4 = (bf16[128,4096]{1,0:T(8,128)(2,1)}, bf16[128,4096]{1,0:T(8,128)(2,1)}, u32[]{:S(2)}, u32[]{:S(2)}) collective-permute-start(bf16[128,4096]{1,0:T(8,128)(2,1)} %collective-permute-done), channel_id=1, source_target_pairs={{0,32},{32,64},{64,96},{96,0},{1,33},{33,65},{65,97},{97,1},{2,34}... | collective-permute-start | bytes 3145736 | tf_op jit(solution)/shard_map/ppermute | solution.py:28
  69.2 44.9 %collective-permute-start.5 = (bf16[128,4096]{1,0:T(8,128)(2,1)}, bf16[128,4096]{1,0:T(8,128)(2,1)}, u32[]{:S(2)}, u32[]{:S(2)}) collective-permute-start(bf16[128,4096]{1,0:T(8,128)(2,1)} %collective-permute-done.3), channel_id=1, source_target_pairs={{0,96},{32,0},{64,32},{96,64},{1,97},{33,1},{65,33},{97,65},{2,98}... | collective-permute-start | bytes 3145736 | tf_op jit(solution)/shard_map/ppermute | solution.py:28
  114.3 36.6 %collective-permute-start.8 = (bf16[128,4096]{1,0:T(8,128)(2,1)S(1)}, bf16[128,4096]{1,0:T(8,128)(2,1)S(1)}, u32[]{:S(2)}, u32[]{:S(2)}) collective-permute-start(bf16[128,4096]{1,0:T(8,128)(2,1)S(1)} %get-tuple-element.59), channel_id=1, source_target_pairs={{0,32},{32,64},{64,96},{96,0},{1,33},{33,65},{65,97},{97,1},{2,34}... | collective-permute-start | bytes 3145736 | tf_op jit(solution)/shard_map/ppermute | solution.py:28
  115.5 46.5 %collective-permute-start.10 = (bf16[128,4096]{1,0:T(8,128)(2,1)S(1)}, bf16[128,4096]{1,0:T(8,128)(2,1)S(1)}, u32[]{:S(2)}, u32[]{:S(2)}) collective-permute-start(bf16[128,4096]{1,0:T(8,128)(2,1)S(1)} %get-tuple-element.59), channel_id=1, source_target_pairs={{0,96},{32,0},{64,32},{96,64},{1,97},{33,1},{65,33},{97,65},{2,98}... | collective-permute-start | bytes 3145736 | tf_op jit(solution)/shard_map/ppermute | solution.py:28
  117.0 44.0 %collective-permute-start.11 = (bf16[128,4096]{1,0:T(8,128)(2,1)S(1)}, bf16[128,4096]{1,0:T(8,128)(2,1)S(1)}, u32[]{:S(2)}, u32[]{:S(2)}) collective-permute-start(bf16[128,4096]{1,0:T(8,128)(2,1)S(1)} %get-tuple-element.58), channel_id=1, source_target_pairs={{0,96},{32,0},{64,32},{96,64},{1,97},{33,1},{65,33},{97,65},{2,98}... | collective-permute-start | bytes 3145736 | tf_op jit(solution)/shard_map/ppermute | solution.py:28
  118.4 50.8 %collective-permute-start.9 = (bf16[128,4096]{1,0:T(8,128)(2,1)S(1)}, bf16[128,4096]{1,0:T(8,128)(2,1)S(1)}, u32[]{:S(2)}, u32[]{:S(2)}) collective-permute-start(bf16[128,4096]{1,0:T(8,128)(2,1)S(1)} %get-tuple-element.58), channel_id=1, source_target_pairs={{0,32},{32,64},{64,96},{96,0},{1,33},{33,65},{65,97},{97,1},{2,34}... | collective-permute-start | bytes 3145736 | tf_op jit(solution)/shard_map/ppermute | solution.py:28
  118.5 16.3 %slice-start = ((s8[9437184]{0:T(1024)(128)(4,1)}), s8[4194304]{0:T(1024)(128)(4,1)S(1)}, s32[]{:S(2)}) async-start(s8[9437184]{0:T(1024)(128)(4,1)} %bitcast.488), calls=%async_computation.4 | async-start | bytes 8388608
  118.5 16.3 %slice-start.1 = ((s8[9437184]{0:T(1024)(128)(4,1)}), s8[4194304]{0:T(1024)(128)(4,1)S(1)}, s32[]{:S(2)}) async-start(s8[9437184]{0:T(1024)(128)(4,1)} %bitcast.488), calls=%async_computation.5 | async-start | bytes 8388608
  126.6 8.2 %slice-start.2 = ((s8[9437184]{0:T(1024)(128)(4,1)}), s8[1048576]{0:T(1024)(128)(4,1)S(1)}, s32[]{:S(2)}) async-start(s8[9437184]{0:T(1024)(128)(4,1)} %bitcast.488), calls=%async_computation.6 | async-start | bytes 2097152
  126.6 56.9 %collective-permute-start.6 = (bf16[128,4096]{1,0:T(8,128)(2,1)S(1)}, bf16[128,4096]{1,0:T(8,128)(2,1)S(1)}, u32[]{:S(2)}, u32[]{:S(2)}) collective-permute-start(bf16[128,4096]{1,0:T(8,128)(2,1)S(1)} %convolution_convert_fusion.8), channel_id=1, source_target_pairs={{0,96},{32,0},{64,32},{96,64},{1,97},{33,1},{65,33},{97,65},{2,98}... | collective-permute-start | bytes 3145736 | tf_op jit(solution)/shard_map/ppermute | solution.py:28
  134.8 4.2 %copy-start.7 = (f32[2,128,384]{2,1,0:T(8,128)}, f32[2,128,384]{2,1,0:T(8,128)S(1)}, u32[]{:S(2)}) copy-start(f32[2,128,384]{2,1,0:T(8,128)S(1)} %fusion.96) | copy-start | bytes 1179652
  150.9 35.5 %collective-permute-start.7 = (bf16[128,4096]{1,0:T(8,128)(2,1)S(1)}, bf16[128,4096]{1,0:T(8,128)(2,1)S(1)}, u32[]{:S(2)}, u32[]{:S(2)}) collective-permute-start(bf16[128,4096]{1,0:T(8,128)(2,1)S(1)} %convolution_convert_fusion.7), channel_id=1, source_target_pairs={{0,32},{32,64},{64,96},{96,0},{1,33},{33,65},{65,97},{97,1},{2,34}... | collective-permute-start | bytes 3145736 | tf_op jit(solution)/shard_map/ppermute | solution.py:28
  161.0 45.4 %collective-permute-start.12 = (bf16[128,4096]{1,0:T(8,128)(2,1)S(1)}, bf16[128,4096]{1,0:T(8,128)(2,1)S(1)}, u32[]{:S(2)}, u32[]{:S(2)}) collective-permute-start(bf16[128,4096]{1,0:T(8,128)(2,1)S(1)} %collective-permute-done.8), channel_id=1, source_target_pairs={{0,32},{32,64},{64,96},{96,0},{1,33},{33,65},{65,97},{97,1},{2,34}... | collective-permute-start | bytes 3145736 | tf_op jit(solution)/shard_map/ppermute | solution.py:28
  162.0 44.5 %collective-permute-start.13 = (bf16[128,4096]{1,0:T(8,128)(2,1)S(1)}, bf16[128,4096]{1,0:T(8,128)(2,1)S(1)}, u32[]{:S(2)}, u32[]{:S(2)}) collective-permute-start(bf16[128,4096]{1,0:T(8,128)(2,1)S(1)} %collective-permute-done.11), channel_id=1, source_target_pairs={{0,96},{32,0},{64,32},{96,64},{1,97},{33,1},{65,33},{97,65},{2,98}... | collective-permute-start | bytes 3145736 | tf_op jit(solution)/shard_map/ppermute | solution.py:28
  164.9 1.6 copy-start.3
  169.2 60.7 %collective-permute-start.15 = (bf16[128,4096]{1,0:T(8,128)(2,1)S(1)}, bf16[128,4096]{1,0:T(8,128)(2,1)S(1)}, u32[]{:S(2)}, u32[]{:S(2)}) collective-permute-start(bf16[128,4096]{1,0:T(8,128)(2,1)S(1)} %convolution_convert_fusion.6), channel_id=1, source_target_pairs={{0,32},{32,64},{64,96},{96,0},{1,33},{33,65},{65,97},{97,1},{2,34}... | collective-permute-start | bytes 3145736 | tf_op jit(solution)/shard_map/ppermute | solution.py:28
  183.5 67.7 %collective-permute-start.16 = (bf16[128,4096]{1,0:T(8,128)(2,1)S(1)}, bf16[128,4096]{1,0:T(8,128)(2,1)S(1)}, u32[]{:S(2)}, u32[]{:S(2)}) collective-permute-start(bf16[128,4096]{1,0:T(8,128)(2,1)S(1)} %convolution_convert_fusion.5), channel_id=1, source_target_pairs={{0,96},{32,0},{64,32},{96,64},{1,97},{33,1},{65,33},{97,65},{2,98}... | collective-permute-start | bytes 3145736 | tf_op jit(solution)/shard_map/ppermute | solution.py:28
  214.4 36.6 %collective-permute-start.14 = (bf16[128,4096]{1,0:T(8,128)(2,1)S(1)}, bf16[128,4096]{1,0:T(8,128)(2,1)S(1)}, u32[]{:S(2)}, u32[]{:S(2)}) collective-permute-start(bf16[128,4096]{1,0:T(8,128)(2,1)S(1)} %add_convert_fusion.3), channel_id=1, source_target_pairs={{0,96},{32,0},{64,32},{96,64},{1,97},{33,1},{65,33},{97,65},{2,98}... | collective-permute-start | bytes 3145736 | tf_op jit(solution)/shard_map/ppermute | solution.py:28
  217.1 34.4 %collective-permute-start.17 = (bf16[128,4096]{1,0:T(8,128)(2,1)S(1)}, bf16[128,4096]{1,0:T(8,128)(2,1)S(1)}, u32[]{:S(2)}, u32[]{:S(2)}) collective-permute-start(bf16[128,4096]{1,0:T(8,128)(2,1)S(1)} %add_convert_fusion.2), channel_id=1, source_target_pairs={{0,32},{32,64},{64,96},{96,0},{1,33},{33,65},{65,97},{97,1},{2,34}... | collective-permute-start | bytes 3145736 | tf_op jit(solution)/shard_map/ppermute | solution.py:28
  222.4 2.0 copy-start.8
  254.4 22.8 %collective-permute-start.18 = (bf16[128,4096]{1,0:T(8,128)(2,1)S(1)}, bf16[128,4096]{1,0:T(8,128)(2,1)S(1)}, u32[]{:S(2)}, u32[]{:S(2)}) collective-permute-start(bf16[128,4096]{1,0:T(8,128)(2,1)S(1)} %fusion.46), channel_id=1, source_target_pairs={{0,96},{32,0},{64,32},{96,64},{1,97},{33,1},{65,33},{97,65},{2,98}... | collective-permute-start | bytes 3145736 | tf_op jit(solution)/shard_map/ppermute | solution.py:28
  257.1 24.0 %collective-permute-start.22 = (bf16[128,4096]{1,0:T(8,128)(2,1)S(1)}, bf16[128,4096]{1,0:T(8,128)(2,1)S(1)}, u32[]{:S(2)}, u32[]{:S(2)}) collective-permute-start(bf16[128,4096]{1,0:T(8,128)(2,1)S(1)} %fusion.49), channel_id=1, source_target_pairs={{0,32},{32,64},{64,96},{96,0},{1,33},{33,65},{65,97},{97,1},{2,34}... | collective-permute-start | bytes 3145736 | tf_op jit(solution)/shard_map/ppermute | solution.py:28
  257.1 45.8 %collective-permute-start.20 = (bf16[128,4096]{1,0:T(8,128)(2,1)}, bf16[128,4096]{1,0:T(8,128)(2,1)}, u32[]{:S(2)}, u32[]{:S(2)}) collective-permute-start(bf16[128,4096]{1,0:T(8,128)(2,1)} %fusion.40), channel_id=1, source_target_pairs={{0,32},{32,64},{64,96},{96,0},{1,33},{33,65},{65,97},{97,1},{2,34}... | collective-permute-start | bytes 3145736 | tf_op jit(solution)/shard_map/ppermute | solution.py:28
  277.5 25.4 %collective-permute-start.19 = (bf16[128,4096]{1,0:T(8,128)(2,1)S(1)}, bf16[128,4096]{1,0:T(8,128)(2,1)}, u32[]{:S(2)}, u32[]{:S(2)}) collective-permute-start(bf16[128,4096]{1,0:T(8,128)(2,1)S(1)} %add_convert_fusion.1), channel_id=1, source_target_pairs={{0,96},{32,0},{64,32},{96,64},{1,97},{33,1},{65,33},{97,65},{2,98}... | collective-permute-start | bytes 3145736 | tf_op jit(solution)/shard_map/ppermute | solution.py:28
  281.0 41.7 %collective-permute-start.21 = (bf16[128,4096]{1,0:T(8,128)(2,1)}, bf16[128,4096]{1,0:T(8,128)(2,1)}, u32[]{:S(2)}, u32[]{:S(2)}) collective-permute-start(bf16[128,4096]{1,0:T(8,128)(2,1)} %fusion.37), channel_id=1, source_target_pairs={{0,96},{32,0},{64,32},{96,64},{1,97},{33,1},{65,33},{97,65},{2,98}... | collective-permute-start | bytes 3145736 | tf_op jit(solution)/shard_map/ppermute | solution.py:28
  282.3 43.1 %collective-permute-start.23 = (bf16[128,4096]{1,0:T(8,128)(2,1)}, bf16[128,4096]{1,0:T(8,128)(2,1)}, u32[]{:S(2)}, u32[]{:S(2)}) collective-permute-start(bf16[128,4096]{1,0:T(8,128)(2,1)} %add_convert_fusion), channel_id=1, source_target_pairs={{0,32},{32,64},{64,96},{96,0},{1,33},{33,65},{65,97},{97,1},{2,34}... | collective-permute-start | bytes 3145736 | tf_op jit(solution)/shard_map/ppermute | solution.py:28
  284.0 45.1 %all-to-all-start.2 = ((bf16[32,8,4096]{2,1,0:T(8,128)(2,1)}), bf16[32,8,4096]{2,1,0:T(8,128)(2,1)S(1)}, u32[]{:S(2)}, u32[]{:S(2)}) async-start(bf16[32,8,4096]{2,1,0:T(8,128)(2,1)} %bitcast.490), calls=%async_computation.2 | async-start | bytes 4194304 | tf_op jit(solution)/shard_map/all_to_all | solution.py:74
  304.7 22.5 %copy-start.5 = (bf16[256,4096]{1,0:T(8,128)(2,1)S(1)}, bf16[256,4096]{1,0:T(8,128)(2,1)}, u32[]{:S(2)}) copy-start(bf16[256,4096]{1,0:T(8,128)(2,1)} %fusion.28) | copy-start | bytes 6291460
  329.1 36.4 %all-to-all-start.3 = ((bf16[32,8,4096]{2,1,0:T(8,128)(2,1)}), bf16[32,8,4096]{2,1,0:T(8,128)(2,1)}, u32[]{:S(2)}, u32[]{:S(2)}) async-start(bf16[32,8,4096]{2,1,0:T(8,128)(2,1)} %fusion.80), calls=%async_computation.3 | async-start | bytes 4194304 | tf_op jit(solution)/shard_map/all_to_all | solution.py:74
  337.0 31.5 %copy-start.1 = (bf16[128,4096]{1,0:T(8,128)(2,1)S(1)}, bf16[128,4096]{1,0:T(8,128)(2,1)}, u32[]{:S(2)}) copy-start(bf16[128,4096]{1,0:T(8,128)(2,1)} %param.5) | copy-start | bytes 3145732

commit v2 on v1

--- a/solution.py
+++ b/solution.py
@@ -114,9 +114,10 @@
     cold_grad_buf = spread(cold_layout, out_grad)
     cold_grad_arrived = arrive_rows(cold_grad_buf, experts, capacity, model_width)
     cold_grad_arrived, tok_blocks = lax.optimization_barrier((cold_grad_arrived, tok_blocks))
+    cot_blocks = group_rows(cold_grad_arrived)
+    tok_blocks, cot_blocks[1] = lax.optimization_barrier((tok_blocks, cot_blocks[1]))
     forward = [forward_rows(block, weights) for block in tok_blocks]
     fwd_parts = [f[2] for f in forward]
-    cot_blocks = group_rows(cold_grad_arrived)
     fwd_received = sum_start(fwd_parts)
     fwd_received, cot_blocks = lax.optimization_barrier((fwd_received, cot_blocks))
     fwd_total = sum_finish(fwd_parts, fwd_received)

time: 376 us -> 377 us (level)
  starting transfers between devices: 52.6 us -> 57.2 us
  matrix products: 65.8 us -> 61.7 us
  transfers between devices with their start and end apart: 27 -> 27, of which waited for: 14 -> 14; matrix products, arithmetic and copies ran while one was open for 18% -> 17% of each run, Pallas kernels for 0% -> 0%
where the time goes in v2:
time: 377 us; the launch traced here: 372 us
  waiting for transfers between devices  199 us (53%)
  matrix products  61.7 us (16%)
  starting transfers between devices  57.2 us (15%)
  blocking collectives  37.6 us (10%)
  other arithmetic  10.5 us (3%)
  local copies, waits for them, and re-layouts  3.89 us (1%)
    ppermute x24, waiting for transfers between devices, shifted(): lax.ppermute(values, 'dp', perm=[(i, (i + step) % n) for i in range(n)])  166 us
    all_to_all x1, blocking collectives, arrive_rows(): lax.all_to_all(cold_buf.reshape(experts, slot_count, model_width), 'exper...  37.6 us
    ppermute x24, starting transfers between devices, shifted(): lax.ppermute(values, 'dp', perm=[(i, (i + step) % n) for i in range(n)])  34.1 us
    dot_general x7, matrix products, forward_rows(): jnp.einsum('rd,kfd->krf', row_block, matrices[:2], preferred_element_type...  26.2 us
    all_to_all x2, waiting for transfers between devices, return_rows(): lax.all_to_all(summed, 'expert', split_axis=0, concat_axis=0, tiled=True)  24.8 us
    all_to_all x2, starting transfers between devices, return_rows(): lax.all_to_all(summed, 'expert', split_axis=0, concat_axis=0, tiled=True)  18.8 us
    dot_general x7, matrix products, backward_rows(): jnp.einsum('krf,kfd->rd', both_grads, matrices[:2], preferred_element_typ...  11.1 us
    all_to_all x1, waiting for transfers between devices, arrive_rows(): lax.all_to_all(cold_buf.reshape(experts, slot_count, model_width), 'exper...  8.51 us
  transfers between devices with their start and end apart: 27, of which 14 were waited for; matrix products, arithmetic and copies ran while one was open for 17% of the time, Pallas kernels for 0%

profile of v2, /device:TPU:1, one launch (start us, length us, event | category | flops | bytes accessed | tf_op | source)
XLA Modules:
  0.0 371.6 jit_solution(284412168220922847)
XLA Ops:
  1.7 0.9 fusion.235
  3.3 37.6 %all_to_all.20 = bf16[32,8,4096]{2,1,0:T(8,128)(2,1)S(1)} all-to-all(bf16[32,8,4096]{2,1,0:T(8,128)(2,1)S(1)} %fusion.33), channel_id=1, replica_groups=mesh['dp'=4,'expert'=32] {'expert'}, dimensions={0} | all-to-all | bytes 4194304 | tf_op jit(solution)/shard_map/all_to_all | solution.py:63
  40.8 1.4 copy-done.2
  42.2 1.5 slice_bitcast_fusion
  43.6 2.5 collective-permute-start.3
  46.1 2.1 fusion.32
  48.2 4.2 %all-to-all-start = ((bf16[32,8,4096]{2,1,0:T(8,128)(2,1)}), bf16[32,8,4096]{2,1,0:T(8,128)(2,1)S(1)}, u32[]{:S(2)}, u32[]{:S(2)}) async-start(bf16[32,8,4096]{2,1,0:T(8,128)(2,1)} %fusion.32), calls=%async_computation | async-start | bytes 4194304 | tf_op jit(solution)/shard_map/all_to_all | solution.py:63
  53.0 2.6 collective-permute-start.2
  55.6 13.3 %collective-permute-done.3 = bf16[128,4096]{1,0:T(8,128)(2,1)} collective-permute-done((bf16[128,4096]{1,0:T(8,128)(2,1)}, bf16[128,4096]{1,0:T(8,128)(2,1)}, u32[]{:S(2)}, u32[]{:S(2)}) %collective-permute-start.3) | collective-permute-done | bytes 1048608 | tf_op jit(solution)/shard_map/ppermute | solution.py:28
  68.8 3.4 collective-permute-start.5
  72.3 8.5 %all-to-all-done = bf16[32,8,4096]{2,1,0:T(8,128)(2,1)S(1)} async-done(((bf16[32,8,4096]{2,1,0:T(8,128)(2,1)}), bf16[32,8,4096]{2,1,0:T(8,128)(2,1)S(1)}, u32[]{:S(2)}, u32[]{:S(2)}) %all-to-all-start) | async-done | bytes 2097184 | tf_op jit(solution)/shard_map/all_to_all | solution.py:63
  80.8 13.6 %collective-permute-done.1 = bf16[128,4096]{1,0:T(8,128)(2,1)} collective-permute-done((bf16[128,4096]{1,0:T(8,128)(2,1)}, bf16[128,4096]{1,0:T(8,128)(2,1)}, u32[]{:S(2)}, u32[]{:S(2)}) %collective-permute-start.1) | collective-permute-done | bytes 1048608 | tf_op jit(solution)/shard_map/ppermute | solution.py:28
  94.4 19.4 %collective-permute-done.5 = bf16[128,4096]{1,0:T(8,128)(2,1)} collective-permute-done((bf16[128,4096]{1,0:T(8,128)(2,1)}, bf16[128,4096]{1,0:T(8,128)(2,1)}, u32[]{:S(2)}, u32[]{:S(2)}) %collective-permute-start.5) | collective-permute-done | bytes 1048608 | tf_op jit(solution)/shard_map/ppermute | solution.py:28
  113.8 3.1 collective-permute-done.4
  117.1 2.7 collective-permute-start.11
  119.8 2.9 collective-permute-start.10
  122.6 19.0 %collective-permute-done.6 = bf16[128,4096]{1,0:T(8,128)(2,1)S(1)} collective-permute-done((bf16[128,4096]{1,0:T(8,128)(2,1)S(1)}, bf16[128,4096]{1,0:T(8,128)(2,1)S(1)}, u32[]{:S(2)}, u32[]{:S(2)}) %collective-permute-start.6) | collective-permute-done | bytes 1048608 | tf_op jit(solution)/shard_map/ppermute | solution.py:28
  141.7 5.5 %fusion.93 = f32[2,128,384]{2,1,0:T(8,128)S(1)} fusion(bf16[128,4096]{1,0:T(8,128)(2,1)} %collective-permute-done.4, bf16[1,3,384,4096]{3,2,1,0:T(8,128)(2,1)} %param.9), kind=kOutput, calls=%fused_computation.95 | convolution fusion | flops 805306368 | bytes 7733248 | tf_op jit(solution)/shard_map/rd,kfd->krf/dot_general | solution.py:80
  147.2 5.4 %fusion.96 = f32[2,128,384]{2,1,0:T(8,128)S(1)} fusion(bf16[128,4096]{1,0:T(8,128)(2,1)} %collective-permute-done.5, bf16[1,3,384,4096]{3,2,1,0:T(8,128)(2,1)} %param.9), kind=kOutput, calls=%fused_computation.96 | convolution fusion | flops 805306368 | bytes 7733248 | tf_op jit(solution)/shard_map/rd,kfd->krf/dot_general | solution.py:80
  152.6 3.4 fusion.102
  156.1 3.4 fusion.105
  161.8 1.8 collective-permute-start.8
  164.4 3.5 fusion.90
  168.0 2.2 fusion.99
  170.3 2.7 collective-permute-start.13
  174.4 0.8 copy-done.3
  175.3 2.7 fusion.85
  178.0 30.1 %collective-permute-done.13 = bf16[128,4096]{1,0:T(8,128)(2,1)S(1)} collective-permute-done((bf16[128,4096]{1,0:T(8,128)(2,1)S(1)}, bf16[128,4096]{1,0:T(8,128)(2,1)S(1)}, u32[]{:S(2)}, u32[]{:S(2)}) %collective-permute-start.13) | collective-permute-done | bytes 1048608 | tf_op jit(solution)/shard_map/ppermute | solution.py:28
  208.1 3.4 collective-permute-start.16
  211.5 1.1 fusion.225
  212.6 1.1 fusion.224
  213.8 1.1 fusion.222
  214.9 1.1 fusion.221
  216.0 1.1 fusion.220
  217.1 1.1 fusion.223
  218.8 2.9 collective-permute-start.14
  221.7 1.3 fusion.202
  223.0 1.0 fusion.34
  224.0 1.0 fusion.43
  225.0 2.0 fusion.37
  227.0 2.0 fusion.40
  229.0 1.0 fusion.46
  230.0 3.2 fusion.28
  233.1 1.0 fusion.49
  234.2 17.4 %collective-permute-done.17 = bf16[128,4096]{1,0:T(8,128)(2,1)S(1)} collective-permute-done((bf16[128,4096]{1,0:T(8,128)(2,1)S(1)}, bf16[128,4096]{1,0:T(8,128)(2,1)S(1)}, u32[]{:S(2)}, u32[]{:S(2)}) %collective-permute-start.17) | collective-permute-done | bytes 1048608 | tf_op jit(solution)/shard_map/ppermute | solution.py:28
  251.9 2.1 collective-permute-done.14
  254.2 2.7 maximum_add_fusion
  256.9 3.4 collective-permute-start.18
  260.4 19.1 %collective-permute-done.18 = bf16[128,4096]{1,0:T(8,128)(2,1)S(1)} collective-permute-done((bf16[128,4096]{1,0:T(8,128)(2,1)S(1)}, bf16[128,4096]{1,0:T(8,128)(2,1)S(1)}, u32[]{:S(2)}, u32[]{:S(2)}) %collective-permute-start.18) | collective-permute-done | bytes 1048608 | tf_op jit(solution)/shard_map/ppermute | solution.py:28
  279.4 1.2 add_convert_fusion.1
  280.6 3.4 collective-permute-start.19
  284.1 1.2 add_convert_fusion
  285.3 1.6 collective-permute-start.23
  286.9 9.8 %all-to-all-start.2 = ((bf16[32,8,4096]{2,1,0:T(8,128)(2,1)}), bf16[32,8,4096]{2,1,0:T(8,128)(2,1)S(1)}, u32[]{:S(2)}, u32[]{:S(2)}) async-start(bf16[32,8,4096]{2,1,0:T(8,128)(2,1)} %bitcast.490), calls=%async_computation.2 | async-start | bytes 4194304 | tf_op jit(solution)/shard_map/all_to_all | solution.py:74
  296.7 8.4 %collective-permute-done.20 = bf16[128,4096]{1,0:T(8,128)(2,1)} collective-permute-done((bf16[128,4096]{1,0:T(8,128)(2,1)}, bf16[128,4096]{1,0:T(8,128)(2,1)}, u32[]{:S(2)}, u32[]{:S(2)}) %collective-permute-start.20) | collective-permute-done | bytes 1048608 | tf_op jit(solution)/shard_map/ppermute | solution.py:28
  305.1 1.8 convert_add_fusion.1
  306.9 18.0 %collective-permute-done.21 = bf16[128,4096]{1,0:T(8,128)(2,1)} collective-permute-done((bf16[128,4096]{1,0:T(8,128)(2,1)}, bf16[128,4096]{1,0:T(8,128)(2,1)}, u32[]{:S(2)}, u32[]{:S(2)}) %collective-permute-start.21) | collective-permute-done | bytes 1048608 | tf_op jit(solution)/shard_map/ppermute | solution.py:28
  325.0 2.5 collective-permute-done.23
  327.5 1.5 convert_add_fusion
  329.0 1.9 fusion.80
  330.9 9.1 %all-to-all-start.3 = ((bf16[32,8,4096]{2,1,0:T(8,128)(2,1)}), bf16[32,8,4096]{2,1,0:T(8,128)(2,1)}, u32[]{:S(2)}, u32[]{:S(2)}) async-start(bf16[32,8,4096]{2,1,0:T(8,128)(2,1)} %fusion.80), calls=%async_computation.3 | async-start | bytes 4194304 | tf_op jit(solution)/shard_map/all_to_all | solution.py:74
  339.9 3.5 fusion.79
  343.5 24.8 %all-to-all-done.3 = bf16[32,8,4096]{2,1,0:T(8,128)(2,1)} async-done(((bf16[32,8,4096]{2,1,0:T(8,128)(2,1)}), bf16[32,8,4096]{2,1,0:T(8,128)(2,1)}, u32[]{:S(2)}, u32[]{:S(2)}) %all-to-all-start.3) | async-done | bytes 2097184 | tf_op jit(solution)/shard_map/all_to_all | solution.py:74
  368.3 3.1 convolution_convert_fusion.3
  (70 shorter events, 8.2 us)
Async XLA Ops:
  0.6 1.9 copy-start
  40.8 1.4 copy-start.2
  42.2 3.9 %copy-start.4 = (bf16[128,4096]{1,0:T(8,128)(2,1)S(1)}, bf16[128,4096]{1,0:T(8,128)(2,1)}, u32[]{:S(2)}) copy-start(bf16[128,4096]{1,0:T(8,128)(2,1)} %param.6) | copy-start | bytes 3145732
  42.2 3.9 %copy-start.6 = (f32[128]{0:T(128)S(1)}, f32[128]{0:T(128)}, u32[]{:S(2)}) copy-start(f32[128]{0:T(128)} %param.8) | copy-start | bytes 1540
  43.6 25.2 %collective-permute-start.3 = (bf16[128,4096]{1,0:T(8,128)(2,1)}, bf16[128,4096]{1,0:T(8,128)(2,1)}, u32[]{:S(2)}, u32[]{:S(2)}) collective-permute-start(bf16[128,4096]{1,0:T(8,128)(2,1)} %get-tuple-element.76), channel_id=1, source_target_pairs={{0,96},{32,0},{64,32},{96,64},{1,97},{33,1},{65,33},{97,65},{2,98}... | collective-permute-start | bytes 3145736 | tf_op jit(solution)/shard_map/ppermute | solution.py:28
  46.1 26.1 %collective-permute-start = (bf16[128,4096]{1,0:T(8,128)(2,1)}, bf16[128,4096]{1,0:T(8,128)(2,1)}, u32[]{:S(2)}, u32[]{:S(2)}) collective-permute-start(bf16[128,4096]{1,0:T(8,128)(2,1)} %get-tuple-element.77), channel_id=1, source_target_pairs={{0,32},{32,64},{64,96},{96,0},{1,33},{33,65},{65,97},{97,1},{2,34}... | collective-permute-start | bytes 3145736 | tf_op jit(solution)/shard_map/ppermute | solution.py:28
  48.2 32.5 %all-to-all-start = ((bf16[32,8,4096]{2,1,0:T(8,128)(2,1)}), bf16[32,8,4096]{2,1,0:T(8,128)(2,1)S(1)}, u32[]{:S(2)}, u32[]{:S(2)}) async-start(bf16[32,8,4096]{2,1,0:T(8,128)(2,1)} %fusion.32), calls=%async_computation | async-start | bytes 4194304 | tf_op jit(solution)/shard_map/all_to_all | solution.py:63
  52.5 41.9 %collective-permute-start.1 = (bf16[128,4096]{1,0:T(8,128)(2,1)}, bf16[128,4096]{1,0:T(8,128)(2,1)}, u32[]{:S(2)}, u32[]{:S(2)}) collective-permute-start(bf16[128,4096]{1,0:T(8,128)(2,1)} %get-tuple-element.76), channel_id=1, source_target_pairs={{0,32},{32,64},{64,96},{96,0},{1,33},{33,65},{65,97},{97,1},{2,34}... | collective-permute-start | bytes 3145736 | tf_op jit(solution)/shard_map/ppermute | solution.py:28
  53.0 41.4 %collective-permute-start.2 = (bf16[128,4096]{1,0:T(8,128)(2,1)}, bf16[128,4096]{1,0:T(8,128)(2,1)S(1)}, u32[]{:S(2)}, u32[]{:S(2)}) collective-permute-start(bf16[128,4096]{1,0:T(8,128)(2,1)} %get-tuple-element.77), channel_id=1, source_target_pairs={{0,96},{32,0},{64,32},{96,64},{1,97},{33,1},{65,33},{97,65},{2,98}... | collective-permute-start | bytes 3145736 | tf_op jit(solution)/shard_map/ppermute | solution.py:28
  68.8 44.9 %collective-permute-start.5 = (bf16[128,4096]{1,0:T(8,128)(2,1)}, bf16[128,4096]{1,0:T(8,128)(2,1)}, u32[]{:S(2)}, u32[]{:S(2)}) collective-permute-start(bf16[128,4096]{1,0:T(8,128)(2,1)} %collective-permute-done.3), channel_id=1, source_target_pairs={{0,96},{32,0},{64,32},{96,64},{1,97},{33,1},{65,33},{97,65},{2,98}... | collective-permute-start | bytes 3145736 | tf_op jit(solution)/shard_map/ppermute | solution.py:28
  72.2 44.6 %collective-permute-start.4 = (bf16[128,4096]{1,0:T(8,128)(2,1)}, bf16[128,4096]{1,0:T(8,128)(2,1)}, u32[]{:S(2)}, u32[]{:S(2)}) collective-permute-start(bf16[128,4096]{1,0:T(8,128)(2,1)} %collective-permute-done), channel_id=1, source_target_pairs={{0,32},{32,64},{64,96},{96,0},{1,33},{33,65},{65,97},{97,1},{2,34}... | collective-permute-start | bytes 3145736 | tf_op jit(solution)/shard_map/ppermute | solution.py:28
  94.4 52.8 %copy-start.7 = (bf16[128,4096]{1,0:T(8,128)(2,1)}, bf16[128,4096]{1,0:T(8,128)(2,1)S(1)}, u32[]{:S(2)}) copy-start(bf16[128,4096]{1,0:T(8,128)(2,1)S(1)} %collective-permute-done.2) | copy-start | bytes 3145732
  117.0 24.7 %collective-permute-start.6 = (bf16[128,4096]{1,0:T(8,128)(2,1)S(1)}, bf16[128,4096]{1,0:T(8,128)(2,1)S(1)}, u32[]{:S(2)}, u32[]{:S(2)}) collective-permute-start(bf16[128,4096]{1,0:T(8,128)(2,1)S(1)} %get-tuple-element.75), channel_id=1, source_target_pairs={{0,32},{32,64},{64,96},{96,0},{1,33},{33,65},{65,97},{97,1},{2,34}... | collective-permute-start | bytes 3145736 | tf_op jit(solution)/shard_map/ppermute | solution.py:28
  117.1 53.1 %collective-permute-start.11 = (bf16[128,4096]{1,0:T(8,128)(2,1)S(1)}, bf16[128,4096]{1,0:T(8,128)(2,1)S(1)}, u32[]{:S(2)}, u32[]{:S(2)}) collective-permute-start(bf16[128,4096]{1,0:T(8,128)(2,1)S(1)} %get-tuple-element.74), channel_id=1, source_target_pairs={{0,96},{32,0},{64,32},{96,64},{1,97},{33,1},{65,33},{97,65},{2,98}... | collective-permute-start | bytes 3145736 | tf_op jit(solution)/shard_map/ppermute | solution.py:28
  119.8 50.5 %collective-permute-start.9 = (bf16[128,4096]{1,0:T(8,128)(2,1)S(1)}, bf16[128,4096]{1,0:T(8,128)(2,1)S(1)}, u32[]{:S(2)}, u32[]{:S(2)}) collective-permute-start(bf16[128,4096]{1,0:T(8,128)(2,1)S(1)} %get-tuple-element.74), channel_id=1, source_target_pairs={{0,32},{32,64},{64,96},{96,0},{1,33},{33,65},{65,97},{97,1},{2,34}... | collective-permute-start | bytes 3145736 | tf_op jit(solution)/shard_map/ppermute | solution.py:28
  119.8 58.2 %collective-permute-start.10 = (bf16[128,4096]{1,0:T(8,128)(2,1)S(1)}, bf16[128,4096]{1,0:T(8,128)(2,1)S(1)}, u32[]{:S(2)}, u32[]{:S(2)}) collective-permute-start(bf16[128,4096]{1,0:T(8,128)(2,1)S(1)} %get-tuple-element.75), channel_id=1, source_target_pairs={{0,96},{32,0},{64,32},{96,64},{1,97},{33,1},{65,33},{97,65},{2,98}... | collective-permute-start | bytes 3145736 | tf_op jit(solution)/shard_map/ppermute | solution.py:28
  141.7 10.9 %slice-start = ((s8[9437184]{0:T(1024)(128)(4,1)}), s8[4194304]{0:T(1024)(128)(4,1)S(1)}, s32[]{:S(2)}) async-start(s8[9437184]{0:T(1024)(128)(4,1)} %bitcast.488), calls=%async_computation.4 | async-start | bytes 8388608
  141.7 10.9 %slice-start.1 = ((s8[9437184]{0:T(1024)(128)(4,1)}), s8[4194304]{0:T(1024)(128)(4,1)S(1)}, s32[]{:S(2)}) async-start(s8[9437184]{0:T(1024)(128)(4,1)} %bitcast.488), calls=%async_computation.5 | async-start | bytes 8388608
  147.2 5.4 %slice-start.2 = ((s8[9437184]{0:T(1024)(128)(4,1)}), s8[1048576]{0:T(1024)(128)(4,1)S(1)}, s32[]{:S(2)}) async-start(s8[9437184]{0:T(1024)(128)(4,1)} %bitcast.488), calls=%async_computation.6 | async-start | bytes 2097152
  161.7 49.8 %collective-permute-start.7 = (bf16[128,4096]{1,0:T(8,128)(2,1)S(1)}, bf16[128,4096]{1,0:T(8,128)(2,1)S(1)}, u32[]{:S(2)}, u32[]{:S(2)}) collective-permute-start(bf16[128,4096]{1,0:T(8,128)(2,1)S(1)} %convolution_convert_fusion.8), channel_id=1, source_target_pairs={{0,96},{32,0},{64,32},{96,64},{1,97},{33,1},{65,33},{97,65},{2,98}... | collective-permute-start | bytes 3145736 | tf_op jit(solution)/shard_map/ppermute | solution.py:28
  161.8 49.7 %collective-permute-start.8 = (bf16[128,4096]{1,0:T(8,128)(2,1)S(1)}, bf16[128,4096]{1,0:T(8,128)(2,1)S(1)}, u32[]{:S(2)}, u32[]{:S(2)}) collective-permute-start(bf16[128,4096]{1,0:T(8,128)(2,1)S(1)} %convolution_convert_fusion.7), channel_id=1, source_target_pairs={{0,32},{32,64},{64,96},{96,0},{1,33},{33,65},{65,97},{97,1},{2,34}... | collective-permute-start | bytes 3145736 | tf_op jit(solution)/shard_map/ppermute | solution.py:28
  164.4 3.6 copy-start.8
  170.2 2.8 copy-start.9
  170.2 41.3 %collective-permute-start.12 = (bf16[128,4096]{1,0:T(8,128)(2,1)S(1)}, bf16[128,4096]{1,0:T(8,128)(2,1)S(1)}, u32[]{:S(2)}, u32[]{:S(2)}) collective-permute-start(bf16[128,4096]{1,0:T(8,128)(2,1)S(1)} %collective-permute-done.6), channel_id=1, source_target_pairs={{0,32},{32,64},{64,96},{96,0},{1,33},{33,65},{65,97},{97,1},{2,34}... | collective-permute-start | bytes 3145736 | tf_op jit(solution)/shard_map/ppermute | solution.py:28
  170.3 37.8 %collective-permute-start.13 = (bf16[128,4096]{1,0:T(8,128)(2,1)S(1)}, bf16[128,4096]{1,0:T(8,128)(2,1)S(1)}, u32[]{:S(2)}, u32[]{:S(2)}) collective-permute-start(bf16[128,4096]{1,0:T(8,128)(2,1)S(1)} %collective-permute-done.11), channel_id=1, source_target_pairs={{0,96},{32,0},{64,32},{96,64},{1,97},{33,1},{65,33},{97,65},{2,98}... | collective-permute-start | bytes 3145736 | tf_op jit(solution)/shard_map/ppermute | solution.py:28
  173.7 1.6 copy-start.3
  178.0 73.8 %collective-permute-start.15 = (bf16[128,4096]{1,0:T(8,128)(2,1)S(1)}, bf16[128,4096]{1,0:T(8,128)(2,1)S(1)}, u32[]{:S(2)}, u32[]{:S(2)}) collective-permute-start(bf16[128,4096]{1,0:T(8,128)(2,1)S(1)} %convolution_convert_fusion.6), channel_id=1, source_target_pairs={{0,32},{32,64},{64,96},{96,0},{1,33},{33,65},{65,97},{97,1},{2,34}... | collective-permute-start | bytes 3145736 | tf_op jit(solution)/shard_map/ppermute | solution.py:28
  208.1 26.1 %collective-permute-start.16 = (bf16[128,4096]{1,0:T(8,128)(2,1)S(1)}, bf16[128,4096]{1,0:T(8,128)(2,1)S(1)}, u32[]{:S(2)}, u32[]{:S(2)}) collective-permute-start(bf16[128,4096]{1,0:T(8,128)(2,1)S(1)} %convolution_convert_fusion.5), channel_id=1, source_target_pairs={{0,96},{32,0},{64,32},{96,64},{1,97},{33,1},{65,33},{97,65},{2,98}... | collective-permute-start | bytes 3145736 | tf_op jit(solution)/shard_map/ppermute | solution.py:28
  212.6 1.1 copy-start.10
  218.4 3.3 copy-start.11
  218.4 33.2 %collective-permute-start.17 = (bf16[128,4096]{1,0:T(8,128)(2,1)S(1)}, bf16[128,4096]{1,0:T(8,128)(2,1)S(1)}, u32[]{:S(2)}, u32[]{:S(2)}) collective-permute-start(bf16[128,4096]{1,0:T(8,128)(2,1)S(1)} %add_convert_fusion.2), channel_id=1, source_target_pairs={{0,32},{32,64},{64,96},{96,0},{1,33},{33,65},{65,97},{97,1},{2,34}... | collective-permute-start | bytes 3145736 | tf_op jit(solution)/shard_map/ppermute | solution.py:28
  218.8 35.2 %collective-permute-start.14 = (bf16[128,4096]{1,0:T(8,128)(2,1)S(1)}, bf16[128,4096]{1,0:T(8,128)(2,1)S(1)}, u32[]{:S(2)}, u32[]{:S(2)}) collective-permute-start(bf16[128,4096]{1,0:T(8,128)(2,1)S(1)} %add_convert_fusion.3), channel_id=1, source_target_pairs={{0,96},{32,0},{64,32},{96,64},{1,97},{33,1},{65,33},{97,65},{2,98}... | collective-permute-start | bytes 3145736 | tf_op jit(solution)/shard_map/ppermute | solution.py:28
  256.9 22.5 %collective-permute-start.18 = (bf16[128,4096]{1,0:T(8,128)(2,1)S(1)}, bf16[128,4096]{1,0:T(8,128)(2,1)S(1)}, u32[]{:S(2)}, u32[]{:S(2)}) collective-permute-start(bf16[128,4096]{1,0:T(8,128)(2,1)S(1)} %fusion.46), channel_id=1, source_target_pairs={{0,96},{32,0},{64,32},{96,64},{1,97},{33,1},{65,33},{97,65},{2,98}... | collective-permute-start | bytes 3145736 | tf_op jit(solution)/shard_map/ppermute | solution.py:28
  260.3 23.7 %collective-permute-start.22 = (bf16[128,4096]{1,0:T(8,128)(2,1)S(1)}, bf16[128,4096]{1,0:T(8,128)(2,1)S(1)}, u32[]{:S(2)}, u32[]{:S(2)}) collective-permute-start(bf16[128,4096]{1,0:T(8,128)(2,1)S(1)} %fusion.49), channel_id=1, source_target_pairs={{0,32},{32,64},{64,96},{96,0},{1,33},{33,65},{65,97},{97,1},{2,34}... | collective-permute-start | bytes 3145736 | tf_op jit(solution)/shard_map/ppermute | solution.py:28
  260.4 44.8 %collective-permute-start.20 = (bf16[128,4096]{1,0:T(8,128)(2,1)}, bf16[128,4096]{1,0:T(8,128)(2,1)}, u32[]{:S(2)}, u32[]{:S(2)}) collective-permute-start(bf16[128,4096]{1,0:T(8,128)(2,1)} %fusion.40), channel_id=1, source_target_pairs={{0,32},{32,64},{64,96},{96,0},{1,33},{33,65},{65,97},{97,1},{2,34}... | collective-permute-start | bytes 3145736 | tf_op jit(solution)/shard_map/ppermute | solution.py:28
  280.6 24.5 %collective-permute-start.19 = (bf16[128,4096]{1,0:T(8,128)(2,1)}, bf16[128,4096]{1,0:T(8,128)(2,1)}, u32[]{:S(2)}, u32[]{:S(2)}) collective-permute-start(bf16[128,4096]{1,0:T(8,128)(2,1)} %add_convert_fusion.1), channel_id=1, source_target_pairs={{0,96},{32,0},{64,32},{96,64},{1,97},{33,1},{65,33},{97,65},{2,98}... | collective-permute-start | bytes 3145736 | tf_op jit(solution)/shard_map/ppermute | solution.py:28
  284.1 40.9 %collective-permute-start.21 = (bf16[128,4096]{1,0:T(8,128)(2,1)}, bf16[128,4096]{1,0:T(8,128)(2,1)}, u32[]{:S(2)}, u32[]{:S(2)}) collective-permute-start(bf16[128,4096]{1,0:T(8,128)(2,1)} %fusion.37), channel_id=1, source_target_pairs={{0,96},{32,0},{64,32},{96,64},{1,97},{33,1},{65,33},{97,65},{2,98}... | collective-permute-start | bytes 3145736 | tf_op jit(solution)/shard_map/ppermute | solution.py:28
  285.3 42.2 %collective-permute-start.23 = (bf16[128,4096]{1,0:T(8,128)(2,1)}, bf16[128,4096]{1,0:T(8,128)(2,1)S(1)}, u32[]{:S(2)}, u32[]{:S(2)}) collective-permute-start(bf16[128,4096]{1,0:T(8,128)(2,1)} %add_convert_fusion), channel_id=1, source_target_pairs={{0,32},{32,64},{64,96},{96,0},{1,33},{33,65},{65,97},{97,1},{2,34}... | collective-permute-start | bytes 3145736 | tf_op jit(solution)/shard_map/ppermute | solution.py:28
  286.9 43.9 %all-to-all-start.2 = ((bf16[32,8,4096]{2,1,0:T(8,128)(2,1)}), bf16[32,8,4096]{2,1,0:T(8,128)(2,1)S(1)}, u32[]{:S(2)}, u32[]{:S(2)}) async-start(bf16[32,8,4096]{2,1,0:T(8,128)(2,1)} %bitcast.490), calls=%async_computation.2 | async-start | bytes 4194304 | tf_op jit(solution)/shard_map/all_to_all | solution.py:74
  306.9 22.0 %copy-start.5 = (bf16[256,4096]{1,0:T(8,128)(2,1)S(1)}, bf16[256,4096]{1,0:T(8,128)(2,1)}, u32[]{:S(2)}) copy-start(bf16[256,4096]{1,0:T(8,128)(2,1)} %fusion.28) | copy-start | bytes 6291460
  330.9 37.4 %all-to-all-start.3 = ((bf16[32,8,4096]{2,1,0:T(8,128)(2,1)}), bf16[32,8,4096]{2,1,0:T(8,128)(2,1)}, u32[]{:S(2)}, u32[]{:S(2)}) async-start(bf16[32,8,4096]{2,1,0:T(8,128)(2,1)} %fusion.80), calls=%async_computation.3 | async-start | bytes 4194304 | tf_op jit(solution)/shard_map/all_to_all | solution.py:74
  339.9 31.4 %copy-start.1 = (bf16[128,4096]{1,0:T(8,128)(2,1)S(1)}, bf16[128,4096]{1,0:T(8,128)(2,1)}, u32[]{:S(2)}) copy-start(bf16[128,4096]{1,0:T(8,128)(2,1)} %param.5) | copy-start | bytes 3145732

commit v3 on v1

--- a/solution.py
+++ b/solution.py
@@ -98,6 +98,16 @@
     return jnp.einsum("krf,kfd->rd", both_grads, matrices[:2], preferred_element_type=jnp.float32)
 
 
+def joined(blocks):
+    return [blocks[0], jnp.concatenate(blocks[1:], 0)]
+
+
+def halves(parts):
+    rest = parts[1]
+    size = rest.shape[0] // 6
+    return [parts[0]] + [rest[k * size:(k + 1) * size] for k in range(6)]
+
+
 def shards(tokens, cotangent, routes, combine, expert_weights):
     weights = expert_weights[0]
     tok_dev = tokens.shape[0]
@@ -114,15 +124,15 @@
     cold_grad_buf = spread(cold_layout, out_grad)
     cold_grad_arrived = arrive_rows(cold_grad_buf, experts, capacity, model_width)
     cold_grad_arrived, tok_blocks = lax.optimization_barrier((cold_grad_arrived, tok_blocks))
-    forward = [forward_rows(block, weights) for block in tok_blocks]
-    fwd_parts = [f[2] for f in forward]
+    forward = [forward_rows(block, weights) for block in joined(tok_blocks)]
+    fwd_parts = halves([f[2] for f in forward])
     cot_blocks = group_rows(cold_grad_arrived)
     fwd_received = sum_start(fwd_parts)
     fwd_received, cot_blocks = lax.optimization_barrier((fwd_received, cot_blocks))
     fwd_total = sum_finish(fwd_parts, fwd_received)
-    grad_parts = [
-        backward_rows(block, f[0], f[1], weights) for block, f in zip(cot_blocks, forward)
-    ]
+    grad_parts = halves(
+        [backward_rows(block, f[0], f[1], weights) for block, f in zip(joined(cot_blocks), forward)]
+    )
     fwd_total, grad_parts = lax.optimization_barrier((fwd_total, grad_parts))
     cold_out = return_rows(fwd_total, experts, capacity, model_width)
     expert_out = collect(cold_layout, cold_out)

time: 376 us -> 395 us (1.051); the launches traced: 369 us -> 394 us
  waiting for transfers between devices: 198 us -> 225 us
  matrix products: 65.8 us -> 56 us
  local copies, waits for them, and re-layouts: 3.5 us -> 12.5 us
    ppermute x24, waiting for transfers between devices: 164 us -> 192 us  [shifted(): lax.ppermute(values, 'dp', perm=[(i, (i + step) % n) for i in range(n)])]
    dot_general x7 -> x2, matrix products: 27.3 us -> 13.4 us  [forward_rows(): jnp.einsum('rd,kfd->krf', row_block, matrices[:2], preferred_element_type...]
    unnamed x24, local copies, waits for them, and re-layouts: 2.26 us -> 7.02 us
    dot_general x7 -> x2, matrix products: 11.2 us -> 14.1 us  [backward_rows(): jnp.einsum('krf,kfd->rd', both_grads, matrices[:2], preferred_element_typ...]
    dot_general x7 -> x2, matrix products: 9.01 us -> 10.2 us  [forward_rows(): jnp.dot(hidden, matrices[2], preferred_element_type=jnp.float32)]
    dot_general x7 -> x2, matrix products: 8.91 us -> 8.85 us  [backward_rows(): lax.dot_general(row_block, matrices[2], (((1,), (1,)), ((), ())), preferr...]
  transfers between devices with their start and end apart: 27 -> 27, of which waited for: 14 -> 14; matrix products, arithmetic and copies ran while one was open for 18% -> 11% of each run, Pallas kernels for 0% -> 0%
where the time goes in v3:
time: 395 us; the launch traced here: 394 us
  waiting for transfers between devices  225 us (57%)
  matrix products  56 us (14%)
  starting transfers between devices  50.8 us (13%)
  blocking collectives  37.6 us (10%)
  local copies, waits for them, and re-layouts  12.5 us (3%)
  other arithmetic  10.9 us (3%)
    ppermute x24, waiting for transfers between devices, shifted(): lax.ppermute(values, 'dp', perm=[(i, (i + step) % n) for i in range(n)])  192 us
    all_to_all x1, blocking collectives, arrive_rows(): lax.all_to_all(cold_buf.reshape(experts, slot_count, model_width), 'exper...  37.6 us
    ppermute x24, starting transfers between devices, shifted(): lax.ppermute(values, 'dp', perm=[(i, (i + step) % n) for i in range(n)])  27.9 us
    all_to_all x2, waiting for transfers between devices, return_rows(): lax.all_to_all(summed, 'expert', split_axis=0, concat_axis=0, tiled=True)  24.8 us
    all_to_all x2, starting transfers between devices, return_rows(): lax.all_to_all(summed, 'expert', split_axis=0, concat_axis=0, tiled=True)  18.4 us
    dot_general x2, matrix products, backward_rows(): jnp.einsum('krf,kfd->rd', both_grads, matrices[:2], preferred_element_typ...  14.1 us
    dot_general x2, matrix products, forward_rows(): jnp.einsum('rd,kfd->krf', row_block, matrices[:2], preferred_element_type...  13.4 us
    dot_general x2, matrix products, forward_rows(): jnp.dot(hidden, matrices[2], preferred_element_type=jnp.float32)  10.2 us
  transfers between devices with their start and end apart: 27, of which 14 were waited for; matrix products, arithmetic and copies ran while one was open for 11% of the time, Pallas kernels for 0%

profile of v3, /device:TPU:1, one launch (start us, length us, event | category | flops | bytes accessed | tf_op | source)
XLA Modules:
  0.0 394.3 jit_solution(7141229280329889380)
XLA Ops:
  0.6 0.8 fusion.89
  1.5 0.2 reduce_window_sum.11
  1.7 0.9 fusion.94
  2.6 0.7 fusion.13
  3.3 37.6 %all_to_all.20 = bf16[32,8,4096]{2,1,0:T(8,128)(2,1)S(1)} all-to-all(bf16[32,8,4096]{2,1,0:T(8,128)(2,1)S(1)} %fusion.13), channel_id=1, replica_groups=mesh['dp'=4,'expert'=32] {'expert'}, dimensions={0} | all-to-all | bytes 4194304 | tf_op jit(solution)/shard_map/all_to_all | solution.py:63
  40.8 1.3 copy-done.2
  42.2 1.5 slice_bitcast_fusion
  43.6 1.2 collective-permute-start
  44.8 1.5 collective-permute-start.3
  46.3 2.1 fusion.12
  48.4 4.5 %all-to-all-start = ((bf16[32,8,4096]{2,1,0:T(8,128)(2,1)}), bf16[32,8,4096]{2,1,0:T(8,128)(2,1)S(1)}, u32[]{:S(2)}, u32[]{:S(2)}) async-start(bf16[32,8,4096]{2,1,0:T(8,128)(2,1)} %fusion.12), calls=%async_computation | async-start | bytes 4194304 | tf_op jit(solution)/shard_map/all_to_all | solution.py:63
  53.0 2.7 collective-permute-start.2
  55.7 14.1 %collective-permute-done = bf16[128,4096]{1,0:T(8,128)(2,1)} collective-permute-done((bf16[128,4096]{1,0:T(8,128)(2,1)}, bf16[128,4096]{1,0:T(8,128)(2,1)}, u32[]{:S(2)}, u32[]{:S(2)}) %collective-permute-start) | collective-permute-done | bytes 1048608 | tf_op jit(solution)/shard_map/ppermute | solution.py:28
  69.8 2.7 collective-permute-start.5
  72.4 8.8 %all-to-all-done = bf16[32,8,4096]{2,1,0:T(8,128)(2,1)S(1)} async-done(((bf16[32,8,4096]{2,1,0:T(8,128)(2,1)}), bf16[32,8,4096]{2,1,0:T(8,128)(2,1)S(1)}, u32[]{:S(2)}, u32[]{:S(2)}) %all-to-all-start) | async-done | bytes 2097184 | tf_op jit(solution)/shard_map/all_to_all | solution.py:63
  81.2 10.9 %collective-permute-done.1 = bf16[128,4096]{1,0:T(8,128)(2,1)S(1)} collective-permute-done((bf16[128,4096]{1,0:T(8,128)(2,1)}, bf16[128,4096]{1,0:T(8,128)(2,1)S(1)}, u32[]{:S(2)}, u32[]{:S(2)}) %collective-permute-start.1) | collective-permute-done | bytes 1048608 | tf_op jit(solution)/shard_map/ppermute | solution.py:28
  92.1 22.6 %collective-permute-done.4 = bf16[128,4096]{1,0:T(8,128)(2,1)} collective-permute-done((bf16[128,4096]{1,0:T(8,128)(2,1)}, bf16[128,4096]{1,0:T(8,128)(2,1)}, u32[]{:S(2)}, u32[]{:S(2)}) %collective-permute-start.4) | collective-permute-done | bytes 1048608 | tf_op jit(solution)/shard_map/ppermute | solution.py:28
  114.7 1.3 constant_dynamic-update-slice_fusion.5
  116.1 1.3 constant_dynamic-update-slice_fusion.3
  117.4 1.3 constant_dynamic-update-slice_fusion.2
  118.7 1.3 constant_dynamic-update-slice_fusion.1
  120.0 1.3 constant_dynamic-update-slice_fusion
  121.3 8.8 %fusion.38 = f32[2,768,384]{2,1,0:T(8,128)S(1)} fusion(bf16[1,3,384,4096]{3,2,1,0:T(8,128)(2,1)} %param.9, bf16[768,4096]{1,0:T(8,128)(2,1)S(1)} %constant_dynamic-update-slice_fusion), kind=kOutput, calls=%fused_computation.54 | convolution fusion | flops 4831838208 | bytes 14942208 | tf_op jit(solution)/shard_map/rd,kfd->krf/dot_general | solution.py:80
  130.1 5.6 %convolution_convert_fusion = bf16[768,4096]{1,0:T(8,128)(2,1)S(1)} fusion(bf16[1,3,384,4096]{3,2,1,0:T(8,128)(2,1)} %param.9, f32[2,768,384]{2,1,0:T(8,128)S(1)} %fusion.38), kind=kOutput, calls=%fused_computation.1 | convolution fusion | flops 2420834304 | bytes 11796480 | tf_op jit(solution)/shard_map/dot_general | solution.py:84
  135.7 0.5 fusion.100
  136.2 2.4 collective-permute-start.6
  138.6 0.2 fusion.101
  138.9 2.7 collective-permute-start.11
  141.6 18.4 %collective-permute-done.6 = bf16[128,4096]{1,0:T(8,128)(2,1)S(1)} collective-permute-done((bf16[128,4096]{1,0:T(8,128)(2,1)S(1)}, bf16[128,4096]{1,0:T(8,128)(2,1)S(1)}, u32[]{:S(2)}, u32[]{:S(2)}) %collective-permute-start.6) | collective-permute-done | bytes 1048608 | tf_op jit(solution)/shard_map/ppermute | solution.py:28
  159.9 3.2 collective-permute-start.10
  163.2 19.2 %collective-permute-done.11 = bf16[128,4096]{1,0:T(8,128)(2,1)S(1)} collective-permute-done((bf16[128,4096]{1,0:T(8,128)(2,1)S(1)}, bf16[128,4096]{1,0:T(8,128)(2,1)S(1)}, u32[]{:S(2)}, u32[]{:S(2)}) %collective-permute-start.11) | collective-permute-done | bytes 1048608 | tf_op jit(solution)/shard_map/ppermute | solution.py:28
  182.4 3.2 collective-permute-start.13
  185.6 4.6 %fusion.43 = f32[2,256,384]{2,1,0:T(8,128)S(1)} fusion(bf16[1,3,384,4096]{3,2,1,0:T(8,128)(2,1)} %param.9, bf16[256,4096]{1,0:T(8,128)(2,1)S(1)} %bitcast.162), kind=kOutput, calls=%fused_computation.55 | convolution fusion | flops 1610612736 | bytes 9175040 | tf_op jit(solution)/shard_map/rd,kfd->krf/dot_general | solution.py:80
  190.4 17.8 %collective-permute-done.9 = bf16[128,4096]{1,0:T(8,128)(2,1)S(1)} collective-permute-done((bf16[128,4096]{1,0:T(8,128)(2,1)S(1)}, bf16[128,4096]{1,0:T(8,128)(2,1)S(1)}, u32[]{:S(2)}, u32[]{:S(2)}) %collective-permute-start.9) | collective-permute-done | bytes 1048608 | tf_op jit(solution)/shard_map/ppermute | solution.py:28
  208.1 22.5 %collective-permute-done.12 = bf16[128,4096]{1,0:T(8,128)(2,1)S(1)} collective-permute-done((bf16[128,4096]{1,0:T(8,128)(2,1)S(1)}, bf16[128,4096]{1,0:T(8,128)(2,1)S(1)}, u32[]{:S(2)}, u32[]{:S(2)}) %collective-permute-start.12) | collective-permute-done | bytes 1048608 | tf_op jit(solution)/shard_map/ppermute | solution.py:28
  230.6 0.8 add_convert_fusion.3
  231.5 2.7 collective-permute-start.14
  234.1 0.1 constant_dynamic-update-slice_fusion.11
  234.2 0.1 constant_dynamic-update-slice_fusion.10
  234.6 5.6 %fusion.64 = (bf16[1,768,384]{2,1,0:T(8,128)(2,1)S(1)}, bf16[1,768,384]{2,1,0:T(8,128)(2,1)S(1)}) fusion(f32[2,768,384]{2,1,0:T(8,128)S(1)} %fusion.38, bf16[768,4096]{1,0:T(8,128)(2,1)S(1)} %constant_dynamic-update-slice_fusion.6, bf16[1,3,384,4096]{3,2,1,0:T(8,128)(2,1)} %param.9), kind=kOutput, calls=%fused_computation.78 | convolution fusion | flops 2419752960 | bytes 12976128 | tf_op jit(solution)/shard_map/dot_general | solution.py:89
  240.3 8.2 %convolution_bitcast_fusion = bf16[768,4096]{1,0:T(8,128)(2,1)S(1)} fusion(bf16[1,3,384,4096]{3,2,1,0:T(8,128)(2,1)} %param.9, bf16[1,768,384]{2,1,0:T(8,128)(2,1)S(1)} %get-tuple-element.69, bf16[1,768,384]{2,1,0:T(8,128)(2,1)S(1)} %get-tuple-element.68), kind=kOutput, calls=%fused_computation | convolution fusion | flops 4832428032 | bytes 13762560 | tf_op jit(solution)/shard_map/krf,kfd->rd/dot_general | solution.py:98
  248.5 1.9 fusion.99
  250.5 3.2 fusion.79
  253.7 5.9 %fusion.8 = bf16[256,4096]{1,0:T(8,128)(2,1)} fusion(bf16[1,3,384,4096]{3,2,1,0:T(8,128)(2,1)} %param.9, bf16[1,256,384]{2,1,0:T(8,128)(2,1)S(1)} %get-tuple-element.77, bf16[1,256,384]{2,1,0:T(8,128)(2,1)S(1)} %get-tuple-element.76), kind=kOutput, calls=%fused_computation.10 | convolution fusion | flops 1610809344 | bytes 8781824 | tf_op jit(solution)/shard_map/krf,kfd->rd/dot_general | solution.py:98
  259.6 15.9 %collective-permute-done.17 = bf16[128,4096]{1,0:T(8,128)(2,1)S(1)} collective-permute-done((bf16[128,4096]{1,0:T(8,128)(2,1)S(1)}, bf16[128,4096]{1,0:T(8,128)(2,1)S(1)}, u32[]{:S(2)}, u32[]{:S(2)}) %collective-permute-start.17) | collective-permute-done | bytes 1048608 | tf_op jit(solution)/shard_map/ppermute | solution.py:28
  275.5 0.3 convert_add_fusion.2
  275.8 0.3 convert_add_fusion.3
  276.1 4.6 %maximum_add_fusion = bf16[256,4096]{1,0:T(8,128)(2,1)} fusion(f32[128,4096]{1,0:T(8,128)S(1)} %convert_add_fusion.2, f32[128,4096]{1,0:T(8,128)S(1)} %convert_add_fusion.3, bf16[1,3,384,4096]{3,2,1,0:T(8,128)(2,1)} %param.9, f32[2,256,384]{2,1,0:T(8,128)S(1)} %fusion.43), kind=kOutput, calls=%fused_computation.18 | convolution fusion | flops 811139072 | bytes 10223616 | tf_op jit(solution)/shard_map/dot_general | solution.py:84
  280.7 2.7 collective-permute-start.18
  283.4 20.7 %collective-permute-done.22 = bf16[128,4096]{1,0:T(8,128)(2,1)S(1)} collective-permute-done((bf16[128,4096]{1,0:T(8,128)(2,1)S(1)}, bf16[128,4096]{1,0:T(8,128)(2,1)S(1)}, u32[]{:S(2)}, u32[]{:S(2)}) %collective-permute-start.22) | collective-permute-done | bytes 1048608 | tf_op jit(solution)/shard_map/ppermute | solution.py:28
  304.1 1.3 add_convert_fusion
  305.4 1.3 add_convert_fusion.1
  306.7 2.7 collective-permute-start.19
  309.4 9.5 %all-to-all-start.2 = ((bf16[32,8,4096]{2,1,0:T(8,128)(2,1)}), bf16[32,8,4096]{2,1,0:T(8,128)(2,1)S(1)}, u32[]{:S(2)}, u32[]{:S(2)}) async-start(bf16[32,8,4096]{2,1,0:T(8,128)(2,1)} %bitcast.163), calls=%async_computation.2 | async-start | bytes 4194304 | tf_op jit(solution)/shard_map/all_to_all | solution.py:74
  318.9 6.7 %collective-permute-done.21 = bf16[128,4096]{1,0:T(8,128)(2,1)} collective-permute-done((bf16[128,4096]{1,0:T(8,128)(2,1)}, bf16[128,4096]{1,0:T(8,128)(2,1)}, u32[]{:S(2)}, u32[]{:S(2)}) %collective-permute-start.21) | collective-permute-done | bytes 1048608 | tf_op jit(solution)/shard_map/ppermute | solution.py:28
  325.6 2.5 collective-permute-done.23
  328.2 1.8 convert_add_fusion
  330.0 20.7 %collective-permute-done.20 = bf16[128,4096]{1,0:T(8,128)(2,1)} collective-permute-done((bf16[128,4096]{1,0:T(8,128)(2,1)}, bf16[128,4096]{1,0:T(8,128)(2,1)}, u32[]{:S(2)}, u32[]{:S(2)}) %collective-permute-start.20) | collective-permute-done | bytes 1048608 | tf_op jit(solution)/shard_map/ppermute | solution.py:28
  350.6 1.5 convert_add_fusion.1
  352.1 1.9 fusion.29
  354.0 8.8 %all-to-all-start.3 = ((bf16[32,8,4096]{2,1,0:T(8,128)(2,1)}), bf16[32,8,4096]{2,1,0:T(8,128)(2,1)}, u32[]{:S(2)}, u32[]{:S(2)}) async-start(bf16[32,8,4096]{2,1,0:T(8,128)(2,1)} %fusion.29), calls=%async_computation.3 | async-start | bytes 4194304 | tf_op jit(solution)/shard_map/all_to_all | solution.py:74
  362.9 3.5 fusion.28
  366.4 24.8 %all-to-all-done.3 = bf16[32,8,4096]{2,1,0:T(8,128)(2,1)} async-done(((bf16[32,8,4096]{2,1,0:T(8,128)(2,1)}), bf16[32,8,4096]{2,1,0:T(8,128)(2,1)}, u32[]{:S(2)}, u32[]{:S(2)}) %all-to-all-start.3) | async-done | bytes 2097184 | tf_op jit(solution)/shard_map/all_to_all | solution.py:74
  391.2 3.1 convolution_convert_fusion.4
  (46 shorter events, 0.8 us)
Async XLA Ops:
  0.6 1.9 copy-start
  40.8 1.3 copy-start.2
  42.2 4.1 %copy-start.4 = (bf16[128,4096]{1,0:T(8,128)(2,1)S(1)}, bf16[128,4096]{1,0:T(8,128)(2,1)}, u32[]{:S(2)}) copy-start(bf16[128,4096]{1,0:T(8,128)(2,1)} %param.6) | copy-start | bytes 3145732
  42.2 4.1 %copy-start.6 = (f32[128]{0:T(128)S(1)}, f32[128]{0:T(128)}, u32[]{:S(2)}) copy-start(f32[128]{0:T(128)} %param.8) | copy-start | bytes 1540
  43.6 26.1 %collective-permute-start = (bf16[128,4096]{1,0:T(8,128)(2,1)}, bf16[128,4096]{1,0:T(8,128)(2,1)}, u32[]{:S(2)}, u32[]{:S(2)}) collective-permute-start(bf16[128,4096]{1,0:T(8,128)(2,1)} %get-tuple-element.75), channel_id=1, source_target_pairs={{0,32},{32,64},{64,96},{96,0},{1,33},{33,65},{65,97},{97,1},{2,34}... | collective-permute-start | bytes 3145736 | tf_op jit(solution)/shard_map/ppermute | solution.py:28
  44.8 24.9 %collective-permute-start.3 = (bf16[128,4096]{1,0:T(8,128)(2,1)}, bf16[128,4096]{1,0:T(8,128)(2,1)}, u32[]{:S(2)}, u32[]{:S(2)}) collective-permute-start(bf16[128,4096]{1,0:T(8,128)(2,1)} %get-tuple-element.74), channel_id=1, source_target_pairs={{0,96},{32,0},{64,32},{96,64},{1,97},{33,1},{65,33},{97,65},{2,98}... | collective-permute-start | bytes 3145736 | tf_op jit(solution)/shard_map/ppermute | solution.py:28
  48.4 32.8 %all-to-all-start = ((bf16[32,8,4096]{2,1,0:T(8,128)(2,1)}), bf16[32,8,4096]{2,1,0:T(8,128)(2,1)S(1)}, u32[]{:S(2)}, u32[]{:S(2)}) async-start(bf16[32,8,4096]{2,1,0:T(8,128)(2,1)} %fusion.12), calls=%async_computation | async-start | bytes 4194304 | tf_op jit(solution)/shard_map/all_to_all | solution.py:63
  52.9 39.2 %collective-permute-start.1 = (bf16[128,4096]{1,0:T(8,128)(2,1)}, bf16[128,4096]{1,0:T(8,128)(2,1)S(1)}, u32[]{:S(2)}, u32[]{:S(2)}) collective-permute-start(bf16[128,4096]{1,0:T(8,128)(2,1)} %get-tuple-element.74), channel_id=1, source_target_pairs={{0,32},{32,64},{64,96},{96,0},{1,33},{33,65},{65,97},{97,1},{2,34}... | collective-permute-start | bytes 3145736 | tf_op jit(solution)/shard_map/ppermute | solution.py:28
  53.0 39.1 %collective-permute-start.2 = (bf16[128,4096]{1,0:T(8,128)(2,1)}, bf16[128,4096]{1,0:T(8,128)(2,1)}, u32[]{:S(2)}, u32[]{:S(2)}) collective-permute-start(bf16[128,4096]{1,0:T(8,128)(2,1)} %get-tuple-element.75), channel_id=1, source_target_pairs={{0,96},{32,0},{64,32},{96,64},{1,97},{33,1},{65,33},{97,65},{2,98}... | collective-permute-start | bytes 3145736 | tf_op jit(solution)/shard_map/ppermute | solution.py:28
  69.8 44.9 %collective-permute-start.4 = (bf16[128,4096]{1,0:T(8,128)(2,1)}, bf16[128,4096]{1,0:T(8,128)(2,1)}, u32[]{:S(2)}, u32[]{:S(2)}) collective-permute-start(bf16[128,4096]{1,0:T(8,128)(2,1)} %collective-permute-done), channel_id=1, source_target_pairs={{0,32},{32,64},{64,96},{96,0},{1,33},{33,65},{65,97},{97,1},{2,34}... | collective-permute-start | bytes 3145736 | tf_op jit(solution)/shard_map/ppermute | solution.py:28
  69.8 44.9 %collective-permute-start.5 = (bf16[128,4096]{1,0:T(8,128)(2,1)}, bf16[128,4096]{1,0:T(8,128)(2,1)}, u32[]{:S(2)}, u32[]{:S(2)}) collective-permute-start(bf16[128,4096]{1,0:T(8,128)(2,1)} %collective-permute-done.3), channel_id=1, source_target_pairs={{0,96},{32,0},{64,32},{96,64},{1,97},{33,1},{65,33},{97,65},{2,98}... | collective-permute-start | bytes 3145736 | tf_op jit(solution)/shard_map/ppermute | solution.py:28
  136.2 49.5 %copy-start.3 = (bf16[32,8,4096]{2,1,0:T(8,128)(2,1)S(1)}, bf16[32,8,4096]{2,1,0:T(8,128)(2,1)}, u32[]{:S(2)}) copy-start(bf16[32,8,4096]{2,1,0:T(8,128)(2,1)} %copy-done.2) | copy-start | bytes 6291460
  136.2 23.8 %collective-permute-start.6 = (bf16[128,4096]{1,0:T(8,128)(2,1)S(1)}, bf16[128,4096]{1,0:T(8,128)(2,1)S(1)}, u32[]{:S(2)}, u32[]{:S(2)}) collective-permute-start(bf16[128,4096]{1,0:T(8,128)(2,1)S(1)} %get-tuple-element.67), channel_id=1, source_target_pairs={{0,96},{32,0},{64,32},{96,64},{1,97},{33,1},{65,33},{97,65},{2,98}... | collective-permute-start | bytes 3145736 | tf_op jit(solution)/shard_map/ppermute | solution.py:28
  138.8 24.4 %collective-permute-start.8 = (bf16[128,4096]{1,0:T(8,128)(2,1)S(1)}, bf16[128,4096]{1,0:T(8,128)(2,1)S(1)}, u32[]{:S(2)}, u32[]{:S(2)}) collective-permute-start(bf16[128,4096]{1,0:T(8,128)(2,1)S(1)} %get-tuple-element.73), channel_id=1, source_target_pairs={{0,32},{32,64},{64,96},{96,0},{1,33},{33,65},{65,97},{97,1},{2,34}... | collective-permute-start | bytes 3145736 | tf_op jit(solution)/shard_map/ppermute | solution.py:28
  138.9 43.5 %collective-permute-start.11 = (bf16[128,4096]{1,0:T(8,128)(2,1)S(1)}, bf16[128,4096]{1,0:T(8,128)(2,1)S(1)}, u32[]{:S(2)}, u32[]{:S(2)}) collective-permute-start(bf16[128,4096]{1,0:T(8,128)(2,1)S(1)} %get-tuple-element.72), channel_id=1, source_target_pairs={{0,96},{32,0},{64,32},{96,64},{1,97},{33,1},{65,33},{97,65},{2,98}... | collective-permute-start | bytes 3145736 | tf_op jit(solution)/shard_map/ppermute | solution.py:28
  141.5 48.7 %collective-permute-start.7 = (bf16[128,4096]{1,0:T(8,128)(2,1)S(1)}, bf16[128,4096]{1,0:T(8,128)(2,1)S(1)}, u32[]{:S(2)}, u32[]{:S(2)}) collective-permute-start(bf16[128,4096]{1,0:T(8,128)(2,1)S(1)} %get-tuple-element.66), channel_id=1, source_target_pairs={{0,32},{32,64},{64,96},{96,0},{1,33},{33,65},{65,97},{97,1},{2,34}... | collective-permute-start | bytes 3145736 | tf_op jit(solution)/shard_map/ppermute | solution.py:28
  141.5 66.6 %collective-permute-start.9 = (bf16[128,4096]{1,0:T(8,128)(2,1)S(1)}, bf16[128,4096]{1,0:T(8,128)(2,1)S(1)}, u32[]{:S(2)}, u32[]{:S(2)}) collective-permute-start(bf16[128,4096]{1,0:T(8,128)(2,1)S(1)} %get-tuple-element.72), channel_id=1, source_target_pairs={{0,32},{32,64},{64,96},{96,0},{1,33},{33,65},{65,97},{97,1},{2,34}... | collective-permute-start | bytes 3145736 | tf_op jit(solution)/shard_map/ppermute | solution.py:28
  159.9 48.2 %collective-permute-start.10 = (bf16[128,4096]{1,0:T(8,128)(2,1)S(1)}, bf16[128,4096]{1,0:T(8,128)(2,1)S(1)}, u32[]{:S(2)}, u32[]{:S(2)}) collective-permute-start(bf16[128,4096]{1,0:T(8,128)(2,1)S(1)} %get-tuple-element.73), channel_id=1, source_target_pairs={{0,96},{32,0},{64,32},{96,64},{1,97},{33,1},{65,33},{97,65},{2,98}... | collective-permute-start | bytes 3145736 | tf_op jit(solution)/shard_map/ppermute | solution.py:28
  163.2 67.4 %collective-permute-start.12 = (bf16[128,4096]{1,0:T(8,128)(2,1)S(1)}, bf16[128,4096]{1,0:T(8,128)(2,1)S(1)}, u32[]{:S(2)}, u32[]{:S(2)}) collective-permute-start(bf16[128,4096]{1,0:T(8,128)(2,1)S(1)} %collective-permute-done.8), channel_id=1, source_target_pairs={{0,32},{32,64},{64,96},{96,0},{1,33},{33,65},{65,97},{97,1},{2,34}... | collective-permute-start | bytes 3145736 | tf_op jit(solution)/shard_map/ppermute | solution.py:28
  182.4 48.2 %collective-permute-start.13 = (bf16[128,4096]{1,0:T(8,128)(2,1)S(1)}, bf16[128,4096]{1,0:T(8,128)(2,1)S(1)}, u32[]{:S(2)}, u32[]{:S(2)}) collective-permute-start(bf16[128,4096]{1,0:T(8,128)(2,1)S(1)} %collective-permute-done.11), channel_id=1, source_target_pairs={{0,96},{32,0},{64,32},{96,64},{1,97},{33,1},{65,33},{97,65},{2,98}... | collective-permute-start | bytes 3145736 | tf_op jit(solution)/shard_map/ppermute | solution.py:28
  190.3 69.3 %collective-permute-start.16 = (bf16[128,4096]{1,0:T(8,128)(2,1)S(1)}, bf16[128,4096]{1,0:T(8,128)(2,1)S(1)}, u32[]{:S(2)}, u32[]{:S(2)}) collective-permute-start(bf16[128,4096]{1,0:T(8,128)(2,1)S(1)} %get-tuple-element.65), channel_id=1, source_target_pairs={{0,96},{32,0},{64,32},{96,64},{1,97},{33,1},{65,33},{97,65},{2,98}... | collective-permute-start | bytes 3145736 | tf_op jit(solution)/shard_map/ppermute | solution.py:28
  208.1 67.7 %collective-permute-start.15 = (bf16[128,4096]{1,0:T(8,128)(2,1)S(1)}, bf16[128,4096]{1,0:T(8,128)(2,1)S(1)}, u32[]{:S(2)}, u32[]{:S(2)}) collective-permute-start(bf16[128,4096]{1,0:T(8,128)(2,1)S(1)} %get-tuple-element.64), channel_id=1, source_target_pairs={{0,32},{32,64},{64,96},{96,0},{1,33},{33,65},{65,97},{97,1},{2,34}... | collective-permute-start | bytes 3145736 | tf_op jit(solution)/shard_map/ppermute | solution.py:28
  231.4 44.1 %collective-permute-start.17 = (bf16[128,4096]{1,0:T(8,128)(2,1)S(1)}, bf16[128,4096]{1,0:T(8,128)(2,1)S(1)}, u32[]{:S(2)}, u32[]{:S(2)}) collective-permute-start(bf16[128,4096]{1,0:T(8,128)(2,1)S(1)} %get-tuple-element.63), channel_id=1, source_target_pairs={{0,32},{32,64},{64,96},{96,0},{1,33},{33,65},{65,97},{97,1},{2,34}... | collective-permute-start | bytes 3145736 | tf_op jit(solution)/shard_map/ppermute | solution.py:28
  231.5 44.3 %collective-permute-start.14 = (bf16[128,4096]{1,0:T(8,128)(2,1)S(1)}, bf16[128,4096]{1,0:T(8,128)(2,1)S(1)}, u32[]{:S(2)}, u32[]{:S(2)}) collective-permute-start(bf16[128,4096]{1,0:T(8,128)(2,1)S(1)} %get-tuple-element.62), channel_id=1, source_target_pairs={{0,96},{32,0},{64,32},{96,64},{1,97},{33,1},{65,33},{97,65},{2,98}... | collective-permute-start | bytes 3145736 | tf_op jit(solution)/shard_map/ppermute | solution.py:28
  280.7 23.4 %collective-permute-start.22 = (bf16[128,4096]{1,0:T(8,128)(2,1)S(1)}, bf16[128,4096]{1,0:T(8,128)(2,1)S(1)}, u32[]{:S(2)}, u32[]{:S(2)}) collective-permute-start(bf16[128,4096]{1,0:T(8,128)(2,1)S(1)} %get-tuple-element.52), channel_id=1, source_target_pairs={{0,32},{32,64},{64,96},{96,0},{1,33},{33,65},{65,97},{97,1},{2,34}... | collective-permute-start | bytes 3145736 | tf_op jit(solution)/shard_map/ppermute | solution.py:28
  280.7 24.7 %collective-permute-start.18 = (bf16[128,4096]{1,0:T(8,128)(2,1)S(1)}, bf16[128,4096]{1,0:T(8,128)(2,1)S(1)}, u32[]{:S(2)}, u32[]{:S(2)}) collective-permute-start(bf16[128,4096]{1,0:T(8,128)(2,1)S(1)} %get-tuple-element.48), channel_id=1, source_target_pairs={{0,96},{32,0},{64,32},{96,64},{1,97},{33,1},{65,33},{97,65},{2,98}... | collective-permute-start | bytes 3145736 | tf_op jit(solution)/shard_map/ppermute | solution.py:28
  283.4 42.3 %collective-permute-start.21 = (bf16[128,4096]{1,0:T(8,128)(2,1)}, bf16[128,4096]{1,0:T(8,128)(2,1)}, u32[]{:S(2)}, u32[]{:S(2)}) collective-permute-start(bf16[128,4096]{1,0:T(8,128)(2,1)} %get-tuple-element.50), channel_id=1, source_target_pairs={{0,96},{32,0},{64,32},{96,64},{1,97},{33,1},{65,33},{97,65},{2,98}... | collective-permute-start | bytes 3145736 | tf_op jit(solution)/shard_map/ppermute | solution.py:28
  305.4 22.8 %collective-permute-start.23 = (bf16[128,4096]{1,0:T(8,128)(2,1)}, bf16[128,4096]{1,0:T(8,128)(2,1)}, u32[]{:S(2)}, u32[]{:S(2)}) collective-permute-start(bf16[128,4096]{1,0:T(8,128)(2,1)} %add_convert_fusion), channel_id=1, source_target_pairs={{0,32},{32,64},{64,96},{96,0},{1,33},{33,65},{65,97},{97,1},{2,34}... | collective-permute-start | bytes 3145736 | tf_op jit(solution)/shard_map/ppermute | solution.py:28
  305.4 45.2 %collective-permute-start.20 = (bf16[128,4096]{1,0:T(8,128)(2,1)}, bf16[128,4096]{1,0:T(8,128)(2,1)}, u32[]{:S(2)}, u32[]{:S(2)}) collective-permute-start(bf16[128,4096]{1,0:T(8,128)(2,1)} %get-tuple-element.49), channel_id=1, source_target_pairs={{0,32},{32,64},{64,96},{96,0},{1,33},{33,65},{65,97},{97,1},{2,34}... | collective-permute-start | bytes 3145736 | tf_op jit(solution)/shard_map/ppermute | solution.py:28
  306.7 43.9 %collective-permute-start.19 = (bf16[128,4096]{1,0:T(8,128)(2,1)}, bf16[128,4096]{1,0:T(8,128)(2,1)S(1)}, u32[]{:S(2)}, u32[]{:S(2)}) collective-permute-start(bf16[128,4096]{1,0:T(8,128)(2,1)} %add_convert_fusion.1), channel_id=1, source_target_pairs={{0,96},{32,0},{64,32},{96,64},{1,97},{33,1},{65,33},{97,65},{2,98}... | collective-permute-start | bytes 3145736 | tf_op jit(solution)/shard_map/ppermute | solution.py:28
  309.4 44.6 %all-to-all-start.2 = ((bf16[32,8,4096]{2,1,0:T(8,128)(2,1)}), bf16[32,8,4096]{2,1,0:T(8,128)(2,1)S(1)}, u32[]{:S(2)}, u32[]{:S(2)}) async-start(bf16[32,8,4096]{2,1,0:T(8,128)(2,1)} %bitcast.163), calls=%async_computation.2 | async-start | bytes 4194304 | tf_op jit(solution)/shard_map/all_to_all | solution.py:74
  330.0 22.2 %copy-start.5 = (bf16[256,4096]{1,0:T(8,128)(2,1)S(1)}, bf16[256,4096]{1,0:T(8,128)(2,1)}, u32[]{:S(2)}) copy-start(bf16[256,4096]{1,0:T(8,128)(2,1)} %fusion.8) | copy-start | bytes 6291460
  354.0 37.2 %all-to-all-start.3 = ((bf16[32,8,4096]{2,1,0:T(8,128)(2,1)}), bf16[32,8,4096]{2,1,0:T(8,128)(2,1)}, u32[]{:S(2)}, u32[]{:S(2)}) async-start(bf16[32,8,4096]{2,1,0:T(8,128)(2,1)} %fusion.29), calls=%async_computation.3 | async-start | bytes 4194304 | tf_op jit(solution)/shard_map/all_to_all | solution.py:74
  362.9 31.4 %copy-start.1 = (bf16[128,4096]{1,0:T(8,128)(2,1)S(1)}, bf16[128,4096]{1,0:T(8,128)(2,1)}, u32[]{:S(2)}) copy-start(bf16[128,4096]{1,0:T(8,128)(2,1)} %param.5) | copy-start | bytes 3145732

commit v4 on v3

--- a/solution.py
+++ b/solution.py
@@ -99,13 +99,15 @@
 
 
 def joined(blocks):
-    return [blocks[0], jnp.concatenate(blocks[1:], 0)]
+    return [blocks[0]] + [jnp.concatenate(blocks[k:k + 2], 0) for k in (1, 3, 5)]
 
 
 def halves(parts):
-    rest = parts[1]
-    size = rest.shape[0] // 6
-    return [parts[0]] + [rest[k * size:(k + 1) * size] for k in range(6)]
+    out = [parts[0]]
+    for part in parts[1:]:
+        half = part.shape[0] // 2
+        out += [part[:half], part[half:]]
+    return out
 
 
 def shards(tokens, cotangent, routes, combine, expert_weights):

time: 395 us -> 399 us (1.010); the launches traced: 394 us -> 391 us
  waiting for transfers between devices: 225 us -> 239 us
  matrix products: 56 us -> 44.6 us
    ppermute x24, waiting for transfers between devices: 192 us -> 205 us  [shifted(): lax.ppermute(values, 'dp', perm=[(i, (i + step) % n) for i in range(n)])]
    dot_general x2 -> x4, matrix products: 14.1 us -> 8.69 us  [backward_rows(): jnp.einsum('krf,kfd->rd', both_grads, matrices[:2], preferred_element_typ...]
    dot_general x2 -> x4, matrix products: 10.2 us -> 6.57 us  [forward_rows(): jnp.dot(hidden, matrices[2], preferred_element_type=jnp.float32)]
    dot_general x2 -> x4, matrix products: 8.85 us -> 6.37 us  [backward_rows(): lax.dot_general(row_block, matrices[2], (((1,), (1,)), ((), ())), preferr...]
    dot_general x2 -> x4, matrix products: 13.4 us -> 13.6 us  [forward_rows(): jnp.einsum('rd,kfd->krf', row_block, matrices[:2], preferred_element_type...]
  transfers between devices with their start and end apart: 27 -> 27, of which waited for: 14 -> 15; matrix products, arithmetic and copies ran while one was open for 11% -> 12% of each run, Pallas kernels for 0% -> 0%
where the time goes in v4:
time: 399 us; the launch traced here: 391 us
  waiting for transfers between devices  239 us (60%)
  starting transfers between devices  50.4 us (13%)
  matrix products  44.6 us (11%)
  blocking collectives  37.5 us (9%)
  other arithmetic  9.83 us (2%)
  local copies, waits for them, and re-layouts  8.57 us (2%)
    ppermute x24, waiting for transfers between devices, shifted(): lax.ppermute(values, 'dp', perm=[(i, (i + step) % n) for i in range(n)])  205 us
    all_to_all x1, blocking collectives, arrive_rows(): lax.all_to_all(cold_buf.reshape(experts, slot_count, model_width), 'exper...  37.5 us
    ppermute x24, starting transfers between devices, shifted(): lax.ppermute(values, 'dp', perm=[(i, (i + step) % n) for i in range(n)])  28.3 us
    all_to_all x2, waiting for transfers between devices, return_rows(): lax.all_to_all(summed, 'expert', split_axis=0, concat_axis=0, tiled=True)  24.9 us
    all_to_all x2, starting transfers between devices, return_rows(): lax.all_to_all(summed, 'expert', split_axis=0, concat_axis=0, tiled=True)  17.6 us
    dot_general x4, matrix products, forward_rows(): jnp.einsum('rd,kfd->krf', row_block, matrices[:2], preferred_element_type...  13.6 us
    all_to_all x1, waiting for transfers between devices, arrive_rows(): lax.all_to_all(cold_buf.reshape(experts, slot_count, model_width), 'exper...  8.79 us
    dot_general x4, matrix products, backward_rows(): jnp.einsum('krf,kfd->rd', both_grads, matrices[:2], preferred_element_typ...  8.69 us
  transfers between devices with their start and end apart: 27, of which 15 were waited for; matrix products, arithmetic and copies ran while one was open for 12% of the time, Pallas kernels for 0%

profile of v4, /device:TPU:1, one launch (start us, length us, event | category | flops | bytes accessed | tf_op | source)
XLA Modules:
  0.0 391.1 jit_solution(18082093436212817298)
XLA Ops:
  3.3 37.5 %all_to_all.20 = bf16[32,8,4096]{2,1,0:T(8,128)(2,1)S(1)} all-to-all(bf16[32,8,4096]{2,1,0:T(8,128)(2,1)S(1)} %fusion.30), channel_id=1, replica_groups=mesh['dp'=4,'expert'=32] {'expert'}, dimensions={0} | all-to-all | bytes 4194304 | tf_op jit(solution)/shard_map/all_to_all | solution.py:63
  40.8 1.5 slice_bitcast_fusion
  42.8 1.2 collective-permute-start
  44.1 1.5 collective-permute-start.3
  45.5 2.1 fusion.29
  47.6 4.5 %all-to-all-start = ((bf16[32,8,4096]{2,1,0:T(8,128)(2,1)}), bf16[32,8,4096]{2,1,0:T(8,128)(2,1)S(1)}, u32[]{:S(2)}, u32[]{:S(2)}) async-start(bf16[32,8,4096]{2,1,0:T(8,128)(2,1)} %fusion.29), calls=%async_computation | async-start | bytes 4194304 | tf_op jit(solution)/shard_map/all_to_all | solution.py:63
  52.2 2.7 collective-permute-start.2
  54.9 14.1 %collective-permute-done = bf16[128,4096]{1,0:T(8,128)(2,1)} collective-permute-done((bf16[128,4096]{1,0:T(8,128)(2,1)}, bf16[128,4096]{1,0:T(8,128)(2,1)}, u32[]{:S(2)}, u32[]{:S(2)}) %collective-permute-start) | collective-permute-done | bytes 1048608 | tf_op jit(solution)/shard_map/ppermute | solution.py:28
  69.0 2.7 collective-permute-start.5
  71.7 8.8 %all-to-all-done = bf16[32,8,4096]{2,1,0:T(8,128)(2,1)S(1)} async-done(((bf16[32,8,4096]{2,1,0:T(8,128)(2,1)}), bf16[32,8,4096]{2,1,0:T(8,128)(2,1)S(1)}, u32[]{:S(2)}, u32[]{:S(2)}) %all-to-all-start) | async-done | bytes 2097184 | tf_op jit(solution)/shard_map/all_to_all | solution.py:63
  80.5 10.9 %collective-permute-done.1 = bf16[128,4096]{1,0:T(8,128)(2,1)S(1)} collective-permute-done((bf16[128,4096]{1,0:T(8,128)(2,1)}, bf16[128,4096]{1,0:T(8,128)(2,1)S(1)}, u32[]{:S(2)}, u32[]{:S(2)}) %collective-permute-start.1) | collective-permute-done | bytes 1048608 | tf_op jit(solution)/shard_map/ppermute | solution.py:28
  91.4 22.6 %collective-permute-done.4 = bf16[128,4096]{1,0:T(8,128)(2,1)} collective-permute-done((bf16[128,4096]{1,0:T(8,128)(2,1)}, bf16[128,4096]{1,0:T(8,128)(2,1)}, u32[]{:S(2)}, u32[]{:S(2)}) %collective-permute-start.4) | collective-permute-done | bytes 1048608 | tf_op jit(solution)/shard_map/ppermute | solution.py:28
  114.1 1.0 collective-permute-start.8
  115.1 1.8 collective-permute-start.10
  116.8 1.2 collective-permute-start.11
  118.3 5.3 %fusion.76 = f32[2,256,384]{2,1,0:T(8,128)S(1)} fusion(bf16[128,4096]{1,0:T(8,128)(2,1)} %collective-permute-done.5, bf16[128,4096]{1,0:T(8,128)(2,1)} %collective-permute-done.4, bf16[1,3,384,4096]{3,2,1,0:T(8,128)(2,1)} %param.9), kind=kOutput, calls=%fused_computation.84 | convolution fusion | flops 1614807040 | bytes 9175040 | tf_op jit(solution)/shard_map/rd,kfd->krf/dot_general | solution.py:80
  123.7 1.3 convolution_convert_fusion.3
  125.2 2.5 collective-permute-start.6
  127.8 3.4 fusion.79
  131.1 0.9 copy-done.11
  132.0 1.3 convolution_convert_fusion.2
  133.4 1.1 copy-done.8
  134.5 3.1 fusion.73
  137.6 45.5 %collective-permute-done.6 = bf16[128,4096]{1,0:T(8,128)(2,1)S(1)} collective-permute-done((bf16[128,4096]{1,0:T(8,128)(2,1)S(1)}, bf16[128,4096]{1,0:T(8,128)(2,1)S(1)}, u32[]{:S(2)}, u32[]{:S(2)}) %collective-permute-start.6) | collective-permute-done | bytes 1048608 | tf_op jit(solution)/shard_map/ppermute | solution.py:28
  183.1 0.9 collective-permute-start.7
  184.0 1.4 collective-permute-start.12
  185.4 1.3 collective-permute-start.13
  186.7 1.3 convolution_convert_fusion.4
  188.1 1.5 copy-done.3
  189.6 1.8 fusion.68
  191.4 16.3 %collective-permute-done.7 = bf16[128,4096]{1,0:T(8,128)(2,1)S(1)} collective-permute-done((bf16[128,4096]{1,0:T(8,128)(2,1)S(1)}, bf16[128,4096]{1,0:T(8,128)(2,1)S(1)}, u32[]{:S(2)}, u32[]{:S(2)}) %collective-permute-start.7) | collective-permute-done | bytes 1048608 | tf_op jit(solution)/shard_map/ppermute | solution.py:28
  207.7 2.7 collective-permute-start.16
  210.4 19.8 %collective-permute-done.12 = bf16[128,4096]{1,0:T(8,128)(2,1)S(1)} collective-permute-done((bf16[128,4096]{1,0:T(8,128)(2,1)S(1)}, bf16[128,4096]{1,0:T(8,128)(2,1)S(1)}, u32[]{:S(2)}, u32[]{:S(2)}) %collective-permute-start.12) | collective-permute-done | bytes 1048608 | tf_op jit(solution)/shard_map/ppermute | solution.py:28
  230.2 2.4 fusion.157
  232.6 1.8 fusion.19
  234.5 1.1 fusion.191
  235.8 1.5 collective-permute-start.14
  237.9 1.3 fusion.158
  239.2 1.8 fusion.22
  241.1 1.3 fusion.159
  242.4 1.8 fusion.25
  244.3 1.4 fusion.189
  245.6 1.3 fusion.156
  247.0 3.2 fusion.16
  250.1 2.5 collective-permute-done.15
  252.7 2.9 collective-permute-done.14
  255.9 19.3 %collective-permute-done.17 = bf16[128,4096]{1,0:T(8,128)(2,1)S(1)} collective-permute-done((bf16[128,4096]{1,0:T(8,128)(2,1)S(1)}, bf16[128,4096]{1,0:T(8,128)(2,1)S(1)}, u32[]{:S(2)}, u32[]{:S(2)}) %collective-permute-start.17) | collective-permute-done | bytes 1048608 | tf_op jit(solution)/shard_map/ppermute | solution.py:28
  275.4 2.7 maximum_add_fusion
  278.1 1.2 collective-permute-start.18
  279.6 20.4 %collective-permute-done.18 = bf16[128,4096]{1,0:T(8,128)(2,1)S(1)} collective-permute-done((bf16[128,4096]{1,0:T(8,128)(2,1)S(1)}, bf16[128,4096]{1,0:T(8,128)(2,1)S(1)}, u32[]{:S(2)}, u32[]{:S(2)}) %collective-permute-start.18) | collective-permute-done | bytes 1048608 | tf_op jit(solution)/shard_map/ppermute | solution.py:28
  300.0 1.2 add_convert_fusion.1
  301.2 2.1 collective-permute-start.19
  303.9 1.5 collective-permute-start.23
  305.4 9.0 %all-to-all-start.2 = ((bf16[32,8,4096]{2,1,0:T(8,128)(2,1)}), bf16[32,8,4096]{2,1,0:T(8,128)(2,1)S(1)}, u32[]{:S(2)}, u32[]{:S(2)}) async-start(bf16[32,8,4096]{2,1,0:T(8,128)(2,1)} %bitcast.296), calls=%async_computation.2 | async-start | bytes 4194304 | tf_op jit(solution)/shard_map/all_to_all | solution.py:74
  314.3 10.1 %collective-permute-done.20 = bf16[128,4096]{1,0:T(8,128)(2,1)} collective-permute-done((bf16[128,4096]{1,0:T(8,128)(2,1)}, bf16[128,4096]{1,0:T(8,128)(2,1)}, u32[]{:S(2)}, u32[]{:S(2)}) %collective-permute-start.20) | collective-permute-done | bytes 1048608 | tf_op jit(solution)/shard_map/ppermute | solution.py:28
  324.4 1.8 convert_add_fusion.1
  326.2 18.7 %collective-permute-done.21 = bf16[128,4096]{1,0:T(8,128)(2,1)} collective-permute-done((bf16[128,4096]{1,0:T(8,128)(2,1)}, bf16[128,4096]{1,0:T(8,128)(2,1)}, u32[]{:S(2)}, u32[]{:S(2)}) %collective-permute-start.21) | collective-permute-done | bytes 1048608 | tf_op jit(solution)/shard_map/ppermute | solution.py:28
  344.9 1.9 collective-permute-done.23
  346.9 1.8 convert_add_fusion
  348.7 1.9 fusion.48
  350.6 8.6 %all-to-all-start.3 = ((bf16[32,8,4096]{2,1,0:T(8,128)(2,1)}), bf16[32,8,4096]{2,1,0:T(8,128)(2,1)}, u32[]{:S(2)}, u32[]{:S(2)}) async-start(bf16[32,8,4096]{2,1,0:T(8,128)(2,1)} %fusion.48), calls=%async_computation.3 | async-start | bytes 4194304 | tf_op jit(solution)/shard_map/all_to_all | solution.py:74
  359.2 3.5 fusion.47
  362.8 24.9 %all-to-all-done.3 = bf16[32,8,4096]{2,1,0:T(8,128)(2,1)} async-done(((bf16[32,8,4096]{2,1,0:T(8,128)(2,1)}), bf16[32,8,4096]{2,1,0:T(8,128)(2,1)}, u32[]{:S(2)}, u32[]{:S(2)}) %all-to-all-start.3) | async-done | bytes 2097184 | tf_op jit(solution)/shard_map/all_to_all | solution.py:74
  387.6 3.1 convolution_convert_fusion.6
  (67 shorter events, 6.3 us)
Async XLA Ops:
  0.6 1.9 copy-start
  40.8 2.0 copy-start.2
  40.8 4.7 %copy-start.4 = (bf16[128,4096]{1,0:T(8,128)(2,1)S(1)}, bf16[128,4096]{1,0:T(8,128)(2,1)}, u32[]{:S(2)}) copy-start(bf16[128,4096]{1,0:T(8,128)(2,1)} %param.6) | copy-start | bytes 3145732
  40.8 4.7 %copy-start.6 = (f32[128]{0:T(128)S(1)}, f32[128]{0:T(128)}, u32[]{:S(2)}) copy-start(f32[128]{0:T(128)} %param.8) | copy-start | bytes 1540
  42.8 26.1 %collective-permute-start = (bf16[128,4096]{1,0:T(8,128)(2,1)}, bf16[128,4096]{1,0:T(8,128)(2,1)}, u32[]{:S(2)}, u32[]{:S(2)}) collective-permute-start(bf16[128,4096]{1,0:T(8,128)(2,1)} %get-tuple-element.69), channel_id=1, source_target_pairs={{0,32},{32,64},{64,96},{96,0},{1,33},{33,65},{65,97},{97,1},{2,34}... | collective-permute-start | bytes 3145736 | tf_op jit(solution)/shard_map/ppermute | solution.py:28
  44.1 24.9 %collective-permute-start.3 = (bf16[128,4096]{1,0:T(8,128)(2,1)}, bf16[128,4096]{1,0:T(8,128)(2,1)}, u32[]{:S(2)}, u32[]{:S(2)}) collective-permute-start(bf16[128,4096]{1,0:T(8,128)(2,1)} %get-tuple-element.68), channel_id=1, source_target_pairs={{0,96},{32,0},{64,32},{96,64},{1,97},{33,1},{65,33},{97,65},{2,98}... | collective-permute-start | bytes 3145736 | tf_op jit(solution)/shard_map/ppermute | solution.py:28
  47.6 32.8 %all-to-all-start = ((bf16[32,8,4096]{2,1,0:T(8,128)(2,1)}), bf16[32,8,4096]{2,1,0:T(8,128)(2,1)S(1)}, u32[]{:S(2)}, u32[]{:S(2)}) async-start(bf16[32,8,4096]{2,1,0:T(8,128)(2,1)} %fusion.29), calls=%async_computation | async-start | bytes 4194304 | tf_op jit(solution)/shard_map/all_to_all | solution.py:63
  52.2 39.2 %collective-permute-start.1 = (bf16[128,4096]{1,0:T(8,128)(2,1)}, bf16[128,4096]{1,0:T(8,128)(2,1)S(1)}, u32[]{:S(2)}, u32[]{:S(2)}) collective-permute-start(bf16[128,4096]{1,0:T(8,128)(2,1)} %get-tuple-element.68), channel_id=1, source_target_pairs={{0,32},{32,64},{64,96},{96,0},{1,33},{33,65},{65,97},{97,1},{2,34}... | collective-permute-start | bytes 3145736 | tf_op jit(solution)/shard_map/ppermute | solution.py:28
  52.2 39.1 %collective-permute-start.2 = (bf16[128,4096]{1,0:T(8,128)(2,1)}, bf16[128,4096]{1,0:T(8,128)(2,1)}, u32[]{:S(2)}, u32[]{:S(2)}) collective-permute-start(bf16[128,4096]{1,0:T(8,128)(2,1)} %get-tuple-element.69), channel_id=1, source_target_pairs={{0,96},{32,0},{64,32},{96,64},{1,97},{33,1},{65,33},{97,65},{2,98}... | collective-permute-start | bytes 3145736 | tf_op jit(solution)/shard_map/ppermute | solution.py:28
  69.0 44.9 %collective-permute-start.4 = (bf16[128,4096]{1,0:T(8,128)(2,1)}, bf16[128,4096]{1,0:T(8,128)(2,1)}, u32[]{:S(2)}, u32[]{:S(2)}) collective-permute-start(bf16[128,4096]{1,0:T(8,128)(2,1)} %collective-permute-done), channel_id=1, source_target_pairs={{0,32},{32,64},{64,96},{96,0},{1,33},{33,65},{65,97},{97,1},{2,34}... | collective-permute-start | bytes 3145736 | tf_op jit(solution)/shard_map/ppermute | solution.py:28
  69.0 44.9 %collective-permute-start.5 = (bf16[128,4096]{1,0:T(8,128)(2,1)}, bf16[128,4096]{1,0:T(8,128)(2,1)}, u32[]{:S(2)}, u32[]{:S(2)}) collective-permute-start(bf16[128,4096]{1,0:T(8,128)(2,1)} %collective-permute-done.3), channel_id=1, source_target_pairs={{0,96},{32,0},{64,32},{96,64},{1,97},{33,1},{65,33},{97,65},{2,98}... | collective-permute-start | bytes 3145736 | tf_op jit(solution)/shard_map/ppermute | solution.py:28
  91.4 22.6 %copy-start.7 = (bf16[128,4096]{1,0:T(8,128)(2,1)}, bf16[128,4096]{1,0:T(8,128)(2,1)S(1)}, u32[]{:S(2)}) copy-start(bf16[128,4096]{1,0:T(8,128)(2,1)S(1)} %collective-permute-done.1) | copy-start | bytes 3145732
  113.9 9.7 %slice-start = ((s8[9437184]{0:T(1024)(128)(4,1)}), s8[4194304]{0:T(1024)(128)(4,1)S(1)}, s32[]{:S(2)}) async-start(s8[9437184]{0:T(1024)(128)(4,1)} %bitcast.297), calls=%async_computation.4 | async-start | bytes 8388608
  114.1 69.9 %collective-permute-start.8 = (bf16[128,4096]{1,0:T(8,128)(2,1)S(1)}, bf16[128,4096]{1,0:T(8,128)(2,1)S(1)}, u32[]{:S(2)}, u32[]{:S(2)}) collective-permute-start(bf16[128,4096]{1,0:T(8,128)(2,1)S(1)} %get-tuple-element.65), channel_id=1, source_target_pairs={{0,32},{32,64},{64,96},{96,0},{1,33},{33,65},{65,97},{97,1},{2,34}... | collective-permute-start | bytes 3145736 | tf_op jit(solution)/shard_map/ppermute | solution.py:28
  115.1 92.7 %collective-permute-start.10 = (bf16[128,4096]{1,0:T(8,128)(2,1)S(1)}, bf16[128,4096]{1,0:T(8,128)(2,1)S(1)}, u32[]{:S(2)}, u32[]{:S(2)}) collective-permute-start(bf16[128,4096]{1,0:T(8,128)(2,1)S(1)} %get-tuple-element.65), channel_id=1, source_target_pairs={{0,96},{32,0},{64,32},{96,64},{1,97},{33,1},{65,33},{97,65},{2,98}... | collective-permute-start | bytes 3145736 | tf_op jit(solution)/shard_map/ppermute | solution.py:28
  116.8 6.8 %slice-start.1 = ((s8[9437184]{0:T(1024)(128)(4,1)}), s8[4194304]{0:T(1024)(128)(4,1)S(1)}, s32[]{:S(2)}) async-start(s8[9437184]{0:T(1024)(128)(4,1)} %bitcast.297), calls=%async_computation.5 | async-start | bytes 8388608
  116.8 6.8 %slice-start.2 = ((s8[9437184]{0:T(1024)(128)(4,1)}), s8[1048576]{0:T(1024)(128)(4,1)S(1)}, s32[]{:S(2)}) async-start(s8[9437184]{0:T(1024)(128)(4,1)} %bitcast.297), calls=%async_computation.6 | async-start | bytes 2097152
  116.8 68.6 %collective-permute-start.11 = (bf16[128,4096]{1,0:T(8,128)(2,1)S(1)}, bf16[128,4096]{1,0:T(8,128)(2,1)S(1)}, u32[]{:S(2)}, u32[]{:S(2)}) collective-permute-start(bf16[128,4096]{1,0:T(8,128)(2,1)S(1)} %get-tuple-element.64), channel_id=1, source_target_pairs={{0,96},{32,0},{64,32},{96,64},{1,97},{33,1},{65,33},{97,65},{2,98}... | collective-permute-start | bytes 3145736 | tf_op jit(solution)/shard_map/ppermute | solution.py:28
  118.0 92.4 %collective-permute-start.9 = (bf16[128,4096]{1,0:T(8,128)(2,1)S(1)}, bf16[128,4096]{1,0:T(8,128)(2,1)S(1)}, u32[]{:S(2)}, u32[]{:S(2)}) collective-permute-start(bf16[128,4096]{1,0:T(8,128)(2,1)S(1)} %get-tuple-element.64), channel_id=1, source_target_pairs={{0,32},{32,64},{64,96},{96,0},{1,33},{33,65},{65,97},{97,1},{2,34}... | collective-permute-start | bytes 3145736 | tf_op jit(solution)/shard_map/ppermute | solution.py:28
  123.7 1.3 copy-start.9
  125.2 57.9 %collective-permute-start.6 = (bf16[128,4096]{1,0:T(8,128)(2,1)S(1)}, bf16[128,4096]{1,0:T(8,128)(2,1)S(1)}, u32[]{:S(2)}, u32[]{:S(2)}) collective-permute-start(bf16[128,4096]{1,0:T(8,128)(2,1)S(1)} %get-tuple-element.67), channel_id=1, source_target_pairs={{0,96},{32,0},{64,32},{96,64},{1,97},{33,1},{65,33},{97,65},{2,98}... | collective-permute-start | bytes 3145736 | tf_op jit(solution)/shard_map/ppermute | solution.py:28
  131.1 0.9 copy-start.11
  133.3 1.2 copy-start.8
  137.6 50.4 %copy-start.13 = (f32[2,256,384]{2,1,0:T(8,128)}, f32[2,256,384]{2,1,0:T(8,128)S(1)}, u32[]{:S(2)}) copy-start(f32[2,256,384]{2,1,0:T(8,128)S(1)} %fusion.73) | copy-start | bytes 2359300
  183.1 24.6 %collective-permute-start.7 = (bf16[128,4096]{1,0:T(8,128)(2,1)S(1)}, bf16[128,4096]{1,0:T(8,128)(2,1)S(1)}, u32[]{:S(2)}, u32[]{:S(2)}) collective-permute-start(bf16[128,4096]{1,0:T(8,128)(2,1)S(1)} %get-tuple-element.66), channel_id=1, source_target_pairs={{0,32},{32,64},{64,96},{96,0},{1,33},{33,65},{65,97},{97,1},{2,34}... | collective-permute-start | bytes 3145736 | tf_op jit(solution)/shard_map/ppermute | solution.py:28
  184.0 46.2 %collective-permute-start.12 = (bf16[128,4096]{1,0:T(8,128)(2,1)S(1)}, bf16[128,4096]{1,0:T(8,128)(2,1)S(1)}, u32[]{:S(2)}, u32[]{:S(2)}) collective-permute-start(bf16[128,4096]{1,0:T(8,128)(2,1)S(1)} %collective-permute-done.8), channel_id=1, source_target_pairs={{0,32},{32,64},{64,96},{96,0},{1,33},{33,65},{65,97},{97,1},{2,34}... | collective-permute-start | bytes 3145736 | tf_op jit(solution)/shard_map/ppermute | solution.py:28
  185.4 44.8 %collective-permute-start.13 = (bf16[128,4096]{1,0:T(8,128)(2,1)S(1)}, bf16[128,4096]{1,0:T(8,128)(2,1)S(1)}, u32[]{:S(2)}, u32[]{:S(2)}) collective-permute-start(bf16[128,4096]{1,0:T(8,128)(2,1)S(1)} %collective-permute-done.11), channel_id=1, source_target_pairs={{0,96},{32,0},{64,32},{96,64},{1,97},{33,1},{65,33},{97,65},{2,98}... | collective-permute-start | bytes 3145736 | tf_op jit(solution)/shard_map/ppermute | solution.py:28
  188.0 1.6 copy-start.3
  207.7 44.9 %collective-permute-start.15 = (bf16[128,4096]{1,0:T(8,128)(2,1)S(1)}, bf16[128,4096]{1,0:T(8,128)(2,1)S(1)}, u32[]{:S(2)}, u32[]{:S(2)}) collective-permute-start(bf16[128,4096]{1,0:T(8,128)(2,1)S(1)} %slice.154), channel_id=1, source_target_pairs={{0,32},{32,64},{64,96},{96,0},{1,33},{33,65},{65,97},{97,1},{2,34}... | collective-permute-start | bytes 3145736 | tf_op jit(solution)/shard_map/ppermute | solution.py:28
  207.7 48.1 %collective-permute-start.16 = (bf16[128,4096]{1,0:T(8,128)(2,1)S(1)}, bf16[128,4096]{1,0:T(8,128)(2,1)S(1)}, u32[]{:S(2)}, u32[]{:S(2)}) collective-permute-start(bf16[128,4096]{1,0:T(8,128)(2,1)S(1)} %slice.155), channel_id=1, source_target_pairs={{0,96},{32,0},{64,32},{96,64},{1,97},{33,1},{65,33},{97,65},{2,98}... | collective-permute-start | bytes 3145736 | tf_op jit(solution)/shard_map/ppermute | solution.py:28
  235.8 2.1 copy-start.12
  235.8 19.7 %collective-permute-start.14 = (bf16[128,4096]{1,0:T(8,128)(2,1)S(1)}, bf16[128,4096]{1,0:T(8,128)(2,1)S(1)}, u32[]{:S(2)}, u32[]{:S(2)}) collective-permute-start(bf16[128,4096]{1,0:T(8,128)(2,1)S(1)} %add_convert_fusion.3), channel_id=1, source_target_pairs={{0,96},{32,0},{64,32},{96,64},{1,97},{33,1},{65,33},{97,65},{2,98}... | collective-permute-start | bytes 3145736 | tf_op jit(solution)/shard_map/ppermute | solution.py:28
  237.6 37.6 %collective-permute-start.17 = (bf16[128,4096]{1,0:T(8,128)(2,1)S(1)}, bf16[128,4096]{1,0:T(8,128)(2,1)S(1)}, u32[]{:S(2)}, u32[]{:S(2)}) collective-permute-start(bf16[128,4096]{1,0:T(8,128)(2,1)S(1)} %add_convert_fusion.2), channel_id=1, source_target_pairs={{0,32},{32,64},{64,96},{96,0},{1,33},{33,65},{65,97},{97,1},{2,34}... | collective-permute-start | bytes 3145736 | tf_op jit(solution)/shard_map/ppermute | solution.py:28
  239.2 1.9 copy-start.10
  278.1 21.9 %collective-permute-start.18 = (bf16[128,4096]{1,0:T(8,128)(2,1)S(1)}, bf16[128,4096]{1,0:T(8,128)(2,1)S(1)}, u32[]{:S(2)}, u32[]{:S(2)}) collective-permute-start(bf16[128,4096]{1,0:T(8,128)(2,1)S(1)} %get-tuple-element.48), channel_id=1, source_target_pairs={{0,96},{32,0},{64,32},{96,64},{1,97},{33,1},{65,33},{97,65},{2,98}... | collective-permute-start | bytes 3145736 | tf_op jit(solution)/shard_map/ppermute | solution.py:28
  279.3 24.3 %collective-permute-start.22 = (bf16[128,4096]{1,0:T(8,128)(2,1)S(1)}, bf16[128,4096]{1,0:T(8,128)(2,1)S(1)}, u32[]{:S(2)}, u32[]{:S(2)}) collective-permute-start(bf16[128,4096]{1,0:T(8,128)(2,1)S(1)} %get-tuple-element.52), channel_id=1, source_target_pairs={{0,32},{32,64},{64,96},{96,0},{1,33},{33,65},{65,97},{97,1},{2,34}... | collective-permute-start | bytes 3145736 | tf_op jit(solution)/shard_map/ppermute | solution.py:28
  279.6 44.8 %collective-permute-start.20 = (bf16[128,4096]{1,0:T(8,128)(2,1)}, bf16[128,4096]{1,0:T(8,128)(2,1)}, u32[]{:S(2)}, u32[]{:S(2)}) collective-permute-start(bf16[128,4096]{1,0:T(8,128)(2,1)} %get-tuple-element.49), channel_id=1, source_target_pairs={{0,32},{32,64},{64,96},{96,0},{1,33},{33,65},{65,97},{97,1},{2,34}... | collective-permute-start | bytes 3145736 | tf_op jit(solution)/shard_map/ppermute | solution.py:28
  301.2 23.2 %collective-permute-start.19 = (bf16[128,4096]{1,0:T(8,128)(2,1)}, bf16[128,4096]{1,0:T(8,128)(2,1)}, u32[]{:S(2)}, u32[]{:S(2)}) collective-permute-start(bf16[128,4096]{1,0:T(8,128)(2,1)} %add_convert_fusion.1), channel_id=1, source_target_pairs={{0,96},{32,0},{64,32},{96,64},{1,97},{33,1},{65,33},{97,65},{2,98}... | collective-permute-start | bytes 3145736 | tf_op jit(solution)/shard_map/ppermute | solution.py:28
  303.3 41.6 %collective-permute-start.21 = (bf16[128,4096]{1,0:T(8,128)(2,1)}, bf16[128,4096]{1,0:T(8,128)(2,1)}, u32[]{:S(2)}, u32[]{:S(2)}) collective-permute-start(bf16[128,4096]{1,0:T(8,128)(2,1)} %get-tuple-element.50), channel_id=1, source_target_pairs={{0,96},{32,0},{64,32},{96,64},{1,97},{33,1},{65,33},{97,65},{2,98}... | collective-permute-start | bytes 3145736 | tf_op jit(solution)/shard_map/ppermute | solution.py:28
  303.9 43.0 %collective-permute-start.23 = (bf16[128,4096]{1,0:T(8,128)(2,1)S(1)}, bf16[128,4096]{1,0:T(8,128)(2,1)}, u32[]{:S(2)}, u32[]{:S(2)}) collective-permute-start(bf16[128,4096]{1,0:T(8,128)(2,1)S(1)} %add_convert_fusion), channel_id=1, source_target_pairs={{0,32},{32,64},{64,96},{96,0},{1,33},{33,65},{65,97},{97,1},{2,34}... | collective-permute-start | bytes 3145736 | tf_op jit(solution)/shard_map/ppermute | solution.py:28
  305.4 45.2 %all-to-all-start.2 = ((bf16[32,8,4096]{2,1,0:T(8,128)(2,1)}), bf16[32,8,4096]{2,1,0:T(8,128)(2,1)S(1)}, u32[]{:S(2)}, u32[]{:S(2)}) async-start(bf16[32,8,4096]{2,1,0:T(8,128)(2,1)} %bitcast.296), calls=%async_computation.2 | async-start | bytes 4194304 | tf_op jit(solution)/shard_map/all_to_all | solution.py:74
  326.2 22.5 %copy-start.5 = (bf16[256,4096]{1,0:T(8,128)(2,1)S(1)}, bf16[256,4096]{1,0:T(8,128)(2,1)}, u32[]{:S(2)}) copy-start(bf16[256,4096]{1,0:T(8,128)(2,1)} %fusion.16) | copy-start | bytes 6291460
  350.6 37.0 %all-to-all-start.3 = ((bf16[32,8,4096]{2,1,0:T(8,128)(2,1)}), bf16[32,8,4096]{2,1,0:T(8,128)(2,1)}, u32[]{:S(2)}, u32[]{:S(2)}) async-start(bf16[32,8,4096]{2,1,0:T(8,128)(2,1)} %fusion.48), calls=%async_computation.3 | async-start | bytes 4194304 | tf_op jit(solution)/shard_map/all_to_all | solution.py:74
  359.2 31.5 %copy-start.1 = (bf16[128,4096]{1,0:T(8,128)(2,1)S(1)}, bf16[128,4096]{1,0:T(8,128)(2,1)}, u32[]{:S(2)}) copy-start(bf16[128,4096]{1,0:T(8,128)(2,1)} %param.5) | copy-start | bytes 3145732

commit v5 on v1

--- a/solution.py
+++ b/solution.py
@@ -123,12 +123,13 @@
     grad_parts = [
         backward_rows(block, f[0], f[1], weights) for block, f in zip(cot_blocks, forward)
     ]
-    fwd_total, grad_parts = lax.optimization_barrier((fwd_total, grad_parts))
+    grad_received = sum_start(grad_parts)
+    fwd_total, grad_received = lax.optimization_barrier((fwd_total, grad_received))
     cold_out = return_rows(fwd_total, experts, capacity, model_width)
     expert_out = collect(cold_layout, cold_out)
     combined = (combine[:, None] * expert_out).astype(jnp.bfloat16)
     combine_grad = jnp.sum(expert_out * cotangent_wide, 1)
-    grad_total = sum_finish(grad_parts, sum_start(grad_parts))
+    grad_total = sum_finish(grad_parts, grad_received)
     cold_grad_out = return_rows(grad_total, experts, capacity, model_width)
     input_grad = collect(cold_layout, cold_grad_out)
     token_grad = input_grad.astype(jnp.bfloat16)

time: 376 us -> 374 us (level)
  transfers between devices with their start and end apart: 27 -> 27, of which waited for: 14 -> 13; matrix products, arithmetic and copies ran while one was open for 18% -> 19% of each run, Pallas kernels for 0% -> 0%
where the time goes in v5:
time: 374 us; the launch traced here: 367 us
  waiting for transfers between devices  198 us (53%)
  matrix products  67.6 us (18%)
  starting transfers between devices  49.6 us (13%)
  blocking collectives  37.6 us (10%)
  other arithmetic  8.91 us (2%)
    ppermute x24, waiting for transfers between devices, shifted(): lax.ppermute(values, 'dp', perm=[(i, (i + step) % n) for i in range(n)])  164 us
    all_to_all x1, blocking collectives, arrive_rows(): lax.all_to_all(cold_buf.reshape(experts, slot_count, model_width), 'exper...  37.6 us
    ppermute x24, starting transfers between devices, shifted(): lax.ppermute(values, 'dp', perm=[(i, (i + step) % n) for i in range(n)])  30 us
    dot_general x7, matrix products, forward_rows(): jnp.einsum('rd,kfd->krf', row_block, matrices[:2], preferred_element_type...  27.3 us
    all_to_all x2, waiting for transfers between devices, return_rows(): lax.all_to_all(summed, 'expert', split_axis=0, concat_axis=0, tiled=True)  24.9 us
    all_to_all x2, starting transfers between devices, return_rows(): lax.all_to_all(summed, 'expert', split_axis=0, concat_axis=0, tiled=True)  15.1 us
    dot_general x7, matrix products, backward_rows(): jnp.einsum('krf,kfd->rd', both_grads, matrices[:2], preferred_element_typ...  14 us
    dot_general x7, matrix products, forward_rows(): jnp.dot(hidden, matrices[2], preferred_element_type=jnp.float32)  9.01 us
  transfers between devices with their start and end apart: 27, of which 13 were waited for; matrix products, arithmetic and copies ran while one was open for 19% of the time, Pallas kernels for 0%

profile of v5, /device:TPU:1, one launch (start us, length us, event | category | flops | bytes accessed | tf_op | source)
XLA Modules:
  0.0 366.9 jit_solution(990965388777659780)
XLA Ops:
  3.3 37.6 %all_to_all.20 = bf16[32,8,4096]{2,1,0:T(8,128)(2,1)S(1)} all-to-all(bf16[32,8,4096]{2,1,0:T(8,128)(2,1)S(1)} %fusion.39), channel_id=1, replica_groups=mesh['dp'=4,'expert'=32] {'expert'}, dimensions={0} | all-to-all | bytes 4194304 | tf_op jit(solution)/shard_map/all_to_all | solution.py:63
  40.8 1.4 copy-done.2
  42.2 1.1 slice_bitcast_fusion
  43.3 1.2 collective-permute-start
  44.5 1.5 collective-permute-start.3
  46.0 2.1 fusion.38
  48.1 4.5 %all-to-all-start = ((bf16[32,8,4096]{2,1,0:T(8,128)(2,1)}), bf16[32,8,4096]{2,1,0:T(8,128)(2,1)S(1)}, u32[]{:S(2)}, u32[]{:S(2)}) async-start(bf16[32,8,4096]{2,1,0:T(8,128)(2,1)} %fusion.38), calls=%async_computation | async-start | bytes 4194304 | tf_op jit(solution)/shard_map/all_to_all | solution.py:63
  52.7 2.7 collective-permute-start.2
  55.3 13.9 %collective-permute-done = bf16[128,4096]{1,0:T(8,128)(2,1)} collective-permute-done((bf16[128,4096]{1,0:T(8,128)(2,1)S(1)}, bf16[128,4096]{1,0:T(8,128)(2,1)}, u32[]{:S(2)}, u32[]{:S(2)}) %collective-permute-start) | collective-permute-done | bytes 1048608 | tf_op jit(solution)/shard_map/ppermute | solution.py:28
  69.2 2.7 collective-permute-start.5
  71.9 9.0 %all-to-all-done = bf16[32,8,4096]{2,1,0:T(8,128)(2,1)S(1)} async-done(((bf16[32,8,4096]{2,1,0:T(8,128)(2,1)}), bf16[32,8,4096]{2,1,0:T(8,128)(2,1)S(1)}, u32[]{:S(2)}, u32[]{:S(2)}) %all-to-all-start) | async-done | bytes 2097184 | tf_op jit(solution)/shard_map/all_to_all | solution.py:63
  80.9 10.8 %collective-permute-done.1 = bf16[128,4096]{1,0:T(8,128)(2,1)} collective-permute-done((bf16[128,4096]{1,0:T(8,128)(2,1)}, bf16[128,4096]{1,0:T(8,128)(2,1)}, u32[]{:S(2)}, u32[]{:S(2)}) %collective-permute-start.1) | collective-permute-done | bytes 1048608 | tf_op jit(solution)/shard_map/ppermute | solution.py:28
  91.7 22.5 %collective-permute-done.4 = bf16[128,4096]{1,0:T(8,128)(2,1)} collective-permute-done((bf16[128,4096]{1,0:T(8,128)(2,1)}, bf16[128,4096]{1,0:T(8,128)(2,1)}, u32[]{:S(2)}, u32[]{:S(2)}) %collective-permute-start.4) | collective-permute-done | bytes 1048608 | tf_op jit(solution)/shard_map/ppermute | solution.py:28
  114.3 1.2 collective-permute-start.8
  115.5 1.6 collective-permute-start.10
  117.0 1.4 collective-permute-start.11
  118.5 5.5 %fusion.123 = f32[2,128,384]{2,1,0:T(8,128)S(1)} fusion(bf16[128,4096]{1,0:T(8,128)(2,1)} %collective-permute-done.4, bf16[1,3,384,4096]{3,2,1,0:T(8,128)(2,1)} %param.9), kind=kOutput, calls=%fused_computation.105 | convolution fusion | flops 805306368 | bytes 7733248 | tf_op jit(solution)/shard_map/rd,kfd->krf/dot_general | solution.py:80
  124.0 2.6 convolution_convert_fusion.8
  126.6 2.8 collective-permute-start.6
  129.4 5.3 %fusion.126 = f32[2,128,384]{2,1,0:T(8,128)S(1)} fusion(bf16[128,4096]{1,0:T(8,128)(2,1)} %collective-permute-done.5, bf16[1,3,384,4096]{3,2,1,0:T(8,128)(2,1)} %param.9), kind=kOutput, calls=%fused_computation.106 | convolution fusion | flops 805306368 | bytes 7733248 | tf_op jit(solution)/shard_map/rd,kfd->krf/dot_general | solution.py:80
  135.6 3.4 fusion.120
  139.8 3.5 fusion.129
  144.0 3.4 fusion.135
  147.4 3.4 fusion.132
  151.0 10.1 %collective-permute-done.11 = bf16[128,4096]{1,0:T(8,128)(2,1)S(1)} collective-permute-done((bf16[128,4096]{1,0:T(8,128)(2,1)S(1)}, bf16[128,4096]{1,0:T(8,128)(2,1)S(1)}, u32[]{:S(2)}, u32[]{:S(2)}) %collective-permute-start.11) | collective-permute-done | bytes 1048608 | tf_op jit(solution)/shard_map/ppermute | solution.py:28
  161.0 0.9 collective-permute-start.12
  162.0 2.2 collective-permute-start.13
  166.5 2.7 fusion.115
  169.2 14.3 %collective-permute-done.6 = bf16[128,4096]{1,0:T(8,128)(2,1)S(1)} collective-permute-done((bf16[128,4096]{1,0:T(8,128)(2,1)S(1)}, bf16[128,4096]{1,0:T(8,128)(2,1)S(1)}, u32[]{:S(2)}, u32[]{:S(2)}) %collective-permute-start.6) | collective-permute-done | bytes 1048608 | tf_op jit(solution)/shard_map/ppermute | solution.py:28
  183.5 2.9 collective-permute-start.16
  186.4 20.1 %collective-permute-done.12 = bf16[128,4096]{1,0:T(8,128)(2,1)S(1)} collective-permute-done((bf16[128,4096]{1,0:T(8,128)(2,1)S(1)}, bf16[128,4096]{1,0:T(8,128)(2,1)S(1)}, u32[]{:S(2)}, u32[]{:S(2)}) %collective-permute-start.12) | collective-permute-done | bytes 1048608 | tf_op jit(solution)/shard_map/ppermute | solution.py:28
  206.5 1.1 fusion.256
  207.6 1.1 fusion.255
  208.7 1.0 fusion.76
  210.2 1.1 fusion.254
  211.5 2.3 collective-permute-start.14
  214.4 1.1 fusion.257
  215.5 1.1 fusion.258
  216.6 1.0 fusion.73
  217.6 1.0 fusion.79
  218.6 2.0 fusion.67
  220.6 1.1 fusion.259
  221.7 2.0 fusion.64
  223.7 1.0 fusion.61
  224.7 4.2 %collective-permute-done.15 = bf16[128,4096]{1,0:T(8,128)(2,1)S(1)} collective-permute-done((bf16[128,4096]{1,0:T(8,128)(2,1)S(1)}, bf16[128,4096]{1,0:T(8,128)(2,1)S(1)}, u32[]{:S(2)}, u32[]{:S(2)}) %collective-permute-start.15) | collective-permute-done | bytes 1048608 | tf_op jit(solution)/shard_map/ppermute | solution.py:28
  228.9 1.2 collective-permute-start.18
  230.2 20.7 %collective-permute-done.14 = bf16[128,4096]{1,0:T(8,128)(2,1)S(1)} collective-permute-done((bf16[128,4096]{1,0:T(8,128)(2,1)S(1)}, bf16[128,4096]{1,0:T(8,128)(2,1)S(1)}, u32[]{:S(2)}, u32[]{:S(2)}) %collective-permute-start.14) | collective-permute-done | bytes 1048608 | tf_op jit(solution)/shard_map/ppermute | solution.py:28
  252.1 2.1 collective-permute-start.22
  254.2 19.7 %collective-permute-done.17 = bf16[128,4096]{1,0:T(8,128)(2,1)S(1)} collective-permute-done((bf16[128,4096]{1,0:T(8,128)(2,1)S(1)}, bf16[128,4096]{1,0:T(8,128)(2,1)S(1)}, u32[]{:S(2)}, u32[]{:S(2)}) %collective-permute-start.17) | collective-permute-done | bytes 1048608 | tf_op jit(solution)/shard_map/ppermute | solution.py:28
  274.2 2.7 maximum_add_fusion
  276.9 1.3 add_convert_fusion.1
  278.2 1.2 collective-permute-start.20
  279.5 1.2 add_convert_fusion
  280.9 1.3 fusion.236
  282.2 8.3 %all-to-all-start.2 = ((bf16[32,8,4096]{2,1,0:T(8,128)(2,1)}), bf16[32,8,4096]{2,1,0:T(8,128)(2,1)S(1)}, u32[]{:S(2)}, u32[]{:S(2)}) async-start(bf16[32,8,4096]{2,1,0:T(8,128)(2,1)} %bitcast.534), calls=%async_computation.2 | async-start | bytes 4194304 | tf_op jit(solution)/shard_map/all_to_all | solution.py:74
  290.5 6.0 %collective-permute-done.21 = bf16[128,4096]{1,0:T(8,128)(2,1)} collective-permute-done((bf16[128,4096]{1,0:T(8,128)(2,1)}, bf16[128,4096]{1,0:T(8,128)(2,1)}, u32[]{:S(2)}, u32[]{:S(2)}) %collective-permute-start.21) | collective-permute-done | bytes 1048608 | tf_op jit(solution)/shard_map/ppermute | solution.py:28
  296.5 22.0 %collective-permute-done.20 = bf16[128,4096]{1,0:T(8,128)(2,1)} collective-permute-done((bf16[128,4096]{1,0:T(8,128)(2,1)}, bf16[128,4096]{1,0:T(8,128)(2,1)}, u32[]{:S(2)}, u32[]{:S(2)}) %collective-permute-start.20) | collective-permute-done | bytes 1048608 | tf_op jit(solution)/shard_map/ppermute | solution.py:28
  318.4 1.8 convert_add_fusion.1
  320.3 1.8 convert_add_fusion
  322.1 6.1 %fusion.110 = bf16[32,8,4096]{2,1,0:T(8,128)(2,1)} fusion(f32[128,4096]{1,0:T(8,128)S(1)} %convert_add_fusion, f32[128,4096]{1,0:T(8,128)S(1)} %convert_add_fusion.1, bf16[1,256,384]{2,1,0:T(8,128)(2,1)S(1)} %get-tuple-element.53, bf16[1,256,384]{2,1,0:T(8,128)(2,1)S(1)} %get-tuple-element.52, bf16[1,3,384,4096]{3,2,1,0:T(8,128)(2,1)} %param.9), kind=kOutput, calls=%fused_computation.88 | convolution fusion | flops 1616052224 | bytes 12976128 | tf_op jit(solution)/shard_map/krf,kfd->rd/dot_general | solution.py:98
  328.1 6.8 %all-to-all-start.3 = ((bf16[32,8,4096]{2,1,0:T(8,128)(2,1)}), bf16[32,8,4096]{2,1,0:T(8,128)(2,1)}, u32[]{:S(2)}, u32[]{:S(2)}) async-start(bf16[32,8,4096]{2,1,0:T(8,128)(2,1)} %fusion.110), calls=%async_computation.3 | async-start | bytes 4194304 | tf_op jit(solution)/shard_map/all_to_all | solution.py:74
  335.0 3.5 fusion.109
  338.5 24.9 %all-to-all-done.3 = bf16[32,8,4096]{2,1,0:T(8,128)(2,1)} async-done(((bf16[32,8,4096]{2,1,0:T(8,128)(2,1)}), bf16[32,8,4096]{2,1,0:T(8,128)(2,1)}, u32[]{:S(2)}, u32[]{:S(2)}) %all-to-all-start.3) | async-done | bytes 2097184 | tf_op jit(solution)/shard_map/all_to_all | solution.py:74
  363.4 3.1 convolution_convert_fusion.3
  (63 shorter events, 10.5 us)
Async XLA Ops:
  0.6 1.9 copy-start
  40.8 1.4 copy-start.2
  42.2 3.8 %copy-start.4 = (bf16[128,4096]{1,0:T(8,128)(2,1)S(1)}, bf16[128,4096]{1,0:T(8,128)(2,1)}, u32[]{:S(2)}) copy-start(bf16[128,4096]{1,0:T(8,128)(2,1)} %param.6) | copy-start | bytes 3145732
  42.2 3.8 %copy-start.5 = (f32[128]{0:T(128)S(1)}, f32[128]{0:T(128)}, u32[]{:S(2)}) copy-start(f32[128]{0:T(128)} %param.8) | copy-start | bytes 1540
  43.3 25.9 %collective-permute-start = (bf16[128,4096]{1,0:T(8,128)(2,1)S(1)}, bf16[128,4096]{1,0:T(8,128)(2,1)}, u32[]{:S(2)}, u32[]{:S(2)}) collective-permute-start(bf16[128,4096]{1,0:T(8,128)(2,1)S(1)} %get-tuple-element.51), channel_id=1, source_target_pairs={{0,32},{32,64},{64,96},{96,0},{1,33},{33,65},{65,97},{97,1},{2,34}... | collective-permute-start | bytes 3145736 | tf_op jit(solution)/shard_map/ppermute | solution.py:28
  44.5 24.7 %collective-permute-start.3 = (bf16[128,4096]{1,0:T(8,128)(2,1)}, bf16[128,4096]{1,0:T(8,128)(2,1)}, u32[]{:S(2)}, u32[]{:S(2)}) collective-permute-start(bf16[128,4096]{1,0:T(8,128)(2,1)} %get-tuple-element.50), channel_id=1, source_target_pairs={{0,96},{32,0},{64,32},{96,64},{1,97},{33,1},{65,33},{97,65},{2,98}... | collective-permute-start | bytes 3145736 | tf_op jit(solution)/shard_map/ppermute | solution.py:28
  48.1 32.8 %all-to-all-start = ((bf16[32,8,4096]{2,1,0:T(8,128)(2,1)}), bf16[32,8,4096]{2,1,0:T(8,128)(2,1)S(1)}, u32[]{:S(2)}, u32[]{:S(2)}) async-start(bf16[32,8,4096]{2,1,0:T(8,128)(2,1)} %fusion.38), calls=%async_computation | async-start | bytes 4194304 | tf_op jit(solution)/shard_map/all_to_all | solution.py:63
  52.6 39.1 %collective-permute-start.1 = (bf16[128,4096]{1,0:T(8,128)(2,1)}, bf16[128,4096]{1,0:T(8,128)(2,1)}, u32[]{:S(2)}, u32[]{:S(2)}) collective-permute-start(bf16[128,4096]{1,0:T(8,128)(2,1)} %get-tuple-element.50), channel_id=1, source_target_pairs={{0,32},{32,64},{64,96},{96,0},{1,33},{33,65},{65,97},{97,1},{2,34}... | collective-permute-start | bytes 3145736 | tf_op jit(solution)/shard_map/ppermute | solution.py:28
  52.7 39.0 %collective-permute-start.2 = (bf16[128,4096]{1,0:T(8,128)(2,1)S(1)}, bf16[128,4096]{1,0:T(8,128)(2,1)}, u32[]{:S(2)}, u32[]{:S(2)}) collective-permute-start(bf16[128,4096]{1,0:T(8,128)(2,1)S(1)} %get-tuple-element.51), channel_id=1, source_target_pairs={{0,96},{32,0},{64,32},{96,64},{1,97},{33,1},{65,33},{97,65},{2,98}... | collective-permute-start | bytes 3145736 | tf_op jit(solution)/shard_map/ppermute | solution.py:28
  69.2 44.9 %collective-permute-start.4 = (bf16[128,4096]{1,0:T(8,128)(2,1)}, bf16[128,4096]{1,0:T(8,128)(2,1)}, u32[]{:S(2)}, u32[]{:S(2)}) collective-permute-start(bf16[128,4096]{1,0:T(8,128)(2,1)} %collective-permute-done), channel_id=1, source_target_pairs={{0,32},{32,64},{64,96},{96,0},{1,33},{33,65},{65,97},{97,1},{2,34}... | collective-permute-start | bytes 3145736 | tf_op jit(solution)/shard_map/ppermute | solution.py:28
  69.2 44.9 %collective-permute-start.5 = (bf16[128,4096]{1,0:T(8,128)(2,1)}, bf16[128,4096]{1,0:T(8,128)(2,1)}, u32[]{:S(2)}, u32[]{:S(2)}) collective-permute-start(bf16[128,4096]{1,0:T(8,128)(2,1)} %collective-permute-done.3), channel_id=1, source_target_pairs={{0,96},{32,0},{64,32},{96,64},{1,97},{33,1},{65,33},{97,65},{2,98}... | collective-permute-start | bytes 3145736 | tf_op jit(solution)/shard_map/ppermute | solution.py:28
  114.3 36.6 %collective-permute-start.8 = (bf16[128,4096]{1,0:T(8,128)(2,1)S(1)}, bf16[128,4096]{1,0:T(8,128)(2,1)S(1)}, u32[]{:S(2)}, u32[]{:S(2)}) collective-permute-start(bf16[128,4096]{1,0:T(8,128)(2,1)S(1)} %get-tuple-element.49), channel_id=1, source_target_pairs={{0,32},{32,64},{64,96},{96,0},{1,33},{33,65},{65,97},{97,1},{2,34}... | collective-permute-start | bytes 3145736 | tf_op jit(solution)/shard_map/ppermute | solution.py:28
  115.5 46.5 %collective-permute-start.10 = (bf16[128,4096]{1,0:T(8,128)(2,1)S(1)}, bf16[128,4096]{1,0:T(8,128)(2,1)S(1)}, u32[]{:S(2)}, u32[]{:S(2)}) collective-permute-start(bf16[128,4096]{1,0:T(8,128)(2,1)S(1)} %get-tuple-element.49), channel_id=1, source_target_pairs={{0,96},{32,0},{64,32},{96,64},{1,97},{33,1},{65,33},{97,65},{2,98}... | collective-permute-start | bytes 3145736 | tf_op jit(solution)/shard_map/ppermute | solution.py:28
  117.0 44.0 %collective-permute-start.11 = (bf16[128,4096]{1,0:T(8,128)(2,1)S(1)}, bf16[128,4096]{1,0:T(8,128)(2,1)S(1)}, u32[]{:S(2)}, u32[]{:S(2)}) collective-permute-start(bf16[128,4096]{1,0:T(8,128)(2,1)S(1)} %get-tuple-element.48), channel_id=1, source_target_pairs={{0,96},{32,0},{64,32},{96,64},{1,97},{33,1},{65,33},{97,65},{2,98}... | collective-permute-start | bytes 3145736 | tf_op jit(solution)/shard_map/ppermute | solution.py:28
  118.4 50.8 %collective-permute-start.9 = (bf16[128,4096]{1,0:T(8,128)(2,1)S(1)}, bf16[128,4096]{1,0:T(8,128)(2,1)S(1)}, u32[]{:S(2)}, u32[]{:S(2)}) collective-permute-start(bf16[128,4096]{1,0:T(8,128)(2,1)S(1)} %get-tuple-element.48), channel_id=1, source_target_pairs={{0,32},{32,64},{64,96},{96,0},{1,33},{33,65},{65,97},{97,1},{2,34}... | collective-permute-start | bytes 3145736 | tf_op jit(solution)/shard_map/ppermute | solution.py:28
  118.5 16.3 %slice-start = ((s8[9437184]{0:T(1024)(128)(4,1)}), s8[4194304]{0:T(1024)(128)(4,1)S(1)}, s32[]{:S(2)}) async-start(s8[9437184]{0:T(1024)(128)(4,1)} %bitcast.532), calls=%async_computation.4 | async-start | bytes 8388608
  118.5 16.3 %slice-start.1 = ((s8[9437184]{0:T(1024)(128)(4,1)}), s8[4194304]{0:T(1024)(128)(4,1)S(1)}, s32[]{:S(2)}) async-start(s8[9437184]{0:T(1024)(128)(4,1)} %bitcast.532), calls=%async_computation.5 | async-start | bytes 8388608
  126.6 8.2 %slice-start.2 = ((s8[9437184]{0:T(1024)(128)(4,1)}), s8[1048576]{0:T(1024)(128)(4,1)S(1)}, s32[]{:S(2)}) async-start(s8[9437184]{0:T(1024)(128)(4,1)} %bitcast.532), calls=%async_computation.6 | async-start | bytes 2097152
  126.6 56.9 %collective-permute-start.6 = (bf16[128,4096]{1,0:T(8,128)(2,1)S(1)}, bf16[128,4096]{1,0:T(8,128)(2,1)S(1)}, u32[]{:S(2)}, u32[]{:S(2)}) collective-permute-start(bf16[128,4096]{1,0:T(8,128)(2,1)S(1)} %convolution_convert_fusion.8), channel_id=1, source_target_pairs={{0,96},{32,0},{64,32},{96,64},{1,97},{33,1},{65,33},{97,65},{2,98}... | collective-permute-start | bytes 3145736 | tf_op jit(solution)/shard_map/ppermute | solution.py:28
  134.8 4.2 %copy-start.6 = (f32[2,128,384]{2,1,0:T(8,128)}, f32[2,128,384]{2,1,0:T(8,128)S(1)}, u32[]{:S(2)}) copy-start(f32[2,128,384]{2,1,0:T(8,128)S(1)} %fusion.126) | copy-start | bytes 1179652
  150.9 35.5 %collective-permute-start.7 = (bf16[128,4096]{1,0:T(8,128)(2,1)S(1)}, bf16[128,4096]{1,0:T(8,128)(2,1)S(1)}, u32[]{:S(2)}, u32[]{:S(2)}) collective-permute-start(bf16[128,4096]{1,0:T(8,128)(2,1)S(1)} %convolution_convert_fusion.7), channel_id=1, source_target_pairs={{0,32},{32,64},{64,96},{96,0},{1,33},{33,65},{65,97},{97,1},{2,34}... | collective-permute-start | bytes 3145736 | tf_op jit(solution)/shard_map/ppermute | solution.py:28
  161.0 45.4 %collective-permute-start.12 = (bf16[128,4096]{1,0:T(8,128)(2,1)S(1)}, bf16[128,4096]{1,0:T(8,128)(2,1)S(1)}, u32[]{:S(2)}, u32[]{:S(2)}) collective-permute-start(bf16[128,4096]{1,0:T(8,128)(2,1)S(1)} %collective-permute-done.8), channel_id=1, source_target_pairs={{0,32},{32,64},{64,96},{96,0},{1,33},{33,65},{65,97},{97,1},{2,34}... | collective-permute-start | bytes 3145736 | tf_op jit(solution)/shard_map/ppermute | solution.py:28
  162.0 44.5 %collective-permute-start.13 = (bf16[128,4096]{1,0:T(8,128)(2,1)S(1)}, bf16[128,4096]{1,0:T(8,128)(2,1)S(1)}, u32[]{:S(2)}, u32[]{:S(2)}) collective-permute-start(bf16[128,4096]{1,0:T(8,128)(2,1)S(1)} %collective-permute-done.11), channel_id=1, source_target_pairs={{0,96},{32,0},{64,32},{96,64},{1,97},{33,1},{65,33},{97,65},{2,98}... | collective-permute-start | bytes 3145736 | tf_op jit(solution)/shard_map/ppermute | solution.py:28
  164.9 1.6 copy-start.3
  169.2 38.4 %copy-start.7 = (f32[2,128,384]{2,1,0:T(8,128)S(1)}, f32[2,128,384]{2,1,0:T(8,128)}, u32[]{:S(2)}) copy-start(f32[2,128,384]{2,1,0:T(8,128)} %copy-done.6) | copy-start | bytes 1179652
  169.2 59.8 %collective-permute-start.15 = (bf16[128,4096]{1,0:T(8,128)(2,1)S(1)}, bf16[128,4096]{1,0:T(8,128)(2,1)S(1)}, u32[]{:S(2)}, u32[]{:S(2)}) collective-permute-start(bf16[128,4096]{1,0:T(8,128)(2,1)S(1)} %convolution_convert_fusion.6), channel_id=1, source_target_pairs={{0,32},{32,64},{64,96},{96,0},{1,33},{33,65},{65,97},{97,1},{2,34}... | collective-permute-start | bytes 3145736 | tf_op jit(solution)/shard_map/ppermute | solution.py:28
  183.5 68.6 %collective-permute-start.16 = (bf16[128,4096]{1,0:T(8,128)(2,1)S(1)}, bf16[128,4096]{1,0:T(8,128)(2,1)S(1)}, u32[]{:S(2)}, u32[]{:S(2)}) collective-permute-start(bf16[128,4096]{1,0:T(8,128)(2,1)S(1)} %convolution_convert_fusion.5), channel_id=1, source_target_pairs={{0,96},{32,0},{64,32},{96,64},{1,97},{33,1},{65,33},{97,65},{2,98}... | collective-permute-start | bytes 3145736 | tf_op jit(solution)/shard_map/ppermute | solution.py:28
  209.7 67.2 %collective-permute-start.19 = (bf16[128,4096]{1,0:T(8,128)(2,1)S(1)}, bf16[128,4096]{1,0:T(8,128)(2,1)S(1)}, u32[]{:S(2)}, u32[]{:S(2)}) collective-permute-start(bf16[128,4096]{1,0:T(8,128)(2,1)S(1)} %fusion.76), channel_id=1, source_target_pairs={{0,32},{32,64},{64,96},{96,0},{1,33},{33,65},{65,97},{97,1},{2,34}... | collective-permute-start | bytes 3145736 | tf_op jit(solution)/shard_map/ppermute | solution.py:28
  211.5 39.4 %collective-permute-start.14 = (bf16[128,4096]{1,0:T(8,128)(2,1)S(1)}, bf16[128,4096]{1,0:T(8,128)(2,1)S(1)}, u32[]{:S(2)}, u32[]{:S(2)}) collective-permute-start(bf16[128,4096]{1,0:T(8,128)(2,1)S(1)} %add_convert_fusion.3), channel_id=1, source_target_pairs={{0,96},{32,0},{64,32},{96,64},{1,97},{33,1},{65,33},{97,65},{2,98}... | collective-permute-start | bytes 3145736 | tf_op jit(solution)/shard_map/ppermute | solution.py:28
  214.1 59.8 %collective-permute-start.17 = (bf16[128,4096]{1,0:T(8,128)(2,1)S(1)}, bf16[128,4096]{1,0:T(8,128)(2,1)S(1)}, u32[]{:S(2)}, u32[]{:S(2)}) collective-permute-start(bf16[128,4096]{1,0:T(8,128)(2,1)S(1)} %add_convert_fusion.2), channel_id=1, source_target_pairs={{0,32},{32,64},{64,96},{96,0},{1,33},{33,65},{65,97},{97,1},{2,34}... | collective-permute-start | bytes 3145736 | tf_op jit(solution)/shard_map/ppermute | solution.py:28
  228.9 48.0 %collective-permute-start.18 = (bf16[128,4096]{1,0:T(8,128)(2,1)S(1)}, bf16[128,4096]{1,0:T(8,128)(2,1)S(1)}, u32[]{:S(2)}, u32[]{:S(2)}) collective-permute-start(bf16[128,4096]{1,0:T(8,128)(2,1)S(1)} %fusion.79), channel_id=1, source_target_pairs={{0,96},{32,0},{64,32},{96,64},{1,97},{33,1},{65,33},{97,65},{2,98}... | collective-permute-start | bytes 3145736 | tf_op jit(solution)/shard_map/ppermute | solution.py:28
  250.9 45.5 %collective-permute-start.21 = (bf16[128,4096]{1,0:T(8,128)(2,1)}, bf16[128,4096]{1,0:T(8,128)(2,1)}, u32[]{:S(2)}, u32[]{:S(2)}) collective-permute-start(bf16[128,4096]{1,0:T(8,128)(2,1)} %fusion.67), channel_id=1, source_target_pairs={{0,32},{32,64},{64,96},{96,0},{1,33},{33,65},{65,97},{97,1},{2,34}... | collective-permute-start | bytes 3145736 | tf_op jit(solution)/shard_map/ppermute | solution.py:28
  252.1 22.1 %copy-start.8 = (f32[2,256,384]{2,1,0:T(8,128)S(1)}, f32[2,256,384]{2,1,0:T(8,128)}, u32[]{:S(2)}) copy-start(f32[2,256,384]{2,1,0:T(8,128)} %fusion.115) | copy-start | bytes 2359300
  252.1 68.1 %collective-permute-start.22 = (bf16[128,4096]{1,0:T(8,128)(2,1)}, bf16[128,4096]{1,0:T(8,128)(2,1)}, u32[]{:S(2)}, u32[]{:S(2)}) collective-permute-start(bf16[128,4096]{1,0:T(8,128)(2,1)} %fusion.64), channel_id=1, source_target_pairs={{0,96},{32,0},{64,32},{96,64},{1,97},{33,1},{65,33},{97,65},{2,98}... | collective-permute-start | bytes 3145736 | tf_op jit(solution)/shard_map/ppermute | solution.py:28
  278.2 40.2 %collective-permute-start.20 = (bf16[128,4096]{1,0:T(8,128)(2,1)}, bf16[128,4096]{1,0:T(8,128)(2,1)}, u32[]{:S(2)}, u32[]{:S(2)}) collective-permute-start(bf16[128,4096]{1,0:T(8,128)(2,1)} %add_convert_fusion.1), channel_id=1, source_target_pairs={{0,96},{32,0},{64,32},{96,64},{1,97},{33,1},{65,33},{97,65},{2,98}... | collective-permute-start | bytes 3145736 | tf_op jit(solution)/shard_map/ppermute | solution.py:28
  280.7 39.6 %collective-permute-start.23 = (bf16[128,4096]{1,0:T(8,128)(2,1)}, bf16[128,4096]{1,0:T(8,128)(2,1)}, u32[]{:S(2)}, u32[]{:S(2)}) collective-permute-start(bf16[128,4096]{1,0:T(8,128)(2,1)} %add_convert_fusion), channel_id=1, source_target_pairs={{0,32},{32,64},{64,96},{96,0},{1,33},{33,65},{65,97},{97,1},{2,34}... | collective-permute-start | bytes 3145736 | tf_op jit(solution)/shard_map/ppermute | solution.py:28
  282.2 45.9 %all-to-all-start.2 = ((bf16[32,8,4096]{2,1,0:T(8,128)(2,1)}), bf16[32,8,4096]{2,1,0:T(8,128)(2,1)S(1)}, u32[]{:S(2)}, u32[]{:S(2)}) async-start(bf16[32,8,4096]{2,1,0:T(8,128)(2,1)} %bitcast.534), calls=%async_computation.2 | async-start | bytes 4194304 | tf_op jit(solution)/shard_map/all_to_all | solution.py:74
  328.1 35.3 %all-to-all-start.3 = ((bf16[32,8,4096]{2,1,0:T(8,128)(2,1)}), bf16[32,8,4096]{2,1,0:T(8,128)(2,1)}, u32[]{:S(2)}, u32[]{:S(2)}) async-start(bf16[32,8,4096]{2,1,0:T(8,128)(2,1)} %fusion.110), calls=%async_computation.3 | async-start | bytes 4194304 | tf_op jit(solution)/shard_map/all_to_all | solution.py:74
  335.0 31.5 %copy-start.1 = (bf16[128,4096]{1,0:T(8,128)(2,1)S(1)}, bf16[128,4096]{1,0:T(8,128)(2,1)}, u32[]{:S(2)}) copy-start(bf16[128,4096]{1,0:T(8,128)(2,1)} %param.5) | copy-start | bytes 3145732

commit v6 on v5

--- a/solution.py
+++ b/solution.py
@@ -118,7 +118,7 @@
     fwd_parts = [f[2] for f in forward]
     cot_blocks = group_rows(cold_grad_arrived)
     fwd_received = sum_start(fwd_parts)
-    fwd_received, cot_blocks = lax.optimization_barrier((fwd_received, cot_blocks))
+    fwd_received, cot_blocks[5:] = lax.optimization_barrier((fwd_received, cot_blocks[5:]))
     fwd_total = sum_finish(fwd_parts, fwd_received)
     grad_parts = [
         backward_rows(block, f[0], f[1], weights) for block, f in zip(cot_blocks, forward)

time: 374 us -> 387 us (1.035)
  waiting for transfers between devices: 198 us -> 220 us
  starting transfers between devices: 49.6 us -> 44.7 us
    ppermute x24, waiting for transfers between devices: 164 us -> 178 us  [shifted(): lax.ppermute(values, 'dp', perm=[(i, (i + step) % n) for i in range(n)])]
    all_to_all x2, waiting for transfers between devices: 24.9 us -> 32.9 us  [return_rows(): lax.all_to_all(summed, 'expert', split_axis=0, concat_axis=0, tiled=True)]
  transfers between devices with their start and end apart: 27 -> 27, of which waited for: 13 -> 15; matrix products, arithmetic and copies ran while one was open for 19% -> 18% of each run, Pallas kernels for 0% -> 0%
where the time goes in v6:
time: 387 us; the launch traced here: 381 us
  waiting for transfers between devices  220 us (57%)
  matrix products  65.8 us (17%)
  starting transfers between devices  44.7 us (12%)
  blocking collectives  37.6 us (10%)
  other arithmetic  8.98 us (2%)
    ppermute x24, waiting for transfers between devices, shifted(): lax.ppermute(values, 'dp', perm=[(i, (i + step) % n) for i in range(n)])  178 us
    all_to_all x1, blocking collectives, arrive_rows(): lax.all_to_all(cold_buf.reshape(experts, slot_count, model_width), 'exper...  37.6 us
    all_to_all x2, waiting for transfers between devices, return_rows(): lax.all_to_all(summed, 'expert', split_axis=0, concat_axis=0, tiled=True)  32.9 us
    dot_general x7, matrix products, forward_rows(): jnp.einsum('rd,kfd->krf', row_block, matrices[:2], preferred_element_type...  27.4 us
    ppermute x24, starting transfers between devices, shifted(): lax.ppermute(values, 'dp', perm=[(i, (i + step) % n) for i in range(n)])  27.3 us
    dot_general x7, matrix products, backward_rows(): jnp.einsum('krf,kfd->rd', both_grads, matrices[:2], preferred_element_typ...  14 us
    all_to_all x2, starting transfers between devices, return_rows(): lax.all_to_all(summed, 'expert', split_axis=0, concat_axis=0, tiled=True)  13.2 us
    all_to_all x1, waiting for transfers between devices, arrive_rows(): lax.all_to_all(cold_buf.reshape(experts, slot_count, model_width), 'exper...  8.52 us
  transfers between devices with their start and end apart: 27, of which 15 were waited for; matrix products, arithmetic and copies ran while one was open for 18% of the time, Pallas kernels for 0%

profile of v6, /device:TPU:1, one launch (start us, length us, event | category | flops | bytes accessed | tf_op | source)
XLA Modules:
  0.0 380.8 jit_solution(17639284676567718550)
XLA Ops:
  0.6 0.8 fusion.264
  1.7 0.9 fusion.269
  3.3 37.6 %all_to_all.20 = bf16[32,8,4096]{2,1,0:T(8,128)(2,1)S(1)} all-to-all(bf16[32,8,4096]{2,1,0:T(8,128)(2,1)S(1)} %fusion.39), channel_id=1, replica_groups=mesh['dp'=4,'expert'=32] {'expert'}, dimensions={0} | all-to-all | bytes 4194304 | tf_op jit(solution)/shard_map/all_to_all | solution.py:63
  40.8 1.4 copy-done.2
  42.2 1.1 slice_bitcast_fusion
  43.3 2.5 collective-permute-start.3
  45.8 2.1 fusion.38
  47.9 4.2 %all-to-all-start = ((bf16[32,8,4096]{2,1,0:T(8,128)(2,1)}), bf16[32,8,4096]{2,1,0:T(8,128)(2,1)S(1)}, u32[]{:S(2)}, u32[]{:S(2)}) async-start(bf16[32,8,4096]{2,1,0:T(8,128)(2,1)} %fusion.38), calls=%async_computation | async-start | bytes 4194304 | tf_op jit(solution)/shard_map/all_to_all | solution.py:63
  52.7 2.6 collective-permute-start.2
  55.2 13.3 %collective-permute-done.3 = bf16[128,4096]{1,0:T(8,128)(2,1)} collective-permute-done((bf16[128,4096]{1,0:T(8,128)(2,1)}, bf16[128,4096]{1,0:T(8,128)(2,1)}, u32[]{:S(2)}, u32[]{:S(2)}) %collective-permute-start.3) | collective-permute-done | bytes 1048608 | tf_op jit(solution)/shard_map/ppermute | solution.py:28
  68.5 3.4 collective-permute-start.5
  71.9 8.5 %all-to-all-done = bf16[32,8,4096]{2,1,0:T(8,128)(2,1)S(1)} async-done(((bf16[32,8,4096]{2,1,0:T(8,128)(2,1)}), bf16[32,8,4096]{2,1,0:T(8,128)(2,1)S(1)}, u32[]{:S(2)}, u32[]{:S(2)}) %all-to-all-start) | async-done | bytes 2097184 | tf_op jit(solution)/shard_map/all_to_all | solution.py:63
  80.4 13.4 %collective-permute-done.1 = bf16[128,4096]{1,0:T(8,128)(2,1)} collective-permute-done((bf16[128,4096]{1,0:T(8,128)(2,1)}, bf16[128,4096]{1,0:T(8,128)(2,1)}, u32[]{:S(2)}, u32[]{:S(2)}) %collective-permute-start.1) | collective-permute-done | bytes 1048608 | tf_op jit(solution)/shard_map/ppermute | solution.py:28
  93.9 19.6 %collective-permute-done.5 = bf16[128,4096]{1,0:T(8,128)(2,1)} collective-permute-done((bf16[128,4096]{1,0:T(8,128)(2,1)}, bf16[128,4096]{1,0:T(8,128)(2,1)}, u32[]{:S(2)}, u32[]{:S(2)}) %collective-permute-start.5) | collective-permute-done | bytes 1048608 | tf_op jit(solution)/shard_map/ppermute | solution.py:28
  113.4 2.9 collective-permute-done.4
  116.5 2.7 collective-permute-start.10
  119.2 1.6 collective-permute-start.8
  120.8 4.8 %fusion.115 = f32[2,256,384]{2,1,0:T(8,128)S(1)} fusion(bf16[256,4096]{1,0:T(8,128)(2,1)S(1)} %bitcast.531, bf16[1,3,384,4096]{3,2,1,0:T(8,128)(2,1)} %param.9), kind=kOutput, calls=%fused_computation.103 | convolution fusion | flops 1610612736 | bytes 9175040 | tf_op jit(solution)/shard_map/rd,kfd->krf/dot_general | solution.py:80
  125.6 5.5 %fusion.120 = f32[2,128,384]{2,1,0:T(8,128)S(1)} fusion(bf16[128,4096]{1,0:T(8,128)(2,1)} %collective-permute-done, bf16[1,3,384,4096]{3,2,1,0:T(8,128)(2,1)} %param.9), kind=kOutput, calls=%fused_computation.104 | convolution fusion | flops 805306368 | bytes 7733248 | tf_op jit(solution)/shard_map/rd,kfd->krf/dot_general | solution.py:80
  131.1 3.4 fusion.123
  134.6 3.4 fusion.126
  138.0 3.4 fusion.129
  141.5 3.4 fusion.132
  144.9 3.4 fusion.135
  149.1 1.5 collective-permute-start.6
  151.4 0.7 convolution_convert_fusion.5
  152.9 0.7 convolution_convert_fusion.6
  154.6 1.1 fusion.258
  155.9 1.1 fusion.259
  157.0 6.6 %collective-permute-done.8 = bf16[128,4096]{1,0:T(8,128)(2,1)S(1)} collective-permute-done((bf16[128,4096]{1,0:T(8,128)(2,1)S(1)}, bf16[128,4096]{1,0:T(8,128)(2,1)S(1)}, u32[]{:S(2)}, u32[]{:S(2)}) %collective-permute-start.8) | collective-permute-done | bytes 1048608 | tf_op jit(solution)/shard_map/ppermute | solution.py:28
  163.6 1.1 fusion.256
  164.7 1.0 fusion.73
  165.7 1.0 fusion.61
  166.7 1.5 collective-permute-start.9
  168.2 1.1 fusion.257
  169.3 2.0 fusion.64
  171.3 2.0 fusion.67
  173.3 11.8 %collective-permute-done.6 = bf16[128,4096]{1,0:T(8,128)(2,1)S(1)} collective-permute-done((bf16[128,4096]{1,0:T(8,128)(2,1)S(1)}, bf16[128,4096]{1,0:T(8,128)(2,1)S(1)}, u32[]{:S(2)}, u32[]{:S(2)}) %collective-permute-start.6) | collective-permute-done | bytes 1048608 | tf_op jit(solution)/shard_map/ppermute | solution.py:28
  185.1 3.8 collective-permute-start.14
  188.9 18.6 %collective-permute-done.11 = bf16[128,4096]{1,0:T(8,128)(2,1)S(1)} collective-permute-done((bf16[128,4096]{1,0:T(8,128)(2,1)S(1)}, bf16[128,4096]{1,0:T(8,128)(2,1)S(1)}, u32[]{:S(2)}, u32[]{:S(2)}) %collective-permute-start.11) | collective-permute-done | bytes 1048608 | tf_op jit(solution)/shard_map/ppermute | solution.py:28
  207.5 23.5 %collective-permute-done.9 = bf16[128,4096]{1,0:T(8,128)(2,1)S(1)} collective-permute-done((bf16[128,4096]{1,0:T(8,128)(2,1)S(1)}, bf16[128,4096]{1,0:T(8,128)(2,1)S(1)}, u32[]{:S(2)}, u32[]{:S(2)}) %collective-permute-start.9) | collective-permute-done | bytes 1048608 | tf_op jit(solution)/shard_map/ppermute | solution.py:28
  231.0 1.1 fusion.255
  232.8 1.1 fusion.254
  233.9 1.5 collective-permute-start.15
  235.4 1.0 fusion.79
  236.4 1.0 fusion.76
  237.5 37.5 %collective-permute-done.12 = bf16[128,4096]{1,0:T(8,128)(2,1)S(1)} collective-permute-done((bf16[128,4096]{1,0:T(8,128)(2,1)S(1)}, bf16[128,4096]{1,0:T(8,128)(2,1)S(1)}, u32[]{:S(2)}, u32[]{:S(2)}) %collective-permute-start.12) | collective-permute-done | bytes 1048608 | tf_op jit(solution)/shard_map/ppermute | solution.py:28
  275.4 3.3 collective-permute-start.16
  278.9 2.7 maximum_add_fusion
  281.6 20.9 %collective-permute-done.17 = bf16[128,4096]{1,0:T(8,128)(2,1)S(1)} collective-permute-done((bf16[128,4096]{1,0:T(8,128)(2,1)S(1)}, bf16[128,4096]{1,0:T(8,128)(2,1)S(1)}, u32[]{:S(2)}, u32[]{:S(2)}) %collective-permute-start.17) | collective-permute-done | bytes 1048608 | tf_op jit(solution)/shard_map/ppermute | solution.py:28
  302.5 1.3 add_convert_fusion.1
  303.8 1.2 add_convert_fusion
  305.0 1.5 collective-permute-start.23
  306.5 1.3 fusion.236
  307.8 7.9 %all-to-all-start.2 = ((bf16[32,8,4096]{2,1,0:T(8,128)(2,1)}), bf16[32,8,4096]{2,1,0:T(8,128)(2,1)S(1)}, u32[]{:S(2)}, u32[]{:S(2)}) async-start(bf16[32,8,4096]{2,1,0:T(8,128)(2,1)} %bitcast.534), calls=%async_computation.2 | async-start | bytes 4194304 | tf_op jit(solution)/shard_map/all_to_all | solution.py:74
  315.8 9.9 %collective-permute-done.18 = bf16[128,4096]{1,0:T(8,128)(2,1)} collective-permute-done((bf16[128,4096]{1,0:T(8,128)(2,1)}, bf16[128,4096]{1,0:T(8,128)(2,1)}, u32[]{:S(2)}, u32[]{:S(2)}) %collective-permute-start.18) | collective-permute-done | bytes 1048608 | tf_op jit(solution)/shard_map/ppermute | solution.py:28
  325.7 1.8 convert_add_fusion.1
  328.0 1.8 convert_add_fusion
  329.8 6.1 %fusion.110 = bf16[32,8,4096]{2,1,0:T(8,128)(2,1)} fusion(f32[128,4096]{1,0:T(8,128)S(1)} %convert_add_fusion, f32[128,4096]{1,0:T(8,128)S(1)} %convert_add_fusion.1, bf16[1,256,384]{2,1,0:T(8,128)(2,1)S(1)} %get-tuple-element.43, bf16[1,256,384]{2,1,0:T(8,128)(2,1)S(1)} %get-tuple-element.42, bf16[1,3,384,4096]{3,2,1,0:T(8,128)(2,1)} %param.9), kind=kOutput, calls=%fused_computation.88 | convolution fusion | flops 1616052224 | bytes 12976128 | tf_op jit(solution)/shard_map/krf,kfd->rd/dot_general | solution.py:98
  335.9 8.0 %all-to-all-done.2 = bf16[32,8,4096]{2,1,0:T(8,128)(2,1)S(1)} async-done(((bf16[32,8,4096]{2,1,0:T(8,128)(2,1)}), bf16[32,8,4096]{2,1,0:T(8,128)(2,1)S(1)}, u32[]{:S(2)}, u32[]{:S(2)}) %all-to-all-start.2) | async-done | bytes 2097184 | tf_op jit(solution)/shard_map/all_to_all | solution.py:74
  343.9 5.2 %all-to-all-start.3 = ((bf16[32,8,4096]{2,1,0:T(8,128)(2,1)}), bf16[32,8,4096]{2,1,0:T(8,128)(2,1)}, u32[]{:S(2)}, u32[]{:S(2)}) async-start(bf16[32,8,4096]{2,1,0:T(8,128)(2,1)} %fusion.110), calls=%async_computation.3 | async-start | bytes 4194304 | tf_op jit(solution)/shard_map/all_to_all | solution.py:74
  349.2 3.5 fusion.109
  352.7 24.9 %all-to-all-done.3 = bf16[32,8,4096]{2,1,0:T(8,128)(2,1)} async-done(((bf16[32,8,4096]{2,1,0:T(8,128)(2,1)}), bf16[32,8,4096]{2,1,0:T(8,128)(2,1)}, u32[]{:S(2)}, u32[]{:S(2)}) %all-to-all-start.3) | async-done | bytes 2097184 | tf_op jit(solution)/shard_map/all_to_all | solution.py:74
  377.6 3.1 convolution_convert_fusion.3
  (57 shorter events, 7.1 us)
Async XLA Ops:
  0.6 1.9 copy-start
  40.8 1.4 copy-start.2
  42.2 3.6 copy-start.4
  42.2 3.6 copy-start.5
  43.3 25.2 %collective-permute-start.3 = (bf16[128,4096]{1,0:T(8,128)(2,1)}, bf16[128,4096]{1,0:T(8,128)(2,1)}, u32[]{:S(2)}, u32[]{:S(2)}) collective-permute-start(bf16[128,4096]{1,0:T(8,128)(2,1)} %get-tuple-element.40), channel_id=1, source_target_pairs={{0,96},{32,0},{64,32},{96,64},{1,97},{33,1},{65,33},{97,65},{2,98}... | collective-permute-start | bytes 3145736 | tf_op jit(solution)/shard_map/ppermute | solution.py:28
  45.8 26.1 %collective-permute-start = (bf16[128,4096]{1,0:T(8,128)(2,1)S(1)}, bf16[128,4096]{1,0:T(8,128)(2,1)}, u32[]{:S(2)}, u32[]{:S(2)}) collective-permute-start(bf16[128,4096]{1,0:T(8,128)(2,1)S(1)} %get-tuple-element.41), channel_id=1, source_target_pairs={{0,32},{32,64},{64,96},{96,0},{1,33},{33,65},{65,97},{97,1},{2,34}... | collective-permute-start | bytes 3145736 | tf_op jit(solution)/shard_map/ppermute | solution.py:28
  47.9 32.5 %all-to-all-start = ((bf16[32,8,4096]{2,1,0:T(8,128)(2,1)}), bf16[32,8,4096]{2,1,0:T(8,128)(2,1)S(1)}, u32[]{:S(2)}, u32[]{:S(2)}) async-start(bf16[32,8,4096]{2,1,0:T(8,128)(2,1)} %fusion.38), calls=%async_computation | async-start | bytes 4194304 | tf_op jit(solution)/shard_map/all_to_all | solution.py:63
  52.1 41.7 %collective-permute-start.1 = (bf16[128,4096]{1,0:T(8,128)(2,1)}, bf16[128,4096]{1,0:T(8,128)(2,1)}, u32[]{:S(2)}, u32[]{:S(2)}) collective-permute-start(bf16[128,4096]{1,0:T(8,128)(2,1)} %get-tuple-element.40), channel_id=1, source_target_pairs={{0,32},{32,64},{64,96},{96,0},{1,33},{33,65},{65,97},{97,1},{2,34}... | collective-permute-start | bytes 3145736 | tf_op jit(solution)/shard_map/ppermute | solution.py:28
  52.7 41.2 %collective-permute-start.2 = (bf16[128,4096]{1,0:T(8,128)(2,1)S(1)}, bf16[128,4096]{1,0:T(8,128)(2,1)}, u32[]{:S(2)}, u32[]{:S(2)}) collective-permute-start(bf16[128,4096]{1,0:T(8,128)(2,1)S(1)} %get-tuple-element.41), channel_id=1, source_target_pairs={{0,96},{32,0},{64,32},{96,64},{1,97},{33,1},{65,33},{97,65},{2,98}... | collective-permute-start | bytes 3145736 | tf_op jit(solution)/shard_map/ppermute | solution.py:28
  68.5 44.9 %collective-permute-start.5 = (bf16[128,4096]{1,0:T(8,128)(2,1)}, bf16[128,4096]{1,0:T(8,128)(2,1)}, u32[]{:S(2)}, u32[]{:S(2)}) collective-permute-start(bf16[128,4096]{1,0:T(8,128)(2,1)} %collective-permute-done.3), channel_id=1, source_target_pairs={{0,96},{32,0},{64,32},{96,64},{1,97},{33,1},{65,33},{97,65},{2,98}... | collective-permute-start | bytes 3145736 | tf_op jit(solution)/shard_map/ppermute | solution.py:28
  71.9 44.4 %collective-permute-start.4 = (bf16[128,4096]{1,0:T(8,128)(2,1)}, bf16[128,4096]{1,0:T(8,128)(2,1)}, u32[]{:S(2)}, u32[]{:S(2)}) collective-permute-start(bf16[128,4096]{1,0:T(8,128)(2,1)} %collective-permute-done), channel_id=1, source_target_pairs={{0,32},{32,64},{64,96},{96,0},{1,33},{33,65},{65,97},{97,1},{2,34}... | collective-permute-start | bytes 3145736 | tf_op jit(solution)/shard_map/ppermute | solution.py:28
  80.4 40.4 %copy-start.3 = (bf16[32,8,4096]{2,1,0:T(8,128)(2,1)S(1)}, bf16[32,8,4096]{2,1,0:T(8,128)(2,1)}, u32[]{:S(2)}) copy-start(bf16[32,8,4096]{2,1,0:T(8,128)(2,1)} %copy-done.2) | copy-start | bytes 6291460
  116.5 37.9 %collective-permute-start.21 = (bf16[128,4096]{1,0:T(8,128)(2,1)S(1)}, bf16[128,4096]{1,0:T(8,128)(2,1)S(1)}, u32[]{:S(2)}, u32[]{:S(2)}) collective-permute-start(bf16[128,4096]{1,0:T(8,128)(2,1)S(1)} %get-tuple-element.38), channel_id=1, source_target_pairs={{0,32},{32,64},{64,96},{96,0},{1,33},{33,65},{65,97},{97,1},{2,34}... | collective-permute-start | bytes 3145736 | tf_op jit(solution)/shard_map/ppermute | solution.py:28
  116.5 39.2 %collective-permute-start.10 = (bf16[128,4096]{1,0:T(8,128)(2,1)S(1)}, bf16[128,4096]{1,0:T(8,128)(2,1)S(1)}, u32[]{:S(2)}, u32[]{:S(2)}) collective-permute-start(bf16[128,4096]{1,0:T(8,128)(2,1)S(1)} %get-tuple-element.38), channel_id=1, source_target_pairs={{0,96},{32,0},{64,32},{96,64},{1,97},{33,1},{65,33},{97,65},{2,98}... | collective-permute-start | bytes 3145736 | tf_op jit(solution)/shard_map/ppermute | solution.py:28
  119.2 47.5 %collective-permute-start.19 = (bf16[128,4096]{1,0:T(8,128)(2,1)S(1)}, bf16[128,4096]{1,0:T(8,128)(2,1)S(1)}, u32[]{:S(2)}, u32[]{:S(2)}) collective-permute-start(bf16[128,4096]{1,0:T(8,128)(2,1)S(1)} %get-tuple-element.39), channel_id=1, source_target_pairs={{0,96},{32,0},{64,32},{96,64},{1,97},{33,1},{65,33},{97,65},{2,98}... | collective-permute-start | bytes 3145736 | tf_op jit(solution)/shard_map/ppermute | solution.py:28
  119.2 44.4 %collective-permute-start.8 = (bf16[128,4096]{1,0:T(8,128)(2,1)S(1)}, bf16[128,4096]{1,0:T(8,128)(2,1)S(1)}, u32[]{:S(2)}, u32[]{:S(2)}) collective-permute-start(bf16[128,4096]{1,0:T(8,128)(2,1)S(1)} %get-tuple-element.39), channel_id=1, source_target_pairs={{0,32},{32,64},{64,96},{96,0},{1,33},{33,65},{65,97},{97,1},{2,34}... | collective-permute-start | bytes 3145736 | tf_op jit(solution)/shard_map/ppermute | solution.py:28
  120.8 10.3 %slice-start = ((s8[9437184]{0:T(1024)(128)(4,1)}), s8[1048576]{0:T(1024)(128)(4,1)S(1)}, s32[]{:S(2)}) async-start(s8[9437184]{0:T(1024)(128)(4,1)} %bitcast.532), calls=%async_computation.4 | async-start | bytes 2097152
  120.8 10.3 %slice-start.1 = ((s8[9437184]{0:T(1024)(128)(4,1)}), s8[4194304]{0:T(1024)(128)(4,1)S(1)}, s32[]{:S(2)}) async-start(s8[9437184]{0:T(1024)(128)(4,1)} %bitcast.532), calls=%async_computation.5 | async-start | bytes 8388608
  125.6 5.5 %slice-start.2 = ((s8[9437184]{0:T(1024)(128)(4,1)}), s8[4194304]{0:T(1024)(128)(4,1)S(1)}, s32[]{:S(2)}) async-start(s8[9437184]{0:T(1024)(128)(4,1)} %bitcast.532), calls=%async_computation.6 | async-start | bytes 8388608
  149.1 35.9 %collective-permute-start.6 = (bf16[128,4096]{1,0:T(8,128)(2,1)S(1)}, bf16[128,4096]{1,0:T(8,128)(2,1)S(1)}, u32[]{:S(2)}, u32[]{:S(2)}) collective-permute-start(bf16[128,4096]{1,0:T(8,128)(2,1)S(1)} %convolution_convert_fusion.8), channel_id=1, source_target_pairs={{0,96},{32,0},{64,32},{96,64},{1,97},{33,1},{65,33},{97,65},{2,98}... | collective-permute-start | bytes 3145736 | tf_op jit(solution)/shard_map/ppermute | solution.py:28
  154.4 34.5 %collective-permute-start.7 = (bf16[128,4096]{1,0:T(8,128)(2,1)S(1)}, bf16[128,4096]{1,0:T(8,128)(2,1)S(1)}, u32[]{:S(2)}, u32[]{:S(2)}) collective-permute-start(bf16[128,4096]{1,0:T(8,128)(2,1)S(1)} %convolution_convert_fusion.7), channel_id=1, source_target_pairs={{0,32},{32,64},{64,96},{96,0},{1,33},{33,65},{65,97},{97,1},{2,34}... | collective-permute-start | bytes 3145736 | tf_op jit(solution)/shard_map/ppermute | solution.py:28
  155.8 81.6 %collective-permute-start.13 = (bf16[128,4096]{1,0:T(8,128)(2,1)S(1)}, bf16[128,4096]{1,0:T(8,128)(2,1)S(1)}, u32[]{:S(2)}, u32[]{:S(2)}) collective-permute-start(bf16[128,4096]{1,0:T(8,128)(2,1)S(1)} %convolution_convert_fusion.6), channel_id=1, source_target_pairs={{0,32},{32,64},{64,96},{96,0},{1,33},{33,65},{65,97},{97,1},{2,34}... | collective-permute-start | bytes 3145736 | tf_op jit(solution)/shard_map/ppermute | solution.py:28
  163.6 43.9 %collective-permute-start.11 = (bf16[128,4096]{1,0:T(8,128)(2,1)S(1)}, bf16[128,4096]{1,0:T(8,128)(2,1)S(1)}, u32[]{:S(2)}, u32[]{:S(2)}) collective-permute-start(bf16[128,4096]{1,0:T(8,128)(2,1)S(1)} %collective-permute-done.10), channel_id=1, source_target_pairs={{0,96},{32,0},{64,32},{96,64},{1,97},{33,1},{65,33},{97,65},{2,98}... | collective-permute-start | bytes 3145736 | tf_op jit(solution)/shard_map/ppermute | solution.py:28
  166.7 64.3 %collective-permute-start.9 = (bf16[128,4096]{1,0:T(8,128)(2,1)S(1)}, bf16[128,4096]{1,0:T(8,128)(2,1)S(1)}, u32[]{:S(2)}, u32[]{:S(2)}) collective-permute-start(bf16[128,4096]{1,0:T(8,128)(2,1)S(1)} %collective-permute-done.8), channel_id=1, source_target_pairs={{0,32},{32,64},{64,96},{96,0},{1,33},{33,65},{65,97},{97,1},{2,34}... | collective-permute-start | bytes 3145736 | tf_op jit(solution)/shard_map/ppermute | solution.py:28
  185.1 90.3 %collective-permute-start.14 = (bf16[128,4096]{1,0:T(8,128)(2,1)S(1)}, bf16[128,4096]{1,0:T(8,128)(2,1)S(1)}, u32[]{:S(2)}, u32[]{:S(2)}) collective-permute-start(bf16[128,4096]{1,0:T(8,128)(2,1)S(1)} %convolution_convert_fusion.5), channel_id=1, source_target_pairs={{0,96},{32,0},{64,32},{96,64},{1,97},{33,1},{65,33},{97,65},{2,98}... | collective-permute-start | bytes 3145736 | tf_op jit(solution)/shard_map/ppermute | solution.py:28
  188.8 138.6 %collective-permute-start.22 = (bf16[128,4096]{1,0:T(8,128)(2,1)}, bf16[128,4096]{1,0:T(8,128)(2,1)}, u32[]{:S(2)}, u32[]{:S(2)}) collective-permute-start(bf16[128,4096]{1,0:T(8,128)(2,1)} %fusion.64), channel_id=1, source_target_pairs={{0,96},{32,0},{64,32},{96,64},{1,97},{33,1},{65,33},{97,65},{2,98}... | collective-permute-start | bytes 3145736 | tf_op jit(solution)/shard_map/ppermute | solution.py:28
  232.4 42.5 %collective-permute-start.12 = (bf16[128,4096]{1,0:T(8,128)(2,1)S(1)}, bf16[128,4096]{1,0:T(8,128)(2,1)S(1)}, u32[]{:S(2)}, u32[]{:S(2)}) collective-permute-start(bf16[128,4096]{1,0:T(8,128)(2,1)S(1)} %add_convert_fusion.3), channel_id=1, source_target_pairs={{0,96},{32,0},{64,32},{96,64},{1,97},{33,1},{65,33},{97,65},{2,98}... | collective-permute-start | bytes 3145736 | tf_op jit(solution)/shard_map/ppermute | solution.py:28
  233.9 44.8 %collective-permute-start.15 = (bf16[128,4096]{1,0:T(8,128)(2,1)S(1)}, bf16[128,4096]{1,0:T(8,128)(2,1)S(1)}, u32[]{:S(2)}, u32[]{:S(2)}) collective-permute-start(bf16[128,4096]{1,0:T(8,128)(2,1)S(1)} %add_convert_fusion.2), channel_id=1, source_target_pairs={{0,32},{32,64},{64,96},{96,0},{1,33},{33,65},{65,97},{97,1},{2,34}... | collective-permute-start | bytes 3145736 | tf_op jit(solution)/shard_map/ppermute | solution.py:28
  237.4 78.4 %collective-permute-start.20 = (bf16[128,4096]{1,0:T(8,128)(2,1)}, bf16[128,4096]{1,0:T(8,128)(2,1)}, u32[]{:S(2)}, u32[]{:S(2)}) collective-permute-start(bf16[128,4096]{1,0:T(8,128)(2,1)} %fusion.67), channel_id=1, source_target_pairs={{0,32},{32,64},{64,96},{96,0},{1,33},{33,65},{65,97},{97,1},{2,34}... | collective-permute-start | bytes 3145736 | tf_op jit(solution)/shard_map/ppermute | solution.py:28
  274.9 27.6 %collective-permute-start.17 = (bf16[128,4096]{1,0:T(8,128)(2,1)S(1)}, bf16[128,4096]{1,0:T(8,128)(2,1)S(1)}, u32[]{:S(2)}, u32[]{:S(2)}) collective-permute-start(bf16[128,4096]{1,0:T(8,128)(2,1)S(1)} %fusion.76), channel_id=1, source_target_pairs={{0,32},{32,64},{64,96},{96,0},{1,33},{33,65},{65,97},{97,1},{2,34}... | collective-permute-start | bytes 3145736 | tf_op jit(solution)/shard_map/ppermute | solution.py:28
  275.4 27.2 %collective-permute-start.16 = (bf16[128,4096]{1,0:T(8,128)(2,1)S(1)}, bf16[128,4096]{1,0:T(8,128)(2,1)S(1)}, u32[]{:S(2)}, u32[]{:S(2)}) collective-permute-start(bf16[128,4096]{1,0:T(8,128)(2,1)S(1)} %fusion.79), channel_id=1, source_target_pairs={{0,96},{32,0},{64,32},{96,64},{1,97},{33,1},{65,33},{97,65},{2,98}... | collective-permute-start | bytes 3145736 | tf_op jit(solution)/shard_map/ppermute | solution.py:28
  303.8 21.9 %collective-permute-start.18 = (bf16[128,4096]{1,0:T(8,128)(2,1)}, bf16[128,4096]{1,0:T(8,128)(2,1)}, u32[]{:S(2)}, u32[]{:S(2)}) collective-permute-start(bf16[128,4096]{1,0:T(8,128)(2,1)} %add_convert_fusion.1), channel_id=1, source_target_pairs={{0,96},{32,0},{64,32},{96,64},{1,97},{33,1},{65,33},{97,65},{2,98}... | collective-permute-start | bytes 3145736 | tf_op jit(solution)/shard_map/ppermute | solution.py:28
  305.0 23.0 %collective-permute-start.23 = (bf16[128,4096]{1,0:T(8,128)(2,1)}, bf16[128,4096]{1,0:T(8,128)(2,1)}, u32[]{:S(2)}, u32[]{:S(2)}) collective-permute-start(bf16[128,4096]{1,0:T(8,128)(2,1)} %add_convert_fusion), channel_id=1, source_target_pairs={{0,32},{32,64},{64,96},{96,0},{1,33},{33,65},{65,97},{97,1},{2,34}... | collective-permute-start | bytes 3145736 | tf_op jit(solution)/shard_map/ppermute | solution.py:28
  307.8 36.1 %all-to-all-start.2 = ((bf16[32,8,4096]{2,1,0:T(8,128)(2,1)}), bf16[32,8,4096]{2,1,0:T(8,128)(2,1)S(1)}, u32[]{:S(2)}, u32[]{:S(2)}) async-start(bf16[32,8,4096]{2,1,0:T(8,128)(2,1)} %bitcast.534), calls=%async_computation.2 | async-start | bytes 4194304 | tf_op jit(solution)/shard_map/all_to_all | solution.py:74
  343.9 33.7 %all-to-all-start.3 = ((bf16[32,8,4096]{2,1,0:T(8,128)(2,1)}), bf16[32,8,4096]{2,1,0:T(8,128)(2,1)}, u32[]{:S(2)}, u32[]{:S(2)}) async-start(bf16[32,8,4096]{2,1,0:T(8,128)(2,1)} %fusion.110), calls=%async_computation.3 | async-start | bytes 4194304 | tf_op jit(solution)/shard_map/all_to_all | solution.py:74
  349.2 31.5 %copy-start.1 = (bf16[128,4096]{1,0:T(8,128)(2,1)S(1)}, bf16[128,4096]{1,0:T(8,128)(2,1)}, u32[]{:S(2)}) copy-start(bf16[128,4096]{1,0:T(8,128)(2,1)} %param.5) | copy-start | bytes 3145732

commit v7 on v5

--- a/solution.py
+++ b/solution.py
@@ -124,7 +124,9 @@
         backward_rows(block, f[0], f[1], weights) for block, f in zip(cot_blocks, forward)
     ]
     grad_received = sum_start(grad_parts)
-    fwd_total, grad_received = lax.optimization_barrier((fwd_total, grad_received))
+    fwd_total, grad_received, grad_parts[2:4] = lax.optimization_barrier(
+        (fwd_total, grad_received, grad_parts[2:4])
+    )
     cold_out = return_rows(fwd_total, experts, capacity, model_width)
     expert_out = collect(cold_layout, cold_out)
     combined = (combine[:, None] * expert_out).astype(jnp.bfloat16)

time: 374 us -> 381 us (1.019)
  waiting for transfers between devices: 198 us -> 205 us
    ppermute x24, waiting for transfers between devices: 164 us -> 171 us  [shifted(): lax.ppermute(values, 'dp', perm=[(i, (i + step) % n) for i in range(n)])]
  transfers between devices with their start and end apart: 27 -> 27, of which waited for: 13 -> 14; matrix products, arithmetic and copies ran while one was open for 19% -> 19% of each run, Pallas kernels for 0% -> 0%
where the time goes in v7:
time: 381 us; the launch traced here: 373 us
  waiting for transfers between devices  205 us (54%)
  matrix products  67.6 us (18%)
  starting transfers between devices  49.3 us (13%)
  blocking collectives  37.6 us (10%)
  other arithmetic  8.91 us (2%)
    ppermute x24, waiting for transfers between devices, shifted(): lax.ppermute(values, 'dp', perm=[(i, (i + step) % n) for i in range(n)])  171 us
    all_to_all x1, blocking collectives, arrive_rows(): lax.all_to_all(cold_buf.reshape(experts, slot_count, model_width), 'exper...  37.6 us
    ppermute x24, starting transfers between devices, shifted(): lax.ppermute(values, 'dp', perm=[(i, (i + step) % n) for i in range(n)])  29.7 us
    dot_general x7, matrix products, forward_rows(): jnp.einsum('rd,kfd->krf', row_block, matrices[:2], preferred_element_type...  27.3 us
    all_to_all x2, waiting for transfers between devices, return_rows(): lax.all_to_all(summed, 'expert', split_axis=0, concat_axis=0, tiled=True)  24.9 us
    all_to_all x2, starting transfers between devices, return_rows(): lax.all_to_all(summed, 'expert', split_axis=0, concat_axis=0, tiled=True)  15 us
    dot_general x7, matrix products, backward_rows(): jnp.einsum('krf,kfd->rd', both_grads, matrices[:2], preferred_element_typ...  14 us
    all_to_all x1, waiting for transfers between devices, arrive_rows(): lax.all_to_all(cold_buf.reshape(experts, slot_count, model_width), 'exper...  9.01 us
  transfers between devices with their start and end apart: 27, of which 14 were waited for; matrix products, arithmetic and copies ran while one was open for 19% of the time, Pallas kernels for 0%

profile of v7, /device:TPU:1, one launch (start us, length us, event | category | flops | bytes accessed | tf_op | source)
XLA Modules:
  0.0 373.2 jit_solution(12646446339426560270)
XLA Ops:
  3.3 37.6 %all_to_all.20 = bf16[32,8,4096]{2,1,0:T(8,128)(2,1)S(1)} all-to-all(bf16[32,8,4096]{2,1,0:T(8,128)(2,1)S(1)} %fusion.39), channel_id=1, replica_groups=mesh['dp'=4,'expert'=32] {'expert'}, dimensions={0} | all-to-all | bytes 4194304 | tf_op jit(solution)/shard_map/all_to_all | solution.py:63
  40.8 1.4 copy-done.2
  42.2 1.1 slice_bitcast_fusion
  43.3 1.2 collective-permute-start
  44.5 1.5 collective-permute-start.3
  46.0 2.1 fusion.38
  48.1 4.5 %all-to-all-start = ((bf16[32,8,4096]{2,1,0:T(8,128)(2,1)}), bf16[32,8,4096]{2,1,0:T(8,128)(2,1)S(1)}, u32[]{:S(2)}, u32[]{:S(2)}) async-start(bf16[32,8,4096]{2,1,0:T(8,128)(2,1)} %fusion.38), calls=%async_computation | async-start | bytes 4194304 | tf_op jit(solution)/shard_map/all_to_all | solution.py:63
  52.7 2.7 collective-permute-start.2
  55.3 13.9 %collective-permute-done = bf16[128,4096]{1,0:T(8,128)(2,1)} collective-permute-done((bf16[128,4096]{1,0:T(8,128)(2,1)S(1)}, bf16[128,4096]{1,0:T(8,128)(2,1)}, u32[]{:S(2)}, u32[]{:S(2)}) %collective-permute-start) | collective-permute-done | bytes 1048608 | tf_op jit(solution)/shard_map/ppermute | solution.py:28
  69.2 2.7 collective-permute-start.5
  71.9 9.0 %all-to-all-done = bf16[32,8,4096]{2,1,0:T(8,128)(2,1)S(1)} async-done(((bf16[32,8,4096]{2,1,0:T(8,128)(2,1)}), bf16[32,8,4096]{2,1,0:T(8,128)(2,1)S(1)}, u32[]{:S(2)}, u32[]{:S(2)}) %all-to-all-start) | async-done | bytes 2097184 | tf_op jit(solution)/shard_map/all_to_all | solution.py:63
  80.9 10.8 %collective-permute-done.1 = bf16[128,4096]{1,0:T(8,128)(2,1)} collective-permute-done((bf16[128,4096]{1,0:T(8,128)(2,1)}, bf16[128,4096]{1,0:T(8,128)(2,1)}, u32[]{:S(2)}, u32[]{:S(2)}) %collective-permute-start.1) | collective-permute-done | bytes 1048608 | tf_op jit(solution)/shard_map/ppermute | solution.py:28
  91.7 22.5 %collective-permute-done.4 = bf16[128,4096]{1,0:T(8,128)(2,1)} collective-permute-done((bf16[128,4096]{1,0:T(8,128)(2,1)}, bf16[128,4096]{1,0:T(8,128)(2,1)}, u32[]{:S(2)}, u32[]{:S(2)}) %collective-permute-start.4) | collective-permute-done | bytes 1048608 | tf_op jit(solution)/shard_map/ppermute | solution.py:28
  114.3 1.2 collective-permute-start.8
  115.5 1.6 collective-permute-start.10
  117.0 1.4 collective-permute-start.11
  118.5 5.5 %fusion.117 = f32[2,128,384]{2,1,0:T(8,128)S(1)} fusion(bf16[128,4096]{1,0:T(8,128)(2,1)} %collective-permute-done.4, bf16[1,3,384,4096]{3,2,1,0:T(8,128)(2,1)} %param.9), kind=kOutput, calls=%fused_computation.103 | convolution fusion | flops 805306368 | bytes 7733248 | tf_op jit(solution)/shard_map/rd,kfd->krf/dot_general | solution.py:80
  124.0 2.6 convolution_convert_fusion.8
  126.6 2.8 collective-permute-start.6
  129.4 5.3 %fusion.120 = f32[2,128,384]{2,1,0:T(8,128)S(1)} fusion(bf16[128,4096]{1,0:T(8,128)(2,1)} %collective-permute-done.5, bf16[1,3,384,4096]{3,2,1,0:T(8,128)(2,1)} %param.9), kind=kOutput, calls=%fused_computation.104 | convolution fusion | flops 805306368 | bytes 7733248 | tf_op jit(solution)/shard_map/rd,kfd->krf/dot_general | solution.py:80
  135.6 3.4 fusion.114
  139.0 3.4 fusion.123
  144.0 3.4 fusion.126
  147.4 3.4 fusion.129
  151.0 10.1 %collective-permute-done.11 = bf16[128,4096]{1,0:T(8,128)(2,1)S(1)} collective-permute-done((bf16[128,4096]{1,0:T(8,128)(2,1)S(1)}, bf16[128,4096]{1,0:T(8,128)(2,1)S(1)}, u32[]{:S(2)}, u32[]{:S(2)}) %collective-permute-start.11) | collective-permute-done | bytes 1048608 | tf_op jit(solution)/shard_map/ppermute | solution.py:28
  162.0 2.2 collective-permute-start.13
  166.5 2.7 fusion.109
  169.2 14.3 %collective-permute-done.6 = bf16[128,4096]{1,0:T(8,128)(2,1)S(1)} collective-permute-done((bf16[128,4096]{1,0:T(8,128)(2,1)S(1)}, bf16[128,4096]{1,0:T(8,128)(2,1)S(1)}, u32[]{:S(2)}, u32[]{:S(2)}) %collective-permute-start.6) | collective-permute-done | bytes 1048608 | tf_op jit(solution)/shard_map/ppermute | solution.py:28
  183.5 2.9 collective-permute-start.16
  186.4 20.1 %collective-permute-done.12 = bf16[128,4096]{1,0:T(8,128)(2,1)S(1)} collective-permute-done((bf16[128,4096]{1,0:T(8,128)(2,1)S(1)}, bf16[128,4096]{1,0:T(8,128)(2,1)S(1)}, u32[]{:S(2)}, u32[]{:S(2)}) %collective-permute-start.12) | collective-permute-done | bytes 1048608 | tf_op jit(solution)/shard_map/ppermute | solution.py:28
  206.5 1.1 fusion.252
  207.6 1.1 fusion.251
  208.7 1.1 fusion.250
  209.8 1.1 fusion.249
  210.9 1.0 fusion.70
  212.4 1.1 fusion.248
  213.7 2.3 collective-permute-start.14
  216.6 1.0 fusion.67
  217.6 2.0 fusion.49
  219.6 2.0 fusion.46
  221.6 1.1 fusion.253
  222.7 1.0 fusion.73
  223.7 1.0 fusion.61
  224.7 4.3 %collective-permute-done.15 = bf16[128,4096]{1,0:T(8,128)(2,1)S(1)} collective-permute-done((bf16[128,4096]{1,0:T(8,128)(2,1)S(1)}, bf16[128,4096]{1,0:T(8,128)(2,1)S(1)}, u32[]{:S(2)}, u32[]{:S(2)}) %collective-permute-start.15) | collective-permute-done | bytes 1048608 | tf_op jit(solution)/shard_map/ppermute | solution.py:28
  228.9 1.2 collective-permute-start.18
  230.2 20.7 %collective-permute-done.14 = bf16[128,4096]{1,0:T(8,128)(2,1)S(1)} collective-permute-done((bf16[128,4096]{1,0:T(8,128)(2,1)S(1)}, bf16[128,4096]{1,0:T(8,128)(2,1)S(1)}, u32[]{:S(2)}, u32[]{:S(2)}) %collective-permute-start.14) | collective-permute-done | bytes 1048608 | tf_op jit(solution)/shard_map/ppermute | solution.py:28
  251.2 22.7 %collective-permute-done.17 = bf16[128,4096]{1,0:T(8,128)(2,1)S(1)} collective-permute-done((bf16[128,4096]{1,0:T(8,128)(2,1)S(1)}, bf16[128,4096]{1,0:T(8,128)(2,1)S(1)}, u32[]{:S(2)}, u32[]{:S(2)}) %collective-permute-start.17) | collective-permute-done | bytes 1048608 | tf_op jit(solution)/shard_map/ppermute | solution.py:28
  274.2 2.7 maximum_add_fusion
  276.9 1.3 add_convert_fusion.1
  278.2 1.2 collective-permute-start.20
  279.7 1.2 add_convert_fusion
  280.9 2.7 collective-permute-start.22
  283.6 1.3 fusion.230
  284.9 7.3 %all-to-all-start.2 = ((bf16[32,8,4096]{2,1,0:T(8,128)(2,1)}), bf16[32,8,4096]{2,1,0:T(8,128)(2,1)S(1)}, u32[]{:S(2)}, u32[]{:S(2)}) async-start(bf16[32,8,4096]{2,1,0:T(8,128)(2,1)} %bitcast.526), calls=%async_computation.2 | async-start | bytes 4194304 | tf_op jit(solution)/shard_map/all_to_all | solution.py:74
  292.2 8.9 %collective-permute-done.20 = bf16[128,4096]{1,0:T(8,128)(2,1)} collective-permute-done((bf16[128,4096]{1,0:T(8,128)(2,1)}, bf16[128,4096]{1,0:T(8,128)(2,1)}, u32[]{:S(2)}, u32[]{:S(2)}) %collective-permute-start.20) | collective-permute-done | bytes 1048608 | tf_op jit(solution)/shard_map/ppermute | solution.py:28
  301.1 2.0 collective-permute-done.21
  303.2 1.8 convert_add_fusion.1
  305.0 20.7 %collective-permute-done.23 = bf16[128,4096]{1,0:T(8,128)(2,1)} collective-permute-done((bf16[128,4096]{1,0:T(8,128)(2,1)}, bf16[128,4096]{1,0:T(8,128)(2,1)}, u32[]{:S(2)}, u32[]{:S(2)}) %collective-permute-start.23) | collective-permute-done | bytes 1048608 | tf_op jit(solution)/shard_map/ppermute | solution.py:28
  325.6 1.8 convert_add_fusion
  327.4 6.1 %fusion.104 = bf16[32,8,4096]{2,1,0:T(8,128)(2,1)} fusion(f32[128,4096]{1,0:T(8,128)S(1)} %convert_add_fusion, f32[128,4096]{1,0:T(8,128)S(1)} %convert_add_fusion.1, bf16[1,256,384]{2,1,0:T(8,128)(2,1)S(1)} %get-tuple-element.57, bf16[1,256,384]{2,1,0:T(8,128)(2,1)S(1)} %get-tuple-element.56, bf16[1,3,384,4096]{3,2,1,0:T(8,128)(2,1)} %param.9), kind=kOutput, calls=%fused_computation.86 | convolution fusion | flops 1616052224 | bytes 12976128 | tf_op jit(solution)/shard_map/krf,kfd->rd/dot_general | solution.py:98
  333.5 7.7 %all-to-all-start.3 = ((bf16[32,8,4096]{2,1,0:T(8,128)(2,1)}), bf16[32,8,4096]{2,1,0:T(8,128)(2,1)}, u32[]{:S(2)}, u32[]{:S(2)}) async-start(bf16[32,8,4096]{2,1,0:T(8,128)(2,1)} %fusion.104), calls=%async_computation.3 | async-start | bytes 4194304 | tf_op jit(solution)/shard_map/all_to_all | solution.py:74
  341.3 3.5 fusion.103
  344.8 24.9 %all-to-all-done.3 = bf16[32,8,4096]{2,1,0:T(8,128)(2,1)} async-done(((bf16[32,8,4096]{2,1,0:T(8,128)(2,1)}), bf16[32,8,4096]{2,1,0:T(8,128)(2,1)}, u32[]{:S(2)}, u32[]{:S(2)}) %all-to-all-start.3) | async-done | bytes 2097184 | tf_op jit(solution)/shard_map/all_to_all | solution.py:74
  369.7 3.1 convolution_convert_fusion.3
  (63 shorter events, 10.4 us)
Async XLA Ops:
  0.6 1.9 copy-start
  40.8 1.4 copy-start.2
  42.2 3.8 %copy-start.4 = (bf16[128,4096]{1,0:T(8,128)(2,1)S(1)}, bf16[128,4096]{1,0:T(8,128)(2,1)}, u32[]{:S(2)}) copy-start(bf16[128,4096]{1,0:T(8,128)(2,1)} %param.6) | copy-start | bytes 3145732
  42.2 3.8 %copy-start.5 = (f32[128]{0:T(128)S(1)}, f32[128]{0:T(128)}, u32[]{:S(2)}) copy-start(f32[128]{0:T(128)} %param.8) | copy-start | bytes 1540
  43.3 25.9 %collective-permute-start = (bf16[128,4096]{1,0:T(8,128)(2,1)S(1)}, bf16[128,4096]{1,0:T(8,128)(2,1)}, u32[]{:S(2)}, u32[]{:S(2)}) collective-permute-start(bf16[128,4096]{1,0:T(8,128)(2,1)S(1)} %get-tuple-element.55), channel_id=1, source_target_pairs={{0,32},{32,64},{64,96},{96,0},{1,33},{33,65},{65,97},{97,1},{2,34}... | collective-permute-start | bytes 3145736 | tf_op jit(solution)/shard_map/ppermute | solution.py:28
  44.5 24.7 %collective-permute-start.3 = (bf16[128,4096]{1,0:T(8,128)(2,1)}, bf16[128,4096]{1,0:T(8,128)(2,1)}, u32[]{:S(2)}, u32[]{:S(2)}) collective-permute-start(bf16[128,4096]{1,0:T(8,128)(2,1)} %get-tuple-element.54), channel_id=1, source_target_pairs={{0,96},{32,0},{64,32},{96,64},{1,97},{33,1},{65,33},{97,65},{2,98}... | collective-permute-start | bytes 3145736 | tf_op jit(solution)/shard_map/ppermute | solution.py:28
  48.1 32.8 %all-to-all-start = ((bf16[32,8,4096]{2,1,0:T(8,128)(2,1)}), bf16[32,8,4096]{2,1,0:T(8,128)(2,1)S(1)}, u32[]{:S(2)}, u32[]{:S(2)}) async-start(bf16[32,8,4096]{2,1,0:T(8,128)(2,1)} %fusion.38), calls=%async_computation | async-start | bytes 4194304 | tf_op jit(solution)/shard_map/all_to_all | solution.py:63
  52.6 39.1 %collective-permute-start.1 = (bf16[128,4096]{1,0:T(8,128)(2,1)}, bf16[128,4096]{1,0:T(8,128)(2,1)}, u32[]{:S(2)}, u32[]{:S(2)}) collective-permute-start(bf16[128,4096]{1,0:T(8,128)(2,1)} %get-tuple-element.54), channel_id=1, source_target_pairs={{0,32},{32,64},{64,96},{96,0},{1,33},{33,65},{65,97},{97,1},{2,34}... | collective-permute-start | bytes 3145736 | tf_op jit(solution)/shard_map/ppermute | solution.py:28
  52.7 39.0 %collective-permute-start.2 = (bf16[128,4096]{1,0:T(8,128)(2,1)S(1)}, bf16[128,4096]{1,0:T(8,128)(2,1)}, u32[]{:S(2)}, u32[]{:S(2)}) collective-permute-start(bf16[128,4096]{1,0:T(8,128)(2,1)S(1)} %get-tuple-element.55), channel_id=1, source_target_pairs={{0,96},{32,0},{64,32},{96,64},{1,97},{33,1},{65,33},{97,65},{2,98}... | collective-permute-start | bytes 3145736 | tf_op jit(solution)/shard_map/ppermute | solution.py:28
  69.2 44.9 %collective-permute-start.4 = (bf16[128,4096]{1,0:T(8,128)(2,1)}, bf16[128,4096]{1,0:T(8,128)(2,1)}, u32[]{:S(2)}, u32[]{:S(2)}) collective-permute-start(bf16[128,4096]{1,0:T(8,128)(2,1)} %collective-permute-done), channel_id=1, source_target_pairs={{0,32},{32,64},{64,96},{96,0},{1,33},{33,65},{65,97},{97,1},{2,34}... | collective-permute-start | bytes 3145736 | tf_op jit(solution)/shard_map/ppermute | solution.py:28
  69.2 44.9 %collective-permute-start.5 = (bf16[128,4096]{1,0:T(8,128)(2,1)}, bf16[128,4096]{1,0:T(8,128)(2,1)}, u32[]{:S(2)}, u32[]{:S(2)}) collective-permute-start(bf16[128,4096]{1,0:T(8,128)(2,1)} %collective-permute-done.3), channel_id=1, source_target_pairs={{0,96},{32,0},{64,32},{96,64},{1,97},{33,1},{65,33},{97,65},{2,98}... | collective-permute-start | bytes 3145736 | tf_op jit(solution)/shard_map/ppermute | solution.py:28
  114.3 36.6 %collective-permute-start.8 = (bf16[128,4096]{1,0:T(8,128)(2,1)S(1)}, bf16[128,4096]{1,0:T(8,128)(2,1)S(1)}, u32[]{:S(2)}, u32[]{:S(2)}) collective-permute-start(bf16[128,4096]{1,0:T(8,128)(2,1)S(1)} %get-tuple-element.53), channel_id=1, source_target_pairs={{0,32},{32,64},{64,96},{96,0},{1,33},{33,65},{65,97},{97,1},{2,34}... | collective-permute-start | bytes 3145736 | tf_op jit(solution)/shard_map/ppermute | solution.py:28
  115.5 46.5 %collective-permute-start.10 = (bf16[128,4096]{1,0:T(8,128)(2,1)S(1)}, bf16[128,4096]{1,0:T(8,128)(2,1)S(1)}, u32[]{:S(2)}, u32[]{:S(2)}) collective-permute-start(bf16[128,4096]{1,0:T(8,128)(2,1)S(1)} %get-tuple-element.53), channel_id=1, source_target_pairs={{0,96},{32,0},{64,32},{96,64},{1,97},{33,1},{65,33},{97,65},{2,98}... | collective-permute-start | bytes 3145736 | tf_op jit(solution)/shard_map/ppermute | solution.py:28
  117.0 44.0 %collective-permute-start.11 = (bf16[128,4096]{1,0:T(8,128)(2,1)S(1)}, bf16[128,4096]{1,0:T(8,128)(2,1)S(1)}, u32[]{:S(2)}, u32[]{:S(2)}) collective-permute-start(bf16[128,4096]{1,0:T(8,128)(2,1)S(1)} %get-tuple-element.52), channel_id=1, source_target_pairs={{0,96},{32,0},{64,32},{96,64},{1,97},{33,1},{65,33},{97,65},{2,98}... | collective-permute-start | bytes 3145736 | tf_op jit(solution)/shard_map/ppermute | solution.py:28
  118.4 50.8 %collective-permute-start.9 = (bf16[128,4096]{1,0:T(8,128)(2,1)S(1)}, bf16[128,4096]{1,0:T(8,128)(2,1)S(1)}, u32[]{:S(2)}, u32[]{:S(2)}) collective-permute-start(bf16[128,4096]{1,0:T(8,128)(2,1)S(1)} %get-tuple-element.52), channel_id=1, source_target_pairs={{0,32},{32,64},{64,96},{96,0},{1,33},{33,65},{65,97},{97,1},{2,34}... | collective-permute-start | bytes 3145736 | tf_op jit(solution)/shard_map/ppermute | solution.py:28
  118.5 16.3 %slice-start = ((s8[9437184]{0:T(1024)(128)(4,1)}), s8[4194304]{0:T(1024)(128)(4,1)S(1)}, s32[]{:S(2)}) async-start(s8[9437184]{0:T(1024)(128)(4,1)} %bitcast.524), calls=%async_computation.4 | async-start | bytes 8388608
  118.5 16.3 %slice-start.1 = ((s8[9437184]{0:T(1024)(128)(4,1)}), s8[4194304]{0:T(1024)(128)(4,1)S(1)}, s32[]{:S(2)}) async-start(s8[9437184]{0:T(1024)(128)(4,1)} %bitcast.524), calls=%async_computation.5 | async-start | bytes 8388608
  126.6 8.2 %slice-start.2 = ((s8[9437184]{0:T(1024)(128)(4,1)}), s8[1048576]{0:T(1024)(128)(4,1)S(1)}, s32[]{:S(2)}) async-start(s8[9437184]{0:T(1024)(128)(4,1)} %bitcast.524), calls=%async_computation.6 | async-start | bytes 2097152
  126.6 56.9 %collective-permute-start.6 = (bf16[128,4096]{1,0:T(8,128)(2,1)S(1)}, bf16[128,4096]{1,0:T(8,128)(2,1)S(1)}, u32[]{:S(2)}, u32[]{:S(2)}) collective-permute-start(bf16[128,4096]{1,0:T(8,128)(2,1)S(1)} %convolution_convert_fusion.8), channel_id=1, source_target_pairs={{0,96},{32,0},{64,32},{96,64},{1,97},{33,1},{65,33},{97,65},{2,98}... | collective-permute-start | bytes 3145736 | tf_op jit(solution)/shard_map/ppermute | solution.py:28
  142.5 1.5 copy-start.6
  150.9 35.5 %collective-permute-start.7 = (bf16[128,4096]{1,0:T(8,128)(2,1)S(1)}, bf16[128,4096]{1,0:T(8,128)(2,1)S(1)}, u32[]{:S(2)}, u32[]{:S(2)}) collective-permute-start(bf16[128,4096]{1,0:T(8,128)(2,1)S(1)} %convolution_convert_fusion.7), channel_id=1, source_target_pairs={{0,32},{32,64},{64,96},{96,0},{1,33},{33,65},{65,97},{97,1},{2,34}... | collective-permute-start | bytes 3145736 | tf_op jit(solution)/shard_map/ppermute | solution.py:28
  161.0 45.4 %collective-permute-start.12 = (bf16[128,4096]{1,0:T(8,128)(2,1)S(1)}, bf16[128,4096]{1,0:T(8,128)(2,1)S(1)}, u32[]{:S(2)}, u32[]{:S(2)}) collective-permute-start(bf16[128,4096]{1,0:T(8,128)(2,1)S(1)} %collective-permute-done.8), channel_id=1, source_target_pairs={{0,32},{32,64},{64,96},{96,0},{1,33},{33,65},{65,97},{97,1},{2,34}... | collective-permute-start | bytes 3145736 | tf_op jit(solution)/shard_map/ppermute | solution.py:28
  162.0 44.5 %collective-permute-start.13 = (bf16[128,4096]{1,0:T(8,128)(2,1)S(1)}, bf16[128,4096]{1,0:T(8,128)(2,1)S(1)}, u32[]{:S(2)}, u32[]{:S(2)}) collective-permute-start(bf16[128,4096]{1,0:T(8,128)(2,1)S(1)} %collective-permute-done.11), channel_id=1, source_target_pairs={{0,96},{32,0},{64,32},{96,64},{1,97},{33,1},{65,33},{97,65},{2,98}... | collective-permute-start | bytes 3145736 | tf_op jit(solution)/shard_map/ppermute | solution.py:28
  164.9 1.6 copy-start.3
  169.2 38.4 %copy-start.7 = (f32[2,128,384]{2,1,0:T(8,128)S(1)}, f32[2,128,384]{2,1,0:T(8,128)}, u32[]{:S(2)}) copy-start(f32[2,128,384]{2,1,0:T(8,128)} %copy-done.6) | copy-start | bytes 1179652
  169.2 59.8 %collective-permute-start.15 = (bf16[128,4096]{1,0:T(8,128)(2,1)S(1)}, bf16[128,4096]{1,0:T(8,128)(2,1)S(1)}, u32[]{:S(2)}, u32[]{:S(2)}) collective-permute-start(bf16[128,4096]{1,0:T(8,128)(2,1)S(1)} %convolution_convert_fusion.6), channel_id=1, source_target_pairs={{0,32},{32,64},{64,96},{96,0},{1,33},{33,65},{65,97},{97,1},{2,34}... | collective-permute-start | bytes 3145736 | tf_op jit(solution)/shard_map/ppermute | solution.py:28
  183.5 67.7 %collective-permute-start.16 = (bf16[128,4096]{1,0:T(8,128)(2,1)S(1)}, bf16[128,4096]{1,0:T(8,128)(2,1)S(1)}, u32[]{:S(2)}, u32[]{:S(2)}) collective-permute-start(bf16[128,4096]{1,0:T(8,128)(2,1)S(1)} %convolution_convert_fusion.5), channel_id=1, source_target_pairs={{0,96},{32,0},{64,32},{96,64},{1,97},{33,1},{65,33},{97,65},{2,98}... | collective-permute-start | bytes 3145736 | tf_op jit(solution)/shard_map/ppermute | solution.py:28
  211.9 65.0 %collective-permute-start.19 = (bf16[128,4096]{1,0:T(8,128)(2,1)S(1)}, bf16[128,4096]{1,0:T(8,128)(2,1)S(1)}, u32[]{:S(2)}, u32[]{:S(2)}) collective-permute-start(bf16[128,4096]{1,0:T(8,128)(2,1)S(1)} %fusion.70), channel_id=1, source_target_pairs={{0,32},{32,64},{64,96},{96,0},{1,33},{33,65},{65,97},{97,1},{2,34}... | collective-permute-start | bytes 3145736 | tf_op jit(solution)/shard_map/ppermute | solution.py:28
  213.7 37.2 %collective-permute-start.14 = (bf16[128,4096]{1,0:T(8,128)(2,1)S(1)}, bf16[128,4096]{1,0:T(8,128)(2,1)S(1)}, u32[]{:S(2)}, u32[]{:S(2)}) collective-permute-start(bf16[128,4096]{1,0:T(8,128)(2,1)S(1)} %add_convert_fusion.3), channel_id=1, source_target_pairs={{0,96},{32,0},{64,32},{96,64},{1,97},{33,1},{65,33},{97,65},{2,98}... | collective-permute-start | bytes 3145736 | tf_op jit(solution)/shard_map/ppermute | solution.py:28
  216.3 57.6 %collective-permute-start.17 = (bf16[128,4096]{1,0:T(8,128)(2,1)S(1)}, bf16[128,4096]{1,0:T(8,128)(2,1)S(1)}, u32[]{:S(2)}, u32[]{:S(2)}) collective-permute-start(bf16[128,4096]{1,0:T(8,128)(2,1)S(1)} %add_convert_fusion.2), channel_id=1, source_target_pairs={{0,32},{32,64},{64,96},{96,0},{1,33},{33,65},{65,97},{97,1},{2,34}... | collective-permute-start | bytes 3145736 | tf_op jit(solution)/shard_map/ppermute | solution.py:28
  228.9 48.0 %collective-permute-start.18 = (bf16[128,4096]{1,0:T(8,128)(2,1)S(1)}, bf16[128,4096]{1,0:T(8,128)(2,1)S(1)}, u32[]{:S(2)}, u32[]{:S(2)}) collective-permute-start(bf16[128,4096]{1,0:T(8,128)(2,1)S(1)} %fusion.73), channel_id=1, source_target_pairs={{0,96},{32,0},{64,32},{96,64},{1,97},{33,1},{65,33},{97,65},{2,98}... | collective-permute-start | bytes 3145736 | tf_op jit(solution)/shard_map/ppermute | solution.py:28
  251.2 23.0 %copy-start.8 = (f32[2,256,384]{2,1,0:T(8,128)S(1)}, f32[2,256,384]{2,1,0:T(8,128)}, u32[]{:S(2)}) copy-start(f32[2,256,384]{2,1,0:T(8,128)} %fusion.109) | copy-start | bytes 2359300
  278.2 22.9 %collective-permute-start.20 = (bf16[128,4096]{1,0:T(8,128)(2,1)}, bf16[128,4096]{1,0:T(8,128)(2,1)}, u32[]{:S(2)}, u32[]{:S(2)}) collective-permute-start(bf16[128,4096]{1,0:T(8,128)(2,1)} %add_convert_fusion.1), channel_id=1, source_target_pairs={{0,96},{32,0},{64,32},{96,64},{1,97},{33,1},{65,33},{97,65},{2,98}... | collective-permute-start | bytes 3145736 | tf_op jit(solution)/shard_map/ppermute | solution.py:28
  279.5 23.7 %collective-permute-start.21 = (bf16[128,4096]{1,0:T(8,128)(2,1)}, bf16[128,4096]{1,0:T(8,128)(2,1)}, u32[]{:S(2)}, u32[]{:S(2)}) collective-permute-start(bf16[128,4096]{1,0:T(8,128)(2,1)} %fusion.49), channel_id=1, source_target_pairs={{0,32},{32,64},{64,96},{96,0},{1,33},{33,65},{65,97},{97,1},{2,34}... | collective-permute-start | bytes 3145736 | tf_op jit(solution)/shard_map/ppermute | solution.py:28
  280.9 44.7 %collective-permute-start.23 = (bf16[128,4096]{1,0:T(8,128)(2,1)}, bf16[128,4096]{1,0:T(8,128)(2,1)}, u32[]{:S(2)}, u32[]{:S(2)}) collective-permute-start(bf16[128,4096]{1,0:T(8,128)(2,1)} %add_convert_fusion), channel_id=1, source_target_pairs={{0,32},{32,64},{64,96},{96,0},{1,33},{33,65},{65,97},{97,1},{2,34}... | collective-permute-start | bytes 3145736 | tf_op jit(solution)/shard_map/ppermute | solution.py:28
  280.9 44.7 %collective-permute-start.22 = (bf16[128,4096]{1,0:T(8,128)(2,1)}, bf16[128,4096]{1,0:T(8,128)(2,1)}, u32[]{:S(2)}, u32[]{:S(2)}) collective-permute-start(bf16[128,4096]{1,0:T(8,128)(2,1)} %fusion.46), channel_id=1, source_target_pairs={{0,96},{32,0},{64,32},{96,64},{1,97},{33,1},{65,33},{97,65},{2,98}... | collective-permute-start | bytes 3145736 | tf_op jit(solution)/shard_map/ppermute | solution.py:28
  284.9 48.6 %all-to-all-start.2 = ((bf16[32,8,4096]{2,1,0:T(8,128)(2,1)}), bf16[32,8,4096]{2,1,0:T(8,128)(2,1)S(1)}, u32[]{:S(2)}, u32[]{:S(2)}) async-start(bf16[32,8,4096]{2,1,0:T(8,128)(2,1)} %bitcast.526), calls=%async_computation.2 | async-start | bytes 4194304 | tf_op jit(solution)/shard_map/all_to_all | solution.py:74
  333.5 36.2 %all-to-all-start.3 = ((bf16[32,8,4096]{2,1,0:T(8,128)(2,1)}), bf16[32,8,4096]{2,1,0:T(8,128)(2,1)}, u32[]{:S(2)}, u32[]{:S(2)}) async-start(bf16[32,8,4096]{2,1,0:T(8,128)(2,1)} %fusion.104), calls=%async_computation.3 | async-start | bytes 4194304 | tf_op jit(solution)/shard_map/all_to_all | solution.py:74
  341.3 31.5 %copy-start.1 = (bf16[128,4096]{1,0:T(8,128)(2,1)S(1)}, bf16[128,4096]{1,0:T(8,128)(2,1)}, u32[]{:S(2)}) copy-start(bf16[128,4096]{1,0:T(8,128)(2,1)} %param.5) | copy-start | bytes 3145732
